TPU v7x, 128 devices: a whole 4x4x4 slice. The times are simulated.
128 devices in a mesh: row: 8 (over x_lo, z), col: 16 (over y, x_hi, core).
Axes of the slice: x: 4 (x_hi: 2, x_lo: 2; x = x_hi * 2 + x_lo), y: 4, z: 4, core: 2. Of those that a mesh axis runs over, the one named last changes fastest.
Arguments:
- hidden_input: bfloat16 [16384, 1536], P(('row', 'col')), may hold values from -6 to 6
- lengths: int32 [8, 4], replicated, may hold values from 1 to 1536, 2048 in all within a row
- prompt_adapter: int32 [8, 4], replicated, may hold values from 0 to 63
- routes: int32 [16384, 4], P(('row', 'col')), may hold values from 0 to 31, all different within a row; in each aligned block of 128 rows (0 to 127, 128 to 255, ...) at most 40 rows name the same one
- attention_norm_gain: bfloat16 [1536], replicated, may hold values from 0.5 to 1.5
- expert_norm_gain: bfloat16 [1536], replicated, may hold values from 0.5 to 1.5
- projection_weight: bfloat16 [1536, 2048], P('row', 'col')
- output_weight: bfloat16 [1536, 1536], P('row', 'col'), may hold values from -0.15625 to 0.15625
- router: bfloat16 [1536, 32], replicated, may hold values from -0.5 to 0.5
- adapter_projection_down: bfloat16 [64, 16, 1536], P('col'), may hold values from -0.15625 to 0.15625
- adapter_projection_up: bfloat16 [64, 16, 2048], P('col'), may hold values from -1.5 to 1.5
- adapter_output_down: bfloat16 [64, 16, 1536], P('col'), may hold values from -0.15625 to 0.15625
- adapter_output_up: bfloat16 [64, 16, 1536], P('col'), may hold values from -1.5 to 1.5
- expert_gate_weight: bfloat16 [32, 1536, 768], P('col'), may hold values from -0.15625 to 0.15625
- expert_up_weight: bfloat16 [32, 1536, 768], P('col'), may hold values from -0.15625 to 0.15625
- expert_down_weight: bfloat16 [32, 768, 1536], P('col'), may hold values from -0.21875 to 0.21875
Outputs:
- hidden_out: bfloat16 [16384, 1536], P(('row', 'col'))
Inputs may be any that keep to these rules, and one draw needn't show every extreme that they name: The 4 lengths of a block sum to 2048; in every block the longest prompt has exactly 1536 tokens. `prompt_adapter`: adapter a is held by index a // 4 of col. `routes`: the 4 experts of a token differ; among the rows of one device no expert is named more than 40 times, a bound that some block reaches. Expert e is held by index e // 2 of col.
All inputs are finite; a program needn't handle non-finite values.
Results may differ from a plain program's by a relative error of at most 0.012.
Values may be sent and summed in bfloat16 or wider, within the bound.
No kernel may reach another device: no remote copies, remote signals or barrier semaphores. Data moves between devices by JAX's collectives and lax.ppermute only.
A program may use at most 128 MiB of HBM per device.

v0:
```python
import jax
import jax.numpy as jnp
from jax import lax
from jax.sharding import PartitionSpec as P

QUERY_HEADS = 12
KEY_HEADS = 2
HEAD_SIZE = 128
QUERY_PER_KEY = 6
CAP = 40


norm_eps = 1e-06
rope_base = 1000000.0
adapter_scale = 0.5


def rms_scaled(value_tensor, norm_gain):
    widened = value_tensor.astype(jnp.float32)
    inverse = lax.rsqrt(jnp.mean(widened * widened, axis=-1, keepdims=True) + norm_eps)
    return (widened * inverse * norm_gain.astype(jnp.float32)).astype(jnp.bfloat16)


def prompt_layout(lengths_row, tok_index):
    prompt_ends = jnp.cumsum(lengths_row)
    starts = prompt_ends - lengths_row
    prompt_of = jnp.sum((tok_index[:, None] >= prompt_ends[None, :]).astype(jnp.int32), axis=1)
    within_prompt = prompt_of[:, None] == jnp.arange(lengths_row.shape[0], dtype=jnp.int32)[None, :]
    token_positions = tok_index - jnp.sum(jnp.where(within_prompt, starts[None, :], 0), axis=1)
    return (prompt_of, within_prompt, token_positions)


def apply_rotary(value_tensor, token_positions):
    half_width = value_tensor.shape[-1] // 2
    frequency = rope_base ** (
        -2.0 * jnp.arange(half_width, dtype=jnp.float32) / value_tensor.shape[-1]
    )
    angles = token_positions.astype(jnp.float32)[:, None] * frequency[None, :]
    cosine = jnp.cos(angles)[:, None, :]
    sine_part = jnp.sin(angles)[:, None, :]
    front_half = value_tensor[..., :half_width]
    back_half = value_tensor[..., half_width:]
    return jnp.concatenate(
        [front_half * cosine - back_half * sine_part, back_half * cosine + front_half * sine_part],
        axis=-1,
    )


def adapter_change(inputs, within_prompt, downs, ups):
    low_rank = jnp.einsum("nk,prk->npr", inputs, downs, preferred_element_type=jnp.float32)
    low_rank = jnp.where(within_prompt[:, :, None], low_rank, 0.0).astype(jnp.bfloat16)
    return jnp.einsum("npr,pro->no", low_rank, ups, preferred_element_type=jnp.float32)


def route_slots(flat_routes, expert_total):
    marks = (flat_routes[:, None] == jnp.arange(expert_total, dtype=jnp.int32)[None, :]).astype(
        jnp.int32
    )
    before = jnp.cumsum(marks, axis=0) - marks
    return jnp.sum(before * marks, axis=1)


def local(
    hidden_input,
    lengths,
    prompt_adapter,
    routes,
    attention_norm_gain,
    expert_norm_gain,
    projection_weight,
    output_weight,
    router,
    adapter_projection_down,
    adapter_projection_up,
    adapter_output_down,
    adapter_output_up,
    expert_gate_weight,
    expert_up_weight,
    expert_down_weight,
):
    token_rows = hidden_input.shape[0]
    model_width = hidden_input.shape[1]
    columns = lax.axis_size("col")
    row_index = lax.axis_index("row")
    col_index = lax.axis_index("col")
    lengths_row = lax.dynamic_index_in_dim(lengths, row_index, 0, keepdims=False)
    adapter_row = lax.dynamic_index_in_dim(prompt_adapter, row_index, 0, keepdims=False)
    tok_index = col_index * token_rows + jnp.arange(token_rows, dtype=jnp.int32)
    prompt_of, within_prompt, token_positions = prompt_layout(lengths_row, tok_index)
    wide_parts = (
        lax.all_gather(projection_weight, "col", axis=1, tiled=True),
        lax.all_gather(output_weight, "col", axis=1, tiled=True),
    )
    qkv_full, out_full = (
        lax.all_gather(wide_parts[0], "row", axis=0, tiled=True),
        lax.all_gather(wide_parts[1], "row", axis=0, tiled=True),
    )
    owner_column = adapter_row // adapter_projection_down.shape[0]
    nearby_slot = adapter_row % adapter_projection_down.shape[0]
    owned_here = (owner_column == col_index)[:, None, None]

    def choose_experts(table):
        return jnp.where(owned_here, jnp.take(table, nearby_slot, axis=0).astype(jnp.float32), 0.0)

    summed = (
        lax.psum(choose_experts(adapter_projection_down).astype(jnp.bfloat16), "col").astype(
            jnp.float32
        ),
        lax.psum(choose_experts(adapter_projection_up).astype(jnp.bfloat16), "col").astype(
            jnp.float32
        ),
        lax.psum(choose_experts(adapter_output_down).astype(jnp.bfloat16), "col").astype(
            jnp.float32
        ),
        lax.psum(choose_experts(adapter_output_up).astype(jnp.bfloat16), "col").astype(jnp.float32),
    )
    projection_down_map = summed[0].astype(jnp.bfloat16)
    projection_up_map = summed[1].astype(jnp.bfloat16)
    output_down_map = summed[2].astype(jnp.bfloat16)
    output_up_map = summed[3].astype(jnp.bfloat16)
    normalized = rms_scaled(hidden_input, attention_norm_gain)
    projection_all = jnp.dot(normalized, qkv_full, preferred_element_type=jnp.float32)
    projection_all = projection_all + adapter_scale * adapter_change(
        normalized, within_prompt, projection_down_map, projection_up_map
    )
    query_slice = apply_rotary(
        projection_all[:, : QUERY_HEADS * HEAD_SIZE].reshape(token_rows, QUERY_HEADS, HEAD_SIZE),
        token_positions,
    ).astype(jnp.bfloat16)
    key_slice = apply_rotary(
        projection_all[:, QUERY_HEADS * HEAD_SIZE : (QUERY_HEADS + KEY_HEADS) * HEAD_SIZE].reshape(
            token_rows, KEY_HEADS, HEAD_SIZE
        ),
        token_positions,
    ).astype(jnp.bfloat16)
    value_slice = projection_all[:, (QUERY_HEADS + KEY_HEADS) * HEAD_SIZE :].astype(jnp.bfloat16)
    flattened_keys = key_slice.reshape(token_rows, KEY_HEADS * HEAD_SIZE)
    grouped = (
        query_slice.reshape(token_rows, KEY_HEADS, QUERY_PER_KEY, HEAD_SIZE)
        .transpose(1, 2, 0, 3)
        .reshape(KEY_HEADS, QUERY_PER_KEY * token_rows, HEAD_SIZE)
    )
    query_index = jnp.tile(tok_index, QUERY_PER_KEY)
    query_prompt = jnp.tile(prompt_of, QUERY_PER_KEY)
    segments = (
        lax.all_gather(flattened_keys, "col", axis=0, tiled=True),
        lax.all_gather(value_slice, "col", axis=0, tiled=True),
    )
    best_experts = jnp.full((KEY_HEADS, QUERY_PER_KEY * token_rows), -1e30, jnp.float32)
    segment_length = segments[0].shape[0]
    key_lines = segments[0].reshape(segment_length, KEY_HEADS, HEAD_SIZE).transpose(1, 0, 2)
    value_lines = segments[1].reshape(segment_length, KEY_HEADS, HEAD_SIZE).transpose(1, 0, 2)
    key_index = jnp.arange(segment_length, dtype=jnp.int32)
    key_prompt = prompt_layout(lengths_row, key_index)[0]
    allowed = (key_prompt[None, :] == query_prompt[:, None]) & (
        key_index[None, :] <= query_index[:, None]
    )
    scores = jnp.einsum(
        "hqd,hkd->hqk", grouped, key_lines, preferred_element_type=jnp.float32
    ) * HEAD_SIZE ** (-0.5)
    masked = jnp.where(allowed[None], scores, -1e30)
    fresh = jnp.maximum(best_experts, jnp.max(masked, axis=-1))
    weights = jnp.where(allowed[None], jnp.exp(scores - fresh[..., None]), 0.0)
    running_new = jnp.sum(weights, axis=-1)
    accum_new = jnp.einsum(
        "hqk,hkd->hqd",
        weights.astype(jnp.bfloat16),
        value_lines,
        preferred_element_type=jnp.float32,
    )
    mixed_output = accum_new / running_new[..., None]
    attention_result = (
        mixed_output.reshape(KEY_HEADS, QUERY_PER_KEY, token_rows, HEAD_SIZE)
        .transpose(2, 0, 1, 3)
        .reshape(token_rows, QUERY_HEADS * HEAD_SIZE)
        .astype(jnp.bfloat16)
    )
    projected_rows = jnp.dot(attention_result, out_full, preferred_element_type=jnp.float32)
    projected_rows = projected_rows + adapter_scale * adapter_change(
        attention_result, within_prompt, output_down_map, output_up_map
    )
    residual = (hidden_input.astype(jnp.float32) + projected_rows).astype(jnp.bfloat16)
    normed_two = rms_scaled(residual, expert_norm_gain)
    logits = jnp.dot(normed_two, router, preferred_element_type=jnp.float32)
    squashed = jax.nn.sigmoid(jnp.take_along_axis(logits, routes, axis=1))
    mixing = squashed / jnp.sum(squashed, axis=1, keepdims=True)
    expert_total = router.shape[1]
    local_experts = expert_gate_weight.shape[0]
    flat_routes = routes.reshape(-1)
    slots = route_slots(flat_routes, expert_total)
    token_of = jnp.arange(flat_routes.shape[0], dtype=jnp.int32) // routes.shape[1]
    dispatch_rows = (
        jnp.zeros((expert_total, CAP, model_width), jnp.bfloat16)
        .at[flat_routes, slots]
        .set(normed_two[token_of])
    )
    sending = dispatch_rows.reshape(columns, local_experts, CAP, model_width)
    arrived = lax.all_to_all(sending, "col", split_axis=0, concat_axis=0, tiled=True)
    gate_vals = jnp.einsum(
        "sjcd,jdf->sjcf", arrived, expert_gate_weight, preferred_element_type=jnp.float32
    )
    up_vals = jnp.einsum(
        "sjcd,jdf->sjcf", arrived, expert_up_weight, preferred_element_type=jnp.float32
    )
    hidden_vals = (jnp.maximum(gate_vals, 0.0) * up_vals).astype(jnp.bfloat16)
    answered = jnp.einsum(
        "sjcf,jfd->sjcd", hidden_vals, expert_down_weight, preferred_element_type=jnp.float32
    ).astype(jnp.bfloat16)
    returned = lax.all_to_all(answered, "col", split_axis=0, concat_axis=0, tiled=True)
    results = returned.reshape(expert_total, CAP, model_width)[flat_routes, slots]
    combined = jnp.sum(
        results.astype(jnp.float32).reshape(token_rows, routes.shape[1], model_width)
        * mixing[:, :, None],
        axis=1,
    )
    return (residual.astype(jnp.float32) + combined).astype(jnp.bfloat16)


def solution(mesh):
    placed = (
        P(("row", "col"), None),
        P(),
        P(),
        P(("row", "col"), None),
        P(),
        P(),
        P("row", "col"),
        P("row", "col"),
        P(),
        P("col", None, None),
        P("col", None, None),
        P("col", None, None),
        P("col", None, None),
        P("col", None, None),
        P("col", None, None),
        P("col", None, None),
    )
    return jax.shard_map(
        local, mesh=mesh, in_specs=placed, out_specs=P(("row", "col"), None), check_vma=False
    )
```

profile of v0, /device:TPU:1, one launch (start us, length us, event | category | flops | bytes accessed | tf_op | source)
XLA Modules:
  0.0 616.5 jit_solution(12963927019934338547)
XLA Ops:
  7.4 30.8 %all_gather.18 = bf16[192,2048]{1,0:T(8,128)(2,1)} all-gather(bf16[192,128]{1,0:T(8,128)(2,1)} %param.24), channel_id=1, replica_groups=mesh['row'=8,'col'=16] {'col'}, dimensions={1}, use_global_device_ids=true | all-gather | bytes 835584 | tf_op jit(solution)/shard_map/all_gather | solution.py:91
  38.2 0.9 dynamic-slice_reduce_fusion
  39.2 1.5 gather_fusion.4
  40.7 1.5 gather_fusion.5
  42.2 1.5 gather_fusion.6
  43.7 0.6 gather_fusion
  44.3 0.8 select_convert_fusion
  45.1 0.9 select_convert_fusion.2
  47.2 63.3 %all-gather.5.cloned.1.call-done = bf16[1536,2048]{1,0:T(8,128)(2,1)} async-done(((bf16[192,2048]{1,0:T(8,128)(2,1)}), bf16[1536,2048]{1,0:T(8,128)(2,1)}) %all-gather.5.cloned.1.call-update) | async-done | bytes 6291472 | tf_op jit(solution)/shard_map/all_gather | solution.py:95
  110.5 3.8 fusion.55
  114.4 100.6 %all-reduce.3.cloned.1.call-done = (bf16[4,16,1536]{2,1,0:T(8,128)(2,1)}, bf16[4,16,2048]{2,1,0:T(8,128)(2,1)}, bf16[4,16,1536]{2,1,0:T(8,128)(2,1)}, bf16[4,16,1536]{2,1,0:T(8,128)(2,1)}) async-done(((bf16[4,16,1536]{2,1,0:T(8,128)(2,1)}, bf16[4,16,2048]{2,1,0:T(8,128)(2,1)}, bf16[4,16,1536]{2,1,0:T(8,128)(2,1)}, bf16[4,16,1536]{2,1,0:T(8,128)(2,1)}), (bf16[4,16,1536]{2,1,0:T(8,128)(2,1)}, ...) | async-done | bytes 851984 | tf_op jit(solution)/shard_map/psum | solution.py:115
  214.9 1.9 fusion.23
  216.9 0.3 subtract_convert_fusion.1
  217.4 0.7 copy.142
  218.2 0.6 slice.71
  219.0 27.7 %all_gather.22 = bf16[192,1536]{0,1:T(8,128)(2,1)S(1)} all-gather(bf16[192,96]{0,1:T(8,128)(2,1)S(1)} %copy.146), channel_id=1, replica_groups=mesh['row'=8,'col'=16] {'col'}, dimensions={1}, use_global_device_ids=true | all-gather | bytes 626688 | tf_op jit(solution)/shard_map/all_gather | solution.py:92
  246.7 1.1 copy.147
  248.3 1.2 reduce-window.11
  250.0 2.3 fusion.4
  252.3 1.0 slice.53
  253.3 1.4 copy.138
  254.8 0.9 copy.139
  255.8 6.7 %all-gather.7.cloned.1.call-done = bf16[2048,256]{0,1:T(8,128)(2,1)} async-done(((bf16[128,256]{0,1:T(8,128)(2,1)}), bf16[2048,256]{0,1:T(8,128)(2,1)}) %all-gather.7.cloned.1.call-update) | async-done | bytes 1048592 | tf_op jit(solution)/shard_map/all_gather | solution.py:146
  262.4 1.6 copy.143
  264.0 4.0 select_reduce_fusion
  268.1 4.5 copy-done.2
  272.6 4.0 fusion
  276.6 32.7 %all-gather.9.cloned.1.call-done = bf16[2048,256]{1,0:T(8,128)(2,1)} async-done(((bf16[128,256]{1,0:T(8,128)(2,1)}), bf16[2048,256]{1,0:T(8,128)(2,1)}) %all-gather.9.cloned.1.call-update) | async-done | bytes 1048592 | tf_op jit(solution)/shard_map/all_gather | solution.py:147
  309.4 6.3 %fusion.45 = bf16[2,768,128]{2,1,0:T(8,128)(2,1)S(1)} fusion(f32[2,768,2048]{2,1,0:T(8,128)} %copy-done.2, f32[2,768]{1,0:T(2,128)S(1)} %broadcast_maximum_fusion, pred[768,2048]{1,0:T(8,128)(4,1)S(1)} %fusion.4, f32[2,768]{1,0:T(2,128)S(1)} %fusion, bf16[2048,256]{1,0:T(8,128)(2,1)} %all-gather.9.cloned.1.call-done), kind=kOutput, calls=%fused_computation.50 | convolution fusion | flops 818282496 | bytes 15609856 | tf_op jit(solution)/shard_map/hqk,hkd->hqd/dot_general | solution.py:165
  315.9 0.5 fusion.21
  316.4 50.6 %all-gather.11.cloned.1.call-done = bf16[1536,1536]{1,0:T(8,128)(2,1)} async-done(((bf16[192,1536]{1,0:T(8,128)(2,1)}), bf16[1536,1536]{1,0:T(8,128)(2,1)}) %all-gather.11.cloned.1.call-update) | async-done | bytes 4718608 | tf_op jit(solution)/shard_map/all_gather | solution.py:96
  366.9 3.3 multiply_reduce_fusion.1
  370.2 0.9 copy-done.3
  371.2 2.1 gather_fusion.1
  373.4 2.1 broadcast_in_dim.160
  375.5 80.2 %scatter_fusion = bf16[32,40,1536]{2,1,0:T(8,128)(2,1)} fusion(bf16[32,40,1536]{2,1,0:T(8,128)(2,1)} %broadcast_in_dim.160, s32[512]{0:T(512)S(1)} %bitcast.137, bf16[512,1536]{1,0:T(8,128)(2,1)S(1)} %gather_fusion.1), kind=kCustom, calls=%fused_computation.7 | custom fusion | bytes 4722688 | tf_op jit(solution)/shard_map/scatter | solution.py:195
  455.7 55.2 %all_to_all.10 = bf16[16,2,40,1536]{3,2,1,0:T(8,128)(2,1)S(1)} all-to-all(bf16[16,2,40,1536]{3,2,1,0:T(8,128)(2,1)} %bitcast.135), channel_id=1, replica_groups=mesh['row'=8,'col'=16] {'col'}, dimensions={0} | all-to-all | bytes 7864320 | tf_op jit(solution)/shard_map/all_to_all | solution.py:198
  510.9 2.0 copy-done.6
  512.9 7.5 %fusion.8 = f32[2,16,40,768]{3,2,1,0:T(8,128)} fusion(bf16[2,1536,768]{2,1,0:T(8,128)(2,1)} %param.32, bf16[16,2,40,1536]{3,2,1,0:T(8,128)(2,1)S(1)} %all_to_all.10), kind=kOutput, calls=%fused_computation.18 | convolution fusion | flops 3019898880 | bytes 12582912 | tf_op jit(solution)/shard_map/sjcd,jdf->sjcf/dot_general | solution.py:202
  520.4 12.6 %fusion.15 = bf16[16,2,40,1536]{3,2,0,1:T(8,128)(2,1)} fusion(bf16[2,768,1536]{2,1,0:T(8,128)(2,1)} %param.33, f32[2,16,40,768]{3,2,1,0:T(8,128)} %fusion.8, bf16[2,1536,768]{2,1,0:T(8,128)(2,1)} %param.31, bf16[16,2,40,1536]{3,2,1,0:T(8,128)(2,1)} %copy-done.6), kind=kOutput, calls=%fused_computation.24 | convolution fusion | flops 6044712960 | bytes 21233664 | tf_op jit(solution)/shard_map/sjcf,jfd->sjcd/dot_general | solution.py:206
  533.0 4.5 copy.155
  537.5 5.3 all-to-all-start.1
  543.2 3.8 gather_fusion.3
  547.4 43.6 %all-to-all-done.1 = bf16[16,2,40,1536]{3,2,1,0:T(8,128)(2,1)} async-done(((bf16[16,2,40,1536]{3,2,1,0:T(8,128)(2,1)}), bf16[16,2,40,1536]{3,2,1,0:T(8,128)(2,1)}, u32[]{:S(2)}, u32[]{:S(2)}) %all-to-all-start.1) | async-done | bytes 3932192 | tf_op jit(solution)/shard_map/all_to_all | solution.py:209
  591.0 11.9 %gather_fusion.2 = bf16[512,1536]{1,0:T(8,128)(2,1)} fusion(bf16[32,40,1536]{2,1,0:T(8,128)(2,1)} %bitcast.37, s32[512]{0:T(512)S(1)} %bitcast.136), kind=kCustom, calls=%fused_computation.5 | custom fusion | bytes 3149824 | tf_op jit(solution)/shard_map/gather | solution.py:210
  602.9 2.9 reshape.450
  605.8 2.2 multiply_reduce_fusion
  608.1 0.8 add_convert_fusion
  (89 shorter events, 4.0 us)
Async XLA Ops:
  7.4 36.3 %copy-start = (bf16[4,16,2048]{2,1,0:T(8,128)(2,1)S(1)}, bf16[4,16,2048]{2,1,0:T(8,128)(2,1)}, u32[]{:S(2)}) copy-start(bf16[4,16,2048]{2,1,0:T(8,128)(2,1)} %param.28) | copy-start | bytes 786436
  7.4 39.0 %copy-start.12 = (bf16[1536]{0:T(1024)(128)(2,1)S(1)}, bf16[1536]{0:T(1024)(128)(2,1)}, u32[]{:S(2)}) copy-start(bf16[1536]{0:T(1024)(128)(2,1)} %param.22) | copy-start | bytes 9220
  7.4 39.0 %copy-start.5 = (bf16[128,1536]{1,0:T(8,128)(2,1)S(1)}, bf16[128,1536]{1,0:T(8,128)(2,1)}, u32[]{:S(2)}) copy-start(bf16[128,1536]{1,0:T(8,128)(2,1)} %param.18) | copy-start | bytes 1179652
  7.4 103.1 %all-gather.5.cloned.1.call-start = ((), (), s32[]{:S(2)}) async-start(), calls=%async_computation.2 | async-start | bytes 7077888 | tf_op jit(solution)/shard_map/all_gather | solution.py:95
  38.2 176.7 %all-reduce.3.cloned.1.call-start = ((), (), s32[]{:S(2)}) async-start(), calls=%async_computation.6 | async-start | bytes 1703936 | tf_op jit(solution)/shard_map/psum | solution.py:115
  46.1 216.4 %all-gather.7.cloned.1.call-start = ((), (), s32[]{:S(2)}) async-start(), calls=%async_computation.3 | async-start | bytes 1114112 | tf_op jit(solution)/shard_map/all_gather | solution.py:146
  114.3 104.6 %copy-start.10 = (bf16[192,96]{1,0:T(8,128)(2,1)S(1)}, bf16[192,96]{1,0:T(8,128)(2,1)}, u32[]{:S(2)}) copy-start(bf16[192,96]{1,0:T(8,128)(2,1)} %param.25) | copy-start | bytes 110596
  114.3 133.5 %copy-start.11 = (s32[128,4]{0,1:T(4,128)S(1)}, s32[128,4]{0,1:T(4,128)}, u32[]{:S(2)}) copy-start(s32[128,4]{0,1:T(4,128)} %param.21) | copy-start | bytes 6148
  114.3 133.9 %copy-start.13 = (bf16[1536]{0:T(1024)(128)(2,1)S(1)}, bf16[1536]{0:T(1024)(128)(2,1)}, u32[]{:S(2)}) copy-start(bf16[1536]{0:T(1024)(128)(2,1)} %param.23) | copy-start | bytes 9220
  218.1 91.2 %all-gather.9.cloned.1.call-start = ((), (), s32[]{:S(2)}) async-start(), calls=%async_computation.4 | async-start | bytes 1114112 | tf_op jit(solution)/shard_map/all_gather | solution.py:147
  218.8 148.1 %all-gather.11.cloned.1.call-start = ((), (), s32[]{:S(2)}) async-start(), calls=%async_computation.5 | async-start | bytes 5308416 | tf_op jit(solution)/shard_map/all_gather | solution.py:96
  268.1 4.6 copy-start.2
  276.6 39.3 %copy-start.7 = (bf16[4,16,1536]{2,1,0:T(8,128)(2,1)S(1)}, bf16[4,16,1536]{2,1,0:T(8,128)(2,1)}, u32[]{:S(2)}) copy-start(bf16[4,16,1536]{2,1,0:T(8,128)(2,1)} %get-tuple-element.6) | copy-start | bytes 589828
  276.6 39.3 %copy-start.8 = (bf16[4,16,1536]{2,1,0:T(8,128)(2,1)S(1)}, bf16[4,16,1536]{2,1,0:T(8,128)(2,1)}, u32[]{:S(2)}) copy-start(bf16[4,16,1536]{2,1,0:T(8,128)(2,1)} %get-tuple-element.9) | copy-start | bytes 589828
  370.2 0.9 copy-start.3
  510.9 2.0 copy-start.6
  537.5 5.5 copy-start.9
  537.5 53.5 %all-to-all-start.1 = ((bf16[16,2,40,1536]{3,2,1,0:T(8,128)(2,1)}), bf16[16,2,40,1536]{3,2,1,0:T(8,128)(2,1)}, u32[]{:S(2)}, u32[]{:S(2)}) async-start(bf16[16,2,40,1536]{3,2,1,0:T(8,128)(2,1)} %copy.155), calls=%async_computation.1 | async-start | bytes 7864320 | tf_op jit(solution)/shard_map/all_to_all | solution.py:209
  602.9 6.0 copy-start.1
  605.8 2.2 copy-start.4
Sparse Core Ops, SparseCore 0:
  38.3 72.1 all-gather.4
Sparse Core Ops, SparseCore 1:
  46.1 168.7 all-reduce.2
  218.2 44.1 all-gather.6
  264.8 44.6 all-gather.8
  311.0 55.8 all-gather.10
where the time goes:
time: 620 us; the launch traced here: 617 us
  waiting for transfers between devices  298 us (48%)
  local copies, waits for them, and re-layouts  130 us (21%)
  blocking collectives  114 us (18%)
  matrix products  40 us (6%)
  between operations  15.6 us (3%)
  other arithmetic  14.1 us (2%)
    psum x1, waiting for transfers between devices, local(): lax.psum(choose_experts(adapter_output_up).astype(jnp.bfloat16), 'col')  101 us
    scatter x1, local copies, waits for them, and re-layouts, local(): dispatch_rows = jnp.zeros((expert_total, CAP, model_width), jnp.bfloat16)...  80.2 us
    all_gather x1, waiting for transfers between devices, local(): lax.all_gather(wide_parts[0], 'row', axis=0, tiled=True)  63.3 us
    all_to_all x1, blocking collectives, local(): lax.all_to_all(sending, 'col', split_axis=0, concat_axis=0, tiled=True)  55.2 us
    all_gather x1, waiting for transfers between devices, local(): lax.all_gather(wide_parts[1], 'row', axis=0, tiled=True)  50.6 us
    all_to_all x1, waiting for transfers between devices, local(): lax.all_to_all(answered, 'col', split_axis=0, concat_axis=0, tiled=True)  43.6 us
    all_gather x1, waiting for transfers between devices, local(): lax.all_gather(value_slice, 'col', axis=0, tiled=True)  32.7 us
    all_gather x1, blocking collectives, local(): lax.all_gather(projection_weight, 'col', axis=1, tiled=True)  30.8 us
  transfers between devices with their start and end apart: 6, of which 6 were waited for; matrix products, arithmetic and copies ran while one was open for 7% of the time, Pallas kernels for 0%

commit v1 on v0

--- a/solution.py
+++ b/solution.py
@@ -87,37 +87,41 @@
     adapter_row = lax.dynamic_index_in_dim(prompt_adapter, row_index, 0, keepdims=False)
     tok_index = col_index * token_rows + jnp.arange(token_rows, dtype=jnp.int32)
     prompt_of, within_prompt, token_positions = prompt_layout(lengths_row, tok_index)
-    wide_parts = (
-        lax.all_gather(projection_weight, "col", axis=1, tiled=True),
-        lax.all_gather(output_weight, "col", axis=1, tiled=True),
-    )
-    qkv_full, out_full = (
-        lax.all_gather(wide_parts[0], "row", axis=0, tiled=True),
-        lax.all_gather(wide_parts[1], "row", axis=0, tiled=True),
-    )
-    owner_column = adapter_row // adapter_projection_down.shape[0]
-    nearby_slot = adapter_row % adapter_projection_down.shape[0]
+    row_count = lax.axis_size("row")
+
+    def gather_whole(block):
+        rows_here, cols_here = block.shape
+        pieces = lax.all_gather(block[None], ("row", "col"), axis=0, tiled=True)
+        pieces = pieces.reshape(row_count, columns, rows_here, cols_here).transpose(0, 2, 1, 3)
+        return pieces.reshape(row_count * rows_here, columns * cols_here)
+
+    qkv_full = gather_whole(projection_weight)
+    out_full = gather_whole(output_weight)
+    local_adapters = adapter_projection_down.shape[0]
+    owner_column = adapter_row // local_adapters
+    nearby_slot = adapter_row % local_adapters
     owned_here = (owner_column == col_index)[:, None, None]
-
-    def choose_experts(table):
-        return jnp.where(owned_here, jnp.take(table, nearby_slot, axis=0).astype(jnp.float32), 0.0)
-
-    summed = (
-        lax.psum(choose_experts(adapter_projection_down).astype(jnp.bfloat16), "col").astype(
-            jnp.float32
-        ),
-        lax.psum(choose_experts(adapter_projection_up).astype(jnp.bfloat16), "col").astype(
-            jnp.float32
-        ),
-        lax.psum(choose_experts(adapter_output_down).astype(jnp.bfloat16), "col").astype(
-            jnp.float32
-        ),
-        lax.psum(choose_experts(adapter_output_up).astype(jnp.bfloat16), "col").astype(jnp.float32),
-    )
-    projection_down_map = summed[0].astype(jnp.bfloat16)
-    projection_up_map = summed[1].astype(jnp.bfloat16)
-    output_down_map = summed[2].astype(jnp.bfloat16)
-    output_up_map = summed[3].astype(jnp.bfloat16)
+    tables = (adapter_projection_down, adapter_projection_up, adapter_output_down, adapter_output_up)
+    picked = jnp.concatenate(
+        [
+            jnp.where(owned_here, jnp.take(table, nearby_slot, axis=0), jnp.zeros((), table.dtype))
+            for table in tables
+        ],
+        axis=-1,
+    )
+    picked_shape = picked.shape
+    chunks = picked.reshape(columns, -1)
+    received = lax.all_to_all(chunks, "col", 0, 0, tiled=True)
+    reduced = jnp.sum(received.astype(jnp.float32), axis=0).astype(jnp.bfloat16)
+    spread = lax.all_to_all(
+        jnp.broadcast_to(reduced[None], (columns, reduced.shape[0])), "col", 0, 0, tiled=True
+    )
+    maps = spread.reshape(picked_shape)
+    widths = [table.shape[-1] for table in tables]
+    bounds = [sum(widths[:i]) for i in range(len(widths) + 1)]
+    projection_down_map, projection_up_map, output_down_map, output_up_map = [
+        maps[..., bounds[i] : bounds[i + 1]] for i in range(len(tables))
+    ]
     normalized = rms_scaled(hidden_input, attention_norm_gain)
     projection_all = jnp.dot(normalized, qkv_full, preferred_element_type=jnp.float32)
     projection_all = projection_all + adapter_scale * adapter_change(
@@ -142,10 +146,10 @@
     )
     query_index = jnp.tile(tok_index, QUERY_PER_KEY)
     query_prompt = jnp.tile(prompt_of, QUERY_PER_KEY)
-    segments = (
-        lax.all_gather(flattened_keys, "col", axis=0, tiled=True),
-        lax.all_gather(value_slice, "col", axis=0, tiled=True),
-    )
+    key_value = lax.all_gather(
+        jnp.concatenate([flattened_keys, value_slice], axis=1), "col", axis=0, tiled=True
+    )
+    segments = (key_value[:, : KEY_HEADS * HEAD_SIZE], key_value[:, KEY_HEADS * HEAD_SIZE :])
     best_experts = jnp.full((KEY_HEADS, QUERY_PER_KEY * token_rows), -1e30, jnp.float32)
     segment_length = segments[0].shape[0]
     key_lines = segments[0].reshape(segment_length, KEY_HEADS, HEAD_SIZE).transpose(1, 0, 2)
@@ -188,12 +192,13 @@
     local_experts = expert_gate_weight.shape[0]
     flat_routes = routes.reshape(-1)
     slots = route_slots(flat_routes, expert_total)
-    token_of = jnp.arange(flat_routes.shape[0], dtype=jnp.int32) // routes.shape[1]
-    dispatch_rows = (
-        jnp.zeros((expert_total, CAP, model_width), jnp.bfloat16)
-        .at[flat_routes, slots]
-        .set(normed_two[token_of])
-    )
+    slot_total = expert_total * CAP
+    route_id = (flat_routes * CAP + slots).reshape(token_rows, routes.shape[1])
+    matches = route_id[:, :, None] == jnp.arange(slot_total, dtype=jnp.int32)[None, None, :]
+    picks = jnp.sum(matches.astype(jnp.float32), axis=1)
+    dispatch_rows = jnp.dot(
+        picks.T.astype(jnp.bfloat16), normed_two, preferred_element_type=jnp.float32
+    ).astype(jnp.bfloat16)
     sending = dispatch_rows.reshape(columns, local_experts, CAP, model_width)
     arrived = lax.all_to_all(sending, "col", split_axis=0, concat_axis=0, tiled=True)
     gate_vals = jnp.einsum(
@@ -207,11 +212,12 @@
         "sjcf,jfd->sjcd", hidden_vals, expert_down_weight, preferred_element_type=jnp.float32
     ).astype(jnp.bfloat16)
     returned = lax.all_to_all(answered, "col", split_axis=0, concat_axis=0, tiled=True)
-    results = returned.reshape(expert_total, CAP, model_width)[flat_routes, slots]
-    combined = jnp.sum(
-        results.astype(jnp.float32).reshape(token_rows, routes.shape[1], model_width)
-        * mixing[:, :, None],
-        axis=1,
+    returned_rows = returned.reshape(slot_total, model_width)
+    mix_matrix = jnp.sum(jnp.where(matches, mixing[:, :, None], 0.0), axis=1)
+    mix_high = mix_matrix.astype(jnp.bfloat16)
+    mix_low = (mix_matrix - mix_high.astype(jnp.float32)).astype(jnp.bfloat16)
+    combined = jnp.dot(mix_high, returned_rows, preferred_element_type=jnp.float32) + jnp.dot(
+        mix_low, returned_rows, preferred_element_type=jnp.float32
     )
     return (residual.astype(jnp.float32) + combined).astype(jnp.bfloat16)
 

time: 620 us -> 641 us (1.034)
  waiting for transfers between devices: 298 us -> 382 us
  local copies, waits for them, and re-layouts: 130 us -> 56.2 us
  other arithmetic: 14.1 us -> 29.3 us
  blocking collectives: 114 us -> 103 us
  starting transfers between devices: 5.48 us -> 13.3 us
    all_gather x4 -> x3, waiting for transfers between devices: 153 us -> 348 us  [the longest x2 322 us: gather_whole(): pieces = lax.all_gather(block[None], ('row', 'col'), axis=0, tiled=True)]
    psum x1 -> x0, waiting for transfers between devices: 101 us -> none  [local(): lax.psum(choose_experts(adapter_output_up).astype(jnp.bfloat16), 'col')]
    scatter x1 -> x0, local copies, waits for them, and re-layouts: 80.2 us -> none  [local(): dispatch_rows = jnp.zeros((expert_total, CAP, model_width), jnp.bfloat16)...]
    all_gather x2 -> x0, blocking collectives: 58.5 us -> none  [the longest x1 30.8 us: local(): lax.all_gather(projection_weight, 'col', axis=1, tiled=True)]
    all_to_all x0 -> x1, blocking collectives: none -> 51.5 us  [local(): lax.all_to_all(answered, 'col', split_axis=0, concat_axis=0, tiled=True)]
    reshape x2 -> x4, local copies, waits for them, and re-layouts: 1.72 us -> 29.1 us  [the longest x2 16.3 us: gather_whole(): pieces.reshape(row_count, columns, rows_here, cols_here)]
    gather x6 -> x4, local copies, waits for them, and re-layouts: 19.1 us -> 5.03 us  [local(): jnp.take(table, nearby_slot, axis=0)]
    all_to_all x1 -> x2, waiting for transfers between devices: 43.6 us -> 32.5 us  [the longest x1 16.3 us: local(): received = lax.all_to_all(chunks, 'col', 0, 0, tiled=True)]
  transfers between devices with their start and end apart: 6 -> 5, of which waited for: 6 -> 5; matrix products, arithmetic and copies ran while one was open for 7% -> 12% of each run, Pallas kernels for 0% -> 0%
where the time goes in v1:
time: 641 us; the launch traced here: 635 us
  waiting for transfers between devices  382 us (60%)
  blocking collectives  103 us (16%)
  local copies, waits for them, and re-layouts  56.2 us (9%)
  matrix products  36.9 us (6%)
  other arithmetic  29.3 us (5%)
  between operations  13.9 us (2%)
  starting transfers between devices  13.3 us (2%)
    all_gather x2, waiting for transfers between devices, gather_whole(): pieces = lax.all_gather(block[None], ('row', 'col'), axis=0, tiled=True)  322 us
    all_to_all x1, blocking collectives, local(): lax.all_to_all(sending, 'col', split_axis=0, concat_axis=0, tiled=True)  51.9 us
    all_to_all x1, blocking collectives, local(): lax.all_to_all(answered, 'col', split_axis=0, concat_axis=0, tiled=True)  51.5 us
    all_gather x1, waiting for transfers between devices, local(): lax.all_gather(jnp.concatenate([flattened_keys, value_slice], axis=1), 'c...  25.8 us
    reshape x2, local copies, waits for them, and re-layouts, gather_whole(): pieces.reshape(row_count, columns, rows_here, cols_here)  16.3 us
    all_to_all x1, waiting for transfers between devices, local(): received = lax.all_to_all(chunks, 'col', 0, 0, tiled=True)  16.3 us
    all_to_all x1, waiting for transfers between devices, local(): lax.all_to_all(jnp.broadcast_to(reduced[None], (columns, reduced.shape[0]...  16.2 us
  transfers between devices with their start and end apart: 5, of which 5 were waited for; matrix products, arithmetic and copies ran while one was open for 12% of the time, Pallas kernels for 0%

profile of v1, /device:TPU:1, one launch (start us, length us, event | category | flops | bytes accessed | tf_op | source)
XLA Modules:
  0.0 634.5 jit_solution(12446009240998358325)
XLA Ops:
  6.5 0.7 all-gather.8.cloned.1.call-update
  7.3 0.7 all-gather.10.cloned.1.call-update
  8.0 0.9 dynamic-slice_reduce_fusion
  8.9 1.5 gather_fusion.2
  10.4 1.5 gather_fusion.3
  11.9 1.5 gather_fusion.4
  15.4 5.8 reduce.8
  21.1 1.6 reshape.465
  22.7 9.0 %all-to-all-start = ((bf16[16,2,13312]{2,1,0:T(2,128)(2,1)}), bf16[16,2,13312]{2,1,0:T(2,128)(2,1)S(1)}, u32[]{:S(2)}, u32[]{:S(2)}) async-start(bf16[16,2,13312]{2,1,0:T(2,128)(2,1)} %reshape.465), calls=%async_computation | async-start | bytes 1703936 | tf_op jit(solution)/shard_map/all_to_all | solution.py:114
  32.2 16.3 %all-to-all-done = bf16[16,2,13312]{2,1,0:T(2,128)(2,1)S(1)} async-done(((bf16[16,2,13312]{2,1,0:T(2,128)(2,1)}), bf16[16,2,13312]{2,1,0:T(2,128)(2,1)S(1)}, u32[]{:S(2)}, u32[]{:S(2)}) %all-to-all-start) | async-done | bytes 852000 | tf_op jit(solution)/shard_map/all_to_all | solution.py:114
  48.5 0.7 reshape.466
  49.2 1.7 reduce_sum.107
  50.9 0.9 broadcast_in_dim.171
  51.8 5.8 reduce.9
  57.6 1.6 reshape.467
  59.2 4.2 all-to-all-start.1
  64.0 16.2 %all-to-all-done.1 = bf16[16,2,13312]{2,1,0:T(2,128)(2,1)S(1)} async-done(((bf16[16,2,13312]{2,1,0:T(2,128)(2,1)}), bf16[16,2,13312]{2,1,0:T(2,128)(2,1)S(1)}, u32[]{:S(2)}, u32[]{:S(2)}) %all-to-all-start.1) | async-done | bytes 852000 | tf_op jit(solution)/shard_map/all_to_all | solution.py:116
  80.3 0.9 reshape.468
  81.2 5.1 reduce.4
  86.3 1.6 reshape.385
  87.9 139.6 %all-gather.8.cloned.1.call-done = bf16[24576,128]{1,0:T(8,128)(2,1)} async-done(((bf16[192,128]{1,0:T(8,128)(2,1)}), bf16[24576,128]{1,0:T(8,128)(2,1)}) %all-gather.8.cloned.1.call-update) | async-done | bytes 6291472 | tf_op jit(solution)/shard_map/all_gather | solution.py:94
  227.5 6.8 %copy.150 = bf16[8,16,192,128]{3,1,2,0:T(8,128)(2,1)S(1)} copy(bf16[8,16,192,128]{3,2,1,0:T(8,128)(2,1)} %bitcast.153) | data formatting | bytes 12582912 | tf_op jit(solution)/shard_map/reshape | solution.py:95
  234.3 2.2 fusion.2
  236.5 2.5 fusion.27
  241.0 1.2 reduce-window.11
  242.9 2.3 fusion.7
  245.2 182.3 %all-gather.10.cloned.1.call-done = bf16[24576,96]{1,0:T(8,128)(2,1)} async-done(((bf16[192,96]{1,0:T(8,128)(2,1)}), bf16[24576,96]{1,0:T(8,128)(2,1)}) %all-gather.10.cloned.1.call-update) | async-done | bytes 4718608 | tf_op jit(solution)/shard_map/all_gather | solution.py:94
  427.5 9.5 %copy.210 = bf16[8,16,192,96]{3,1,2,0:T(8,128)(2,1)} copy(bf16[8,16,192,96]{3,2,1,0:T(8,128)(2,1)} %bitcast.152) | data formatting | bytes 9437184 | tf_op jit(solution)/shard_map/reshape | solution.py:95
  437.0 11.2 %reshape.393 = bf16[1536,1536]{1,0:T(8,128)(2,1)} reshape(bf16[8,192,16,96]{3,2,1,0:T(8,128)(2,1)} %bitcast.150) | data formatting | bytes 9437184 | tf_op jit(solution)/shard_map/reshape | solution.py:96
  448.2 1.0 slice.73
  449.1 1.4 copy.152
  450.9 25.8 %all-gather.6.cloned.1.call-done = bf16[2048,512]{1,0:T(8,128)(2,1)} async-done(((bf16[128,512]{1,0:T(8,128)(2,1)}), bf16[2048,512]{1,0:T(8,128)(2,1)}) %all-gather.6.cloned.1.call-update) | async-done | bytes 2097168 | tf_op jit(solution)/shard_map/all_gather | solution.py:149
  476.7 1.9 slice_bitcast_fusion.1
  478.6 3.1 select_reduce_fusion
  481.7 4.1 fusion
  485.9 2.6 fusion.50
  488.8 1.5 fusion.25
  490.3 3.3 multiply_reduce_fusion
  493.9 3.8 gather_fusion.1
  498.5 1.3 convolution_convert_fusion
  499.8 51.9 %all_to_all.26 = bf16[16,2,40,1536]{3,2,1,0:T(8,128)(2,1)S(1)} all-to-all(bf16[16,2,40,1536]{3,2,1,0:T(8,128)(2,1)S(1)} %bitcast.151), channel_id=1, replica_groups=mesh['row'=8,'col'=16] {'col'}, dimensions={0} | all-to-all | bytes 7864320 | tf_op jit(solution)/shard_map/all_to_all | solution.py:203
  551.8 1.9 copy-done.2
  553.7 5.2 fusion.11
  558.8 12.6 %fusion.18 = bf16[16,2,40,1536]{3,2,0,1:T(8,128)(2,1)} fusion(bf16[2,768,1536]{2,1,0:T(8,128)(2,1)} %param.33, f32[2,16,40,768]{3,2,1,0:T(8,128)} %fusion.11, bf16[2,1536,768]{2,1,0:T(8,128)(2,1)} %param.31, bf16[16,2,40,1536]{3,2,1,0:T(8,128)(2,1)} %copy-done.2), kind=kOutput, calls=%fused_computation.26 | convolution fusion | flops 6044712960 | bytes 21233664 | tf_op jit(solution)/shard_map/sjcf,jfd->sjcd/dot_general | solution.py:211
  571.5 2.6 copy.169
  574.1 51.5 %all_to_all.27 = bf16[16,2,40,1536]{3,2,1,0:T(8,128)(2,1)S(1)} all-to-all(bf16[16,2,40,1536]{3,2,1,0:T(8,128)(2,1)S(1)} %copy.169), channel_id=1, replica_groups=mesh['row'=8,'col'=16] {'col'}, dimensions={0} | all-to-all | bytes 7864320 | tf_op jit(solution)/shard_map/all_to_all | solution.py:214
  625.5 0.7 fusion.66
  626.2 1.6 fusion.30
  (88 shorter events, 7.3 us)
Async XLA Ops:
  6.5 6.9 %copy-start = (bf16[4,16,2048]{2,1,0:T(8,128)(2,1)S(1)}, bf16[4,16,2048]{2,1,0:T(8,128)(2,1)}, u32[]{:S(2)}) copy-start(bf16[4,16,2048]{2,1,0:T(8,128)(2,1)} %param.28) | copy-start | bytes 786436
  6.5 220.9 %all-gather.8.cloned.1.call-start = ((), (), s32[]{:S(2)}) async-start(), calls=%async_computation.5 | async-start | bytes 6340608 | tf_op jit(solution)/shard_map/all_gather | solution.py:94
  7.3 420.2 %all-gather.10.cloned.1.call-start = ((), (), s32[]{:S(2)}) async-start(), calls=%async_computation.6 | async-start | bytes 6340608 | tf_op jit(solution)/shard_map/all_gather | solution.py:94
  14.3 17.4 %copy-start.7 = (bf16[1536]{0:T(1024)(128)(2,1)S(1)}, bf16[1536]{0:T(1024)(128)(2,1)}, u32[]{:S(2)}) copy-start(bf16[1536]{0:T(1024)(128)(2,1)} %param.22) | copy-start | bytes 9220
  22.7 25.8 %all-to-all-start = ((bf16[16,2,13312]{2,1,0:T(2,128)(2,1)}), bf16[16,2,13312]{2,1,0:T(2,128)(2,1)S(1)}, u32[]{:S(2)}, u32[]{:S(2)}) async-start(bf16[16,2,13312]{2,1,0:T(2,128)(2,1)} %reshape.465), calls=%async_computation | async-start | bytes 1703936 | tf_op jit(solution)/shard_map/all_to_all | solution.py:114
  50.9 12.9 %copy-start.3 = (bf16[128,1536]{1,0:T(8,128)(2,1)S(1)}, bf16[128,1536]{1,0:T(8,128)(2,1)}, u32[]{:S(2)}) copy-start(bf16[128,1536]{1,0:T(8,128)(2,1)} %param.18) | copy-start | bytes 1179652
  59.2 21.1 %all-to-all-start.1 = ((bf16[16,2,13312]{2,1,0:T(2,128)(2,1)}), bf16[16,2,13312]{2,1,0:T(2,128)(2,1)S(1)}, u32[]{:S(2)}, u32[]{:S(2)}) async-start(bf16[16,2,13312]{2,1,0:T(2,128)(2,1)} %reshape.467), calls=%async_computation.1 | async-start | bytes 1703936 | tf_op jit(solution)/shard_map/all_to_all | solution.py:116
  63.4 413.3 %all-gather.6.cloned.1.call-start = ((), (), s32[]{:S(2)}) async-start(), calls=%async_computation.4 | async-start | bytes 2228224 | tf_op jit(solution)/shard_map/all_gather | solution.py:149
  234.3 2.2 copy-start.4
  236.5 3.8 copy-start.6
  236.5 4.2 copy-start.8
  490.3 3.3 copy-start.5
  498.5 55.1 %slice-start = ((s8[4718592]{0:T(1024)(128)(4,1)}), s8[4194304]{0:T(1024)(128)(4,1)S(1)}, s32[]{:S(2)}) async-start(s8[4718592]{0:T(1024)(128)(4,1)} %bitcast.167), calls=%async_computation.7 | async-start | bytes 8388608
  499.8 53.9 %slice-start.1 = ((s8[4718592]{0:T(1024)(128)(4,1)}), s8[524288]{0:T(1024)(128)(4,1)S(1)}, s32[]{:S(2)}) async-start(s8[4718592]{0:T(1024)(128)(4,1)} %bitcast.167), calls=%async_computation.8 | async-start | bytes 1048576
  551.8 1.9 copy-start.2
  625.5 2.3 copy-start.1
Sparse Core Ops, SparseCore 0:
  9.1 218.3 all-gather.7
  229.2 198.2 all-gather.9
  429.9 46.7 all-gather.5

commit v2 on v1

--- a/solution.py
+++ b/solution.py
@@ -87,16 +87,34 @@
     adapter_row = lax.dynamic_index_in_dim(prompt_adapter, row_index, 0, keepdims=False)
     tok_index = col_index * token_rows + jnp.arange(token_rows, dtype=jnp.int32)
     prompt_of, within_prompt, token_positions = prompt_layout(lengths_row, tok_index)
-    row_count = lax.axis_size("row")
-
-    def gather_whole(block):
-        rows_here, cols_here = block.shape
-        pieces = lax.all_gather(block[None], ("row", "col"), axis=0, tiled=True)
-        pieces = pieces.reshape(row_count, columns, rows_here, cols_here).transpose(0, 2, 1, 3)
-        return pieces.reshape(row_count * rows_here, columns * cols_here)
-
-    qkv_full = gather_whole(projection_weight)
-    out_full = gather_whole(output_weight)
+    core_index = col_index % 2
+    partner = [(c, c ^ 1) for c in range(columns)]
+
+    def gather_halves(block):
+        rows_here = block.shape[0]
+        slab = lax.all_gather(block.T, "col", axis=0, tiled=True).T
+        half = slab.shape[1] // 2
+        own = lax.dynamic_slice_in_dim(slab, core_index * half, half, axis=1)
+        own = lax.all_gather(own, "row", axis=0, tiled=True)
+        other = lax.ppermute(own, "col", partner)
+        return own, other
+
+    def times_halves(inputs, halves):
+        own, other = halves
+        half = own.shape[1]
+        placed = jnp.zeros((inputs.shape[0], 2 * half), jnp.float32)
+        placed = lax.dynamic_update_slice_in_dim(
+            placed, jnp.dot(inputs, own, preferred_element_type=jnp.float32), core_index * half, 1
+        )
+        return lax.dynamic_update_slice_in_dim(
+            placed,
+            jnp.dot(inputs, other, preferred_element_type=jnp.float32),
+            (1 - core_index) * half,
+            1,
+        )
+
+    qkv_halves = gather_halves(projection_weight)
+    out_halves = gather_halves(output_weight)
     local_adapters = adapter_projection_down.shape[0]
     owner_column = adapter_row // local_adapters
     nearby_slot = adapter_row % local_adapters
@@ -123,7 +141,7 @@
         maps[..., bounds[i] : bounds[i + 1]] for i in range(len(tables))
     ]
     normalized = rms_scaled(hidden_input, attention_norm_gain)
-    projection_all = jnp.dot(normalized, qkv_full, preferred_element_type=jnp.float32)
+    projection_all = times_halves(normalized, qkv_halves)
     projection_all = projection_all + adapter_scale * adapter_change(
         normalized, within_prompt, projection_down_map, projection_up_map
     )
@@ -146,9 +164,14 @@
     )
     query_index = jnp.tile(tok_index, QUERY_PER_KEY)
     query_prompt = jnp.tile(prompt_of, QUERY_PER_KEY)
-    key_value = lax.all_gather(
-        jnp.concatenate([flattened_keys, value_slice], axis=1), "col", axis=0, tiled=True
-    )
+    key_value_piece = jnp.concatenate([flattened_keys, value_slice], axis=1)
+    key_value = lax.all_to_all(
+        jnp.broadcast_to(key_value_piece[None], (columns,) + key_value_piece.shape),
+        "col",
+        0,
+        0,
+        tiled=True,
+    ).reshape(columns * token_rows, key_value_piece.shape[1])
     segments = (key_value[:, : KEY_HEADS * HEAD_SIZE], key_value[:, KEY_HEADS * HEAD_SIZE :])
     best_experts = jnp.full((KEY_HEADS, QUERY_PER_KEY * token_rows), -1e30, jnp.float32)
     segment_length = segments[0].shape[0]
@@ -179,7 +202,7 @@
         .reshape(token_rows, QUERY_HEADS * HEAD_SIZE)
         .astype(jnp.bfloat16)
     )
-    projected_rows = jnp.dot(attention_result, out_full, preferred_element_type=jnp.float32)
+    projected_rows = times_halves(attention_result, out_halves)
     projected_rows = projected_rows + adapter_scale * adapter_change(
         attention_result, within_prompt, output_down_map, output_up_map
     )

time: 641 us -> 399 us (0.62)
  waiting for transfers between devices: 382 us -> 74.1 us
  blocking collectives: 103 us -> 165 us
  local copies, waits for them, and re-layouts: 56.2 us -> 35.6 us
  matrix products: 36.9 us -> 47.7 us
  other arithmetic: 29.3 us -> 36.2 us
    all_gather x3 -> x2, waiting for transfers between devices: 348 us -> 32.5 us  [gather_halves(): own = lax.all_gather(own, 'row', axis=0, tiled=True)]
    all_gather x0 -> x2, blocking collectives: none -> 61.4 us  [gather_halves(): slab = lax.all_gather(block.T, 'col', axis=0, tiled=True).T]
    reshape x3, local copies, waits for them, and re-layouts: 27.5 us -> 3.91 us  [the longest x1 2.28 us: local(): segments[0].reshape(segment_length, KEY_HEADS, HEAD_SIZE).transpose(1, 0, 2)]
    all_to_all x0 -> x1, waiting for transfers between devices: none -> 18.2 us  [local(): lax.all_to_all(jnp.broadcast_to(key_value_piece[None], (columns,) + key_v...]
    all_to_all x1, waiting for transfers between devices: 16.3 us -> 0.01 us  [local(): received = lax.all_to_all(chunks, 'col', 0, 0, tiled=True)]
    all_to_all x1, waiting for transfers between devices: 16.2 us -> 23.5 us  [local(): lax.all_to_all(jnp.broadcast_to(reduced[None], (columns, reduced.shape[0]...]
  transfers between devices with their start and end apart: 5 -> 7, of which waited for: 5 -> 3; matrix products, arithmetic and copies ran while one was open for 12% -> 21% of each run, Pallas kernels for 0% -> 0%
where the time goes in v2:
time: 399 us; the launch traced here: 393 us
  blocking collectives  165 us (41%)
  waiting for transfers between devices  74.1 us (19%)
  matrix products  47.7 us (12%)
  other arithmetic  36.2 us (9%)
  local copies, waits for them, and re-layouts  35.6 us (9%)
  starting transfers between devices  19.6 us (5%)
  between operations  14.3 us (4%)
    all_gather x2, blocking collectives, gather_halves(): slab = lax.all_gather(block.T, 'col', axis=0, tiled=True).T  61.4 us
    all_to_all x1, blocking collectives, local(): lax.all_to_all(sending, 'col', split_axis=0, concat_axis=0, tiled=True)  52.2 us
    all_to_all x1, blocking collectives, local(): lax.all_to_all(answered, 'col', split_axis=0, concat_axis=0, tiled=True)  51.5 us
    all_gather x2, waiting for transfers between devices, gather_halves(): own = lax.all_gather(own, 'row', axis=0, tiled=True)  32.5 us
    all_to_all x1, waiting for transfers between devices, local(): lax.all_to_all(jnp.broadcast_to(reduced[None], (columns, reduced.shape[0]...  23.5 us
    all_to_all x1, waiting for transfers between devices, local(): lax.all_to_all(jnp.broadcast_to(key_value_piece[None], (columns,) + key_v...  18.2 us
    dot_general x1, matrix products, local(): jnp.einsum('sjcf,jfd->sjcd', hidden_vals, expert_down_weight, preferred_e...  12.6 us
    dot_general x1, matrix products, local(): jnp.einsum('hqd,hkd->hqk', grouped, key_lines, preferred_element_type=jnp...  8.73 us
  transfers between devices with their start and end apart: 7, of which 3 were waited for; matrix products, arithmetic and copies ran while one was open for 21% of the time, Pallas kernels for 0%

profile of v2, /device:TPU:1, one launch (start us, length us, event | category | flops | bytes accessed | tf_op | source)
XLA Modules:
  0.0 392.6 jit_solution(17117590972583606410)
XLA Ops:
  6.5 29.7 %all_gather.12 = bf16[2048,192]{0,1:T(8,128)(2,1)S(1)} all-gather(bf16[128,192]{0,1:T(8,128)(2,1)} %bitcast.160), channel_id=1, replica_groups=mesh['row'=8,'col'=16] {'col'}, dimensions={0}, use_global_device_ids=true | all-gather | bytes 835584 | tf_op jit(solution)/shard_map/all_gather | solution.py:95
  37.1 0.9 dynamic-slice_reduce_fusion
  38.0 1.5 gather_fusion.2
  39.5 1.5 gather_fusion.3
  41.0 1.5 gather_fusion.4
  43.3 32.5 %all-gather.3.cloned.1.call-done = bf16[1536,1024]{1,0:T(8,128)(2,1)} async-done(((bf16[192,1024]{1,0:T(8,128)(2,1)}), bf16[1536,1024]{1,0:T(8,128)(2,1)}) %all-gather.3.cloned.1.call-update) | async-done | bytes 3145744 | tf_op jit(solution)/shard_map/all_gather | solution.py:98
  75.8 3.0 collective-permute-start
  80.0 5.8 %reduce.8 = bf16[16,26624]{1,0:T(8,128)(2,1)S(1)} reduce(bf16[16,1,26624]{2,1,0:T(2,128)(2,1)S(1)} %all_to_all.25, bf16[]{:T(256)} %broadcast.406), dimensions={1}, to_apply=%all_to_all.25.reduce_sub_computation | reduce | bytes 1703938 | tf_op jit(solution)/shard_map/all_to_all | solution.py:132
  85.9 1.5 reshape.448
  87.4 6.5 %all-to-all-start = ((bf16[16,2,13312]{2,1,0:T(2,128)(2,1)}), bf16[16,2,13312]{2,1,0:T(2,128)(2,1)S(1)}, u32[]{:S(2)}, u32[]{:S(2)}) async-start(bf16[16,2,13312]{2,1,0:T(2,128)(2,1)} %reshape.448), calls=%async_computation | async-start | bytes 1703936 | tf_op jit(solution)/shard_map/all_to_all | solution.py:132
  94.1 31.6 %all_gather.14 = bf16[1536,192]{1,0:T(8,128)(2,1)S(1)} all-gather(bf16[96,192]{1,0:T(8,128)(2,1)S(1)} %bitcast.159), channel_id=1, replica_groups=mesh['row'=8,'col'=16] {'col'}, dimensions={0}, use_global_device_ids=true | all-gather | bytes 626688 | tf_op jit(solution)/shard_map/all_gather | solution.py:95
  128.6 1.7 reduce_sum.107
  130.2 0.9 broadcast_in_dim.178
  131.1 5.8 %reduce.9 = bf16[16,26624]{1,0:T(8,128)(2,1)S(1)} reduce(bf16[16,1,26624]{2,1,0:T(2,128)(2,1)S(1)} %broadcast_in_dim.178, bf16[]{:T(256)} %broadcast.406), dimensions={1}, to_apply=%broadcast_in_dim.178.reduce_sub_computation | reduce | bytes 1703938 | tf_op jit(solution)/shard_map/broadcast_in_dim | solution.py:135
  137.0 1.5 reshape.450
  138.5 5.2 %all-to-all-start.1 = ((bf16[16,2,13312]{2,1,0:T(2,128)(2,1)}), bf16[16,2,13312]{2,1,0:T(2,128)(2,1)S(1)}, u32[]{:S(2)}, u32[]{:S(2)}) async-start(bf16[16,2,13312]{2,1,0:T(2,128)(2,1)} %reshape.450), calls=%async_computation.1 | async-start | bytes 1703936 | tf_op jit(solution)/shard_map/all_to_all | solution.py:134
  144.6 23.5 %all-to-all-done.1 = bf16[16,2,13312]{2,1,0:T(2,128)(2,1)S(1)} async-done(((bf16[16,2,13312]{2,1,0:T(2,128)(2,1)}), bf16[16,2,13312]{2,1,0:T(2,128)(2,1)S(1)}, u32[]{:S(2)}, u32[]{:S(2)}) %all-to-all-start.1) | async-done | bytes 852000 | tf_op jit(solution)/shard_map/all_to_all | solution.py:134
  168.7 5.1 %reduce.4 = bf16[16,26624]{1,0:T(8,128)(2,1)S(1)} reduce(bf16[16,1,26624]{2,1,0:T(2,128)(2,1)S(1)} %reshape.451, bf16[]{:T(256)} %constant.171), dimensions={1}, to_apply=%all_to_all.21.reduce_sub_computation | reduce | bytes 1703938 | tf_op jit(solution)/shard_map/all_to_all | solution.py:134
  173.9 1.6 reshape.373
  175.6 2.5 convolution_dynamic-update-slice_fusion.1
  178.1 2.5 convolution_dynamic-update-slice_fusion
  180.6 1.9 fusion.25
  183.3 1.8 broadcast_in_dim.183
  185.1 4.4 %all-to-all-start.2 = ((bf16[16,128,512]{1,2,0:T(8,128)(2,1)}), bf16[16,128,512]{1,2,0:T(8,128)(2,1)S(1)}, u32[]{:S(2)}, u32[]{:S(2)}) async-start(bf16[16,128,512]{1,2,0:T(8,128)(2,1)} %broadcast_in_dim.183), calls=%async_computation.2 | async-start | bytes 4194304 | tf_op jit(solution)/shard_map/all_to_all | solution.py:168
  189.9 2.3 reduce-window.11
  192.8 3.2 fusion.4
  196.4 1.2 copy.154
  197.6 1.2 subtract_convert_fusion.1
  198.8 0.9 copy.155
  199.7 18.2 %all-to-all-done.2 = bf16[16,128,512]{1,2,0:T(8,128)(2,1)S(1)} async-done(((bf16[16,128,512]{1,2,0:T(8,128)(2,1)}), bf16[16,128,512]{1,2,0:T(8,128)(2,1)S(1)}, u32[]{:S(2)}, u32[]{:S(2)}) %all-to-all-start.2) | async-done | bytes 2097184 | tf_op jit(solution)/shard_map/all_to_all | solution.py:168
  218.2 1.1 fusion.92
  219.4 2.3 copy.160
  221.6 8.7 %select_reduce_fusion = (f32[2,768]{1,0:T(2,128)S(1)}, f32[2,768,2048]{2,1,0:T(8,128)}) fusion(pred[768,2048]{1,0:T(8,128)(4,1)S(1)} %copy-done.4, bf16[2,768,128]{2,1,0:T(8,128)(2,1)} %bitcast.155, bf16[2048,2,128]{2,0,1:T(8,128)(2,1)} %copy.160), kind=kOutput, calls=%fused_computation.6 | convolution fusion | flops 814742016 | bytes 15603712 | tf_op jit(solution)/shard_map/hqd,hkd->hqk/dot_general | solution.py:185
  230.4 1.3 copy.161
  231.7 7.9 %fusion = f32[2,768]{1,0:T(2,128)S(1)} fusion(f32[2,768,2048]{2,1,0:T(8,128)} %get-tuple-element.23, f32[2,768]{1,0:T(2,128)S(1)} %broadcast_maximum_fusion, pred[768,2048]{1,0:T(8,128)(4,1)S(1)} %copy-done.4), kind=kLoop, calls=%fused_computation.7 | loop fusion | flops 12581376 | bytes 14168064 | tf_op jit(solution)/shard_map/reduce_sum | solution.py:191
  240.2 4.4 %fusion.50 = bf16[2,768,128]{2,1,0:T(8,128)(2,1)S(1)} fusion(bf16[2048,2,128]{2,0,1:T(8,128)(2,1)S(1)} %copy-done.7, f32[2,768,2048]{2,1,0:T(8,128)S(1)} %copy-done.2, f32[2,768]{1,0:T(2,128)S(1)} %broadcast_maximum_fusion, pred[768,2048]{1,0:T(8,128)(4,1)S(1)} %copy-done.4, f32[2,768]{1,0:T(2,128)S(1)} %fusion), kind=kOutput, calls=%fused_computation.57 | convolution fusion | flops 818282496 | bytes 15609856 | tf_op jit(solution)/shard_map/hqk,hkd->hqd/dot_general | solution.py:192
  245.0 2.2 convolution_dynamic-update-slice_fusion.3
  247.2 2.2 convolution_dynamic-update-slice_fusion.2
  249.4 1.6 multiply_reduce_fusion
  251.4 3.8 gather_fusion.1
  256.0 1.3 convolution_convert_fusion
  257.3 52.2 %all_to_all.31 = bf16[16,2,40,1536]{3,2,1,0:T(8,128)(2,1)S(1)} all-to-all(bf16[16,2,40,1536]{3,2,1,0:T(8,128)(2,1)S(1)} %bitcast.146), channel_id=1, replica_groups=mesh['row'=8,'col'=16] {'col'}, dimensions={0} | all-to-all | bytes 7864320 | tf_op jit(solution)/shard_map/all_to_all | solution.py:226
  309.5 1.9 copy-done.6
  311.4 5.2 %fusion.8 = f32[2,16,40,768]{3,2,1,0:T(8,128)} fusion(bf16[2,1536,768]{2,1,0:T(8,128)(2,1)S(1)} %bitcast.165, bf16[16,2,40,1536]{3,2,1,0:T(8,128)(2,1)S(1)} %all_to_all.31), kind=kOutput, calls=%fused_computation.16 | convolution fusion | flops 3019898880 | bytes 12582912 | tf_op jit(solution)/shard_map/sjcd,jdf->sjcf/dot_general | solution.py:230
  316.6 12.6 %fusion.15 = bf16[16,2,40,1536]{3,2,0,1:T(8,128)(2,1)} fusion(bf16[2,768,1536]{2,1,0:T(8,128)(2,1)} %param.33, f32[2,16,40,768]{3,2,1,0:T(8,128)} %fusion.8, bf16[2,1536,768]{2,1,0:T(8,128)(2,1)} %param.31, bf16[16,2,40,1536]{3,2,1,0:T(8,128)(2,1)} %copy-done.6), kind=kOutput, calls=%fused_computation.22 | convolution fusion | flops 6044712960 | bytes 21233664 | tf_op jit(solution)/shard_map/sjcf,jfd->sjcd/dot_general | solution.py:234
  329.2 2.6 copy.174
  331.8 51.5 %all_to_all.32 = bf16[16,2,40,1536]{3,2,1,0:T(8,128)(2,1)S(1)} all-to-all(bf16[16,2,40,1536]{3,2,1,0:T(8,128)(2,1)S(1)} %copy.174), channel_id=1, replica_groups=mesh['row'=8,'col'=16] {'col'}, dimensions={0} | all-to-all | bytes 7864320 | tf_op jit(solution)/shard_map/all_to_all | solution.py:237
  384.0 1.6 fusion.28
  (114 shorter events, 12.5 us)
Async XLA Ops:
  6.5 36.0 %copy-start = (bf16[4,16,2048]{2,1,0:T(8,128)(2,1)S(1)}, bf16[4,16,2048]{2,1,0:T(8,128)(2,1)}, u32[]{:S(2)}) copy-start(bf16[4,16,2048]{2,1,0:T(8,128)(2,1)} %param.28) | copy-start | bytes 786436
  6.5 69.3 %all-gather.3.cloned.1.call-start = ((), (), s32[]{:S(2)}) async-start(), calls=%async_computation.5 | async-start | bytes 3538944 | tf_op jit(solution)/shard_map/all_gather | solution.py:98
  75.8 102.3 %collective-permute-start = (bf16[1536,1024]{1,0:T(8,128)(2,1)}, bf16[1536,1024]{1,0:T(8,128)(2,1)}, u32[]{:S(2)}, u32[]{:S(2)}) collective-permute-start(bf16[1536,1024]{1,0:T(8,128)(2,1)} %all-gather.3.cloned.1.call-done), channel_id=1, source_target_pairs={{0,1},{1,0},{2,3},{3,2},{4,5},{5,4},{6,7},{7,6},{8,9},{9,8},{10,11... | collective-permute-start | bytes 9437192 | tf_op jit(solution)/shard_map/ppermute | solution.py:99
  78.9 15.1 %copy-start.11 = (bf16[192,96]{1,0:T(8,128)(2,1)S(1)}, bf16[192,96]{1,0:T(8,128)(2,1)}, u32[]{:S(2)}) copy-start(bf16[192,96]{1,0:T(8,128)(2,1)} %param.25) | copy-start | bytes 110596
  80.0 47.0 %copy-start.12 = (bf16[1536]{0:T(1024)(128)(2,1)S(1)}, bf16[1536]{0:T(1024)(128)(2,1)}, u32[]{:S(2)}) copy-start(bf16[1536]{0:T(1024)(128)(2,1)} %param.22) | copy-start | bytes 9220
  80.0 47.6 %copy-start.10 = (s32[128,4]{0,1:T(4,128)S(1)}, s32[128,4]{0,1:T(4,128)}, u32[]{:S(2)}) copy-start(s32[128,4]{0,1:T(4,128)} %param.21) | copy-start | bytes 6148
  87.4 40.4 %all-to-all-start = ((bf16[16,2,13312]{2,1,0:T(2,128)(2,1)}), bf16[16,2,13312]{2,1,0:T(2,128)(2,1)S(1)}, u32[]{:S(2)}, u32[]{:S(2)}) async-start(bf16[16,2,13312]{2,1,0:T(2,128)(2,1)} %reshape.448), calls=%async_computation | async-start | bytes 1703936 | tf_op jit(solution)/shard_map/all_to_all | solution.py:132
  93.9 102.1 %all-gather.5.cloned.1.call-start = ((), (), s32[]{:S(2)}) async-start(), calls=%async_computation.6 | async-start | bytes 2654208 | tf_op jit(solution)/shard_map/all_gather | solution.py:98
  127.4 9.6 %copy-start.8 = (f32[128,64]{0,1:T(8,128)}, f32[128,64]{0,1:T(8,128)S(1)}, u32[]{:S(2)}) copy-start(f32[128,64]{0,1:T(8,128)S(1)} %get-tuple-element.17) | copy-start | bytes 98308
  130.2 13.5 %copy-start.3 = (bf16[128,1536]{1,0:T(8,128)(2,1)S(1)}, bf16[128,1536]{1,0:T(8,128)(2,1)}, u32[]{:S(2)}) copy-start(bf16[128,1536]{1,0:T(8,128)(2,1)} %param.18) | copy-start | bytes 1179652
  138.5 29.5 %all-to-all-start.1 = ((bf16[16,2,13312]{2,1,0:T(2,128)(2,1)}), bf16[16,2,13312]{2,1,0:T(2,128)(2,1)S(1)}, u32[]{:S(2)}, u32[]{:S(2)}) async-start(bf16[16,2,13312]{2,1,0:T(2,128)(2,1)} %reshape.450), calls=%async_computation.1 | async-start | bytes 1703936 | tf_op jit(solution)/shard_map/all_to_all | solution.py:134
  182.5 2.5 copy-start.5
  182.7 6.9 %copy-start.13 = (bf16[1536]{0:T(1024)(128)(2,1)S(1)}, bf16[1536]{0:T(1024)(128)(2,1)}, u32[]{:S(2)}) copy-start(bf16[1536]{0:T(1024)(128)(2,1)} %param.23) | copy-start | bytes 9220
  185.1 32.8 %all-to-all-start.2 = ((bf16[16,128,512]{1,2,0:T(8,128)(2,1)}), bf16[16,128,512]{1,2,0:T(8,128)(2,1)S(1)}, u32[]{:S(2)}, u32[]{:S(2)}) async-start(bf16[16,128,512]{1,2,0:T(8,128)(2,1)} %broadcast_in_dim.183), calls=%async_computation.2 | async-start | bytes 4194304 | tf_op jit(solution)/shard_map/all_to_all | solution.py:168
  189.5 6.9 %slice-start = ((f32[128,2048]{1,0:T(8,128)}), f32[128,1536]{1,0:T(8,128)S(1)}, s32[]{:S(2)}) async-start(f32[128,2048]{1,0:T(8,128)} %copy-done.5), calls=%async_computation.7 | async-start | bytes 1572864 | tf_op jit(solution)/shard_map/slice | solution.py:149
  196.0 51.2 %collective-permute-start.1 = (bf16[1536,768]{1,0:T(8,128)(2,1)}, bf16[1536,768]{1,0:T(8,128)(2,1)}, u32[]{:S(2)}, u32[]{:S(2)}) collective-permute-start(bf16[1536,768]{1,0:T(8,128)(2,1)} %all-gather.5.cloned.1.call-done), channel_id=1, source_target_pairs={{0,1},{1,0},{2,3},{3,2},{4,5},{5,4},{6,7},{7,6},{8,9},{9,8},{10,11... | collective-permute-start | bytes 7077896 | tf_op jit(solution)/shard_map/ppermute | solution.py:99
  218.2 3.4 copy-start.4
  231.7 8.3 %copy-start.2 = (f32[2,768,2048]{2,1,0:T(8,128)S(1)}, f32[2,768,2048]{2,1,0:T(8,128)}, u32[]{:S(2)}) copy-start(f32[2,768,2048]{2,1,0:T(8,128)} %get-tuple-element.23) | copy-start | bytes 37748740
  231.7 8.5 %copy-start.7 = (bf16[2048,2,128]{2,0,1:T(8,128)(2,1)S(1)}, bf16[2048,2,128]{2,0,1:T(8,128)(2,1)}, u32[]{:S(2)}) copy-start(bf16[2048,2,128]{2,0,1:T(8,128)(2,1)} %copy.161) | copy-start | bytes 3145732
  245.0 6.1 %copy-start.9 = (bf16[1536,32]{0,1:T(8,128)(2,1)S(1)}, bf16[1536,32]{0,1:T(8,128)(2,1)}, u32[]{:S(2)}) copy-start(bf16[1536,32]{0,1:T(8,128)(2,1)} %param.26) | copy-start | bytes 294916
  256.0 55.4 %slice-start.1 = ((s8[4718592]{0:T(1024)(128)(4,1)}), s8[4194304]{0:T(1024)(128)(4,1)S(1)}, s32[]{:S(2)}) async-start(s8[4718592]{0:T(1024)(128)(4,1)} %bitcast.164), calls=%async_computation.8 | async-start | bytes 8388608
  257.3 54.1 %slice-start.2 = ((s8[4718592]{0:T(1024)(128)(4,1)}), s8[524288]{0:T(1024)(128)(4,1)S(1)}, s32[]{:S(2)}) async-start(s8[4718592]{0:T(1024)(128)(4,1)} %bitcast.164), calls=%async_computation.9 | async-start | bytes 1048576
  309.5 1.9 copy-start.6
  383.3 2.3 copy-start.1
Sparse Core Ops, SparseCore 0:
  37.2 38.5 all-gather.2
  126.8 42.0 all-gather.4

commit v3 on v2

--- a/solution.py
+++ b/solution.py
@@ -91,8 +91,11 @@
     partner = [(c, c ^ 1) for c in range(columns)]
 
     def gather_halves(block):
-        rows_here = block.shape[0]
-        slab = lax.all_gather(block.T, "col", axis=0, tiled=True).T
+        rows_here, cols_here = block.shape
+        slab = lax.all_to_all(
+            jnp.broadcast_to(block[None], (columns, rows_here, cols_here)), "col", 0, 0, tiled=True
+        )
+        slab = slab.transpose(1, 0, 2).reshape(rows_here, columns * cols_here)
         half = slab.shape[1] // 2
         own = lax.dynamic_slice_in_dim(slab, core_index * half, half, axis=1)
         own = lax.all_gather(own, "row", axis=0, tiled=True)

time: 399 us -> 383 us (0.960)
  blocking collectives: 165 us -> 104 us
  waiting for transfers between devices: 74.1 us -> 104 us
  starting transfers between devices: 19.6 us -> 33 us
    all_gather x2 -> x0, blocking collectives: 61.4 us -> none  [gather_halves(): slab = lax.all_gather(block.T, 'col', axis=0, tiled=True).T]
    all_to_all x0 -> x2, waiting for transfers between devices: none -> 13.9 us  [gather_halves(): lax.all_to_all(jnp.broadcast_to(block[None], (columns, rows_here, cols_he...]
    all_to_all x0 -> x2, starting transfers between devices: none -> 13.9 us  [gather_halves(): lax.all_to_all(jnp.broadcast_to(block[None], (columns, rows_here, cols_he...]
    all_to_all x1, waiting for transfers between devices: 0.01 us -> 9.99 us  [local(): received = lax.all_to_all(chunks, 'col', 0, 0, tiled=True)]
    all_gather x2, waiting for transfers between devices: 32.5 us -> 39.4 us  [gather_halves(): own = lax.all_gather(own, 'row', axis=0, tiled=True)]
  transfers between devices with their start and end apart: 7 -> 9, of which waited for: 3 -> 5; matrix products, arithmetic and copies ran while one was open for 21% -> 22% of each run, Pallas kernels for 0% -> 0%
where the time goes in v3:
time: 383 us; the launch traced here: 376 us
  waiting for transfers between devices  104 us (27%)
  blocking collectives  104 us (27%)
  matrix products  47.7 us (12%)
  local copies, waits for them, and re-layouts  37.5 us (10%)
  other arithmetic  36.1 us (9%)
  starting transfers between devices  33 us (9%)
  between operations  14.6 us (4%)
    all_to_all x1, blocking collectives, local(): lax.all_to_all(sending, 'col', split_axis=0, concat_axis=0, tiled=True)  52.2 us
    all_to_all x1, blocking collectives, local(): lax.all_to_all(answered, 'col', split_axis=0, concat_axis=0, tiled=True)  51.5 us
    all_gather x2, waiting for transfers between devices, gather_halves(): own = lax.all_gather(own, 'row', axis=0, tiled=True)  39.4 us
    all_to_all x1, waiting for transfers between devices, local(): lax.all_to_all(jnp.broadcast_to(reduced[None], (columns, reduced.shape[0]...  22.2 us
    all_to_all x1, waiting for transfers between devices, local(): lax.all_to_all(jnp.broadcast_to(key_value_piece[None], (columns,) + key_v...  18.1 us
    all_to_all x2, waiting for transfers between devices, gather_halves(): lax.all_to_all(jnp.broadcast_to(block[None], (columns, rows_here, cols_he...  13.9 us
    all_to_all x2, starting transfers between devices, gather_halves(): lax.all_to_all(jnp.broadcast_to(block[None], (columns, rows_here, cols_he...  13.9 us
    dot_general x1, matrix products, local(): jnp.einsum('sjcf,jfd->sjcd', hidden_vals, expert_down_weight, preferred_e...  12.6 us
  transfers between devices with their start and end apart: 9, of which 5 were waited for; matrix products, arithmetic and copies ran while one was open for 22% of the time, Pallas kernels for 0%

profile of v3, /device:TPU:1, one launch (start us, length us, event | category | flops | bytes accessed | tf_op | source)
XLA Modules:
  0.0 376.3 jit_solution(12186196569600556870)
XLA Ops:
  6.6 1.9 broadcast_in_dim.183
  8.5 8.6 %all-to-all-start = ((bf16[16,192,128]{2,1,0:T(8,128)(2,1)}), bf16[16,192,128]{2,1,0:T(8,128)(2,1)S(1)}, u32[]{:S(2)}, u32[]{:S(2)}) async-start(bf16[16,192,128]{2,1,0:T(8,128)(2,1)} %broadcast_in_dim.183), calls=%async_computation | async-start | bytes 1572864 | tf_op jit(solution)/shard_map/all_to_all | solution.py:95
  17.1 13.9 %all-to-all-done = bf16[16,192,128]{2,1,0:T(8,128)(2,1)S(1)} async-done(((bf16[16,192,128]{2,1,0:T(8,128)(2,1)}), bf16[16,192,128]{2,1,0:T(8,128)(2,1)S(1)}, u32[]{:S(2)}, u32[]{:S(2)}) %all-to-all-start) | async-done | bytes 786464 | tf_op jit(solution)/shard_map/all_to_all | solution.py:95
  31.9 1.1 broadcast_in_dim.200
  33.1 5.3 %all-to-all-start.4 = ((bf16[16,192,96]{2,1,0:T(8,128)(2,1)}), bf16[16,192,96]{2,1,0:T(8,128)(2,1)}, u32[]{:S(2)}, u32[]{:S(2)}) async-start(bf16[16,192,96]{2,1,0:T(8,128)(2,1)} %broadcast_in_dim.200), calls=%async_computation.4 | async-start | bytes 1572864 | tf_op jit(solution)/shard_map/all_to_all | solution.py:95
  41.2 39.4 %all-gather.3.cloned.1.call-done = bf16[1536,1024]{1,0:T(8,128)(2,1)} async-done(((bf16[192,1024]{1,0:T(8,128)(2,1)}), bf16[1536,1024]{1,0:T(8,128)(2,1)}) %all-gather.3.cloned.1.call-update) | async-done | bytes 3145744 | tf_op jit(solution)/shard_map/all_gather | solution.py:101
  80.5 2.5 collective-permute-start
  84.2 5.8 %reduce.8 = bf16[16,26624]{1,0:T(8,128)(2,1)S(1)} reduce(bf16[16,1,26624]{2,1,0:T(2,128)(2,1)S(1)} %all_to_all.33, bf16[]{:T(256)} %broadcast.408), dimensions={1}, to_apply=%all_to_all.33.reduce_sub_computation | reduce | bytes 1703938 | tf_op jit(solution)/shard_map/all_to_all | solution.py:135
  90.0 1.5 reshape.458
  91.8 6.6 %all-to-all-start.1 = ((bf16[16,2,13312]{2,1,0:T(2,128)(2,1)}), bf16[16,2,13312]{2,1,0:T(2,128)(2,1)S(1)}, u32[]{:S(2)}, u32[]{:S(2)}) async-start(bf16[16,2,13312]{2,1,0:T(2,128)(2,1)} %reshape.458), calls=%async_computation.1 | async-start | bytes 1703936 | tf_op jit(solution)/shard_map/all_to_all | solution.py:135
  99.2 1.6 copy.166
  103.1 10.0 %all-to-all-done.1 = bf16[16,2,13312]{2,1,0:T(2,128)(2,1)S(1)} async-done(((bf16[16,2,13312]{2,1,0:T(2,128)(2,1)}), bf16[16,2,13312]{2,1,0:T(2,128)(2,1)S(1)}, u32[]{:S(2)}, u32[]{:S(2)}) %all-to-all-start.1) | async-done | bytes 852000 | tf_op jit(solution)/shard_map/all_to_all | solution.py:135
  113.8 1.7 reduce_sum.107
  116.4 5.8 %reduce.9 = bf16[16,26624]{1,0:T(8,128)(2,1)S(1)} reduce(bf16[16,1,26624]{2,1,0:T(2,128)(2,1)S(1)} %broadcast_in_dim.191, bf16[]{:T(256)} %broadcast.408), dimensions={1}, to_apply=%broadcast_in_dim.191.reduce_sub_computation | reduce | bytes 1703938 | tf_op jit(solution)/shard_map/broadcast_in_dim | solution.py:138
  122.2 1.5 reshape.460
  123.7 4.9 %all-to-all-start.2 = ((bf16[16,2,13312]{2,1,0:T(2,128)(2,1)}), bf16[16,2,13312]{2,1,0:T(2,128)(2,1)S(1)}, u32[]{:S(2)}, u32[]{:S(2)}) async-start(bf16[16,2,13312]{2,1,0:T(2,128)(2,1)} %reshape.460), calls=%async_computation.2 | async-start | bytes 1703936 | tf_op jit(solution)/shard_map/all_to_all | solution.py:137
  129.5 22.2 %all-to-all-done.2 = bf16[16,2,13312]{2,1,0:T(2,128)(2,1)S(1)} async-done(((bf16[16,2,13312]{2,1,0:T(2,128)(2,1)}), bf16[16,2,13312]{2,1,0:T(2,128)(2,1)S(1)}, u32[]{:S(2)}, u32[]{:S(2)}) %all-to-all-start.2) | async-done | bytes 852000 | tf_op jit(solution)/shard_map/all_to_all | solution.py:137
  152.4 5.1 %reduce.4 = bf16[16,26624]{1,0:T(8,128)(2,1)S(1)} reduce(bf16[16,1,26624]{2,1,0:T(2,128)(2,1)S(1)} %reshape.461, bf16[]{:T(256)} %constant.171), dimensions={1}, to_apply=%all_to_all.28.reduce_sub_computation | reduce | bytes 1703938 | tf_op jit(solution)/shard_map/all_to_all | solution.py:137
  157.6 1.6 reshape.382
  159.3 2.5 convolution_dynamic-update-slice_fusion.1
  161.8 2.5 convolution_dynamic-update-slice_fusion
  164.3 1.9 fusion.25
  167.0 1.8 broadcast_in_dim.196
  168.8 4.2 %all-to-all-start.3 = ((bf16[16,128,512]{1,2,0:T(8,128)(2,1)}), bf16[16,128,512]{1,2,0:T(8,128)(2,1)S(1)}, u32[]{:S(2)}, u32[]{:S(2)}) async-start(bf16[16,128,512]{1,2,0:T(8,128)(2,1)} %broadcast_in_dim.196), calls=%async_computation.3 | async-start | bytes 4194304 | tf_op jit(solution)/shard_map/all_to_all | solution.py:171
  173.3 2.3 reduce-window.11
  176.3 3.2 fusion.4
  179.9 1.2 copy.157
  181.1 1.2 subtract_convert_fusion.1
  182.3 0.9 copy.158
  183.3 18.1 %all-to-all-done.3 = bf16[16,128,512]{1,2,0:T(8,128)(2,1)S(1)} async-done(((bf16[16,128,512]{1,2,0:T(8,128)(2,1)}), bf16[16,128,512]{1,2,0:T(8,128)(2,1)S(1)}, u32[]{:S(2)}, u32[]{:S(2)}) %all-to-all-start.3) | async-done | bytes 2097184 | tf_op jit(solution)/shard_map/all_to_all | solution.py:171
  201.7 1.1 fusion.92
  202.8 2.3 copy.163
  205.1 8.7 %select_reduce_fusion = (f32[2,768]{1,0:T(2,128)S(1)}, f32[2,768,2048]{2,1,0:T(8,128)}) fusion(pred[768,2048]{1,0:T(8,128)(4,1)S(1)} %copy-done.4, bf16[2,768,128]{2,1,0:T(8,128)(2,1)} %bitcast.156, bf16[2048,2,128]{2,0,1:T(8,128)(2,1)} %copy.163), kind=kOutput, calls=%fused_computation.6 | convolution fusion | flops 814742016 | bytes 15603712 | tf_op jit(solution)/shard_map/hqd,hkd->hqk/dot_general | solution.py:188
  213.9 1.3 copy.164
  215.2 7.9 %fusion = f32[2,768]{1,0:T(2,128)S(1)} fusion(f32[2,768,2048]{2,1,0:T(8,128)} %get-tuple-element.23, f32[2,768]{1,0:T(2,128)S(1)} %broadcast_maximum_fusion, pred[768,2048]{1,0:T(8,128)(4,1)S(1)} %copy-done.4), kind=kLoop, calls=%fused_computation.7 | loop fusion | flops 12581376 | bytes 14168064 | tf_op jit(solution)/shard_map/reduce_sum | solution.py:194
  223.7 4.4 %fusion.50 = bf16[2,768,128]{2,1,0:T(8,128)(2,1)S(1)} fusion(bf16[2048,2,128]{2,0,1:T(8,128)(2,1)S(1)} %copy-done.7, f32[2,768,2048]{2,1,0:T(8,128)S(1)} %copy-done.2, f32[2,768]{1,0:T(2,128)S(1)} %broadcast_maximum_fusion, pred[768,2048]{1,0:T(8,128)(4,1)S(1)} %copy-done.4, f32[2,768]{1,0:T(2,128)S(1)} %fusion), kind=kOutput, calls=%fused_computation.57 | convolution fusion | flops 818282496 | bytes 15609856 | tf_op jit(solution)/shard_map/hqk,hkd->hqd/dot_general | solution.py:195
  228.5 2.2 convolution_dynamic-update-slice_fusion.3
  230.7 2.2 convolution_dynamic-update-slice_fusion.2
  232.9 1.6 multiply_reduce_fusion
  234.8 3.8 %gather_fusion.1 = f32[512]{0:T(512)S(1)} fusion(f32[128,32]{0,1:T(8,128)S(1)} %fusion.87, s32[512]{0:T(512)S(1)} %reshape.427), kind=kCustom, calls=%fused_computation.4 | custom fusion | bytes 8192 | tf_op jit(solution)/shard_map/jit(take_along_axis)/gather | solution.py:215
  239.5 1.3 convolution_convert_fusion
  240.8 52.2 %all_to_all.41 = bf16[16,2,40,1536]{3,2,1,0:T(8,128)(2,1)S(1)} all-to-all(bf16[16,2,40,1536]{3,2,1,0:T(8,128)(2,1)S(1)} %bitcast.147), channel_id=1, replica_groups=mesh['row'=8,'col'=16] {'col'}, dimensions={0} | all-to-all | bytes 7864320 | tf_op jit(solution)/shard_map/all_to_all | solution.py:229
  293.0 1.9 copy-done.6
  294.9 5.2 %fusion.8 = f32[2,16,40,768]{3,2,1,0:T(8,128)} fusion(bf16[2,1536,768]{2,1,0:T(8,128)(2,1)S(1)} %bitcast.164, bf16[16,2,40,1536]{3,2,1,0:T(8,128)(2,1)S(1)} %all_to_all.41), kind=kOutput, calls=%fused_computation.16 | convolution fusion | flops 3019898880 | bytes 12582912 | tf_op jit(solution)/shard_map/sjcd,jdf->sjcf/dot_general | solution.py:233
  300.1 12.6 %fusion.15 = bf16[16,2,40,1536]{3,2,0,1:T(8,128)(2,1)} fusion(bf16[2,768,1536]{2,1,0:T(8,128)(2,1)} %param.33, f32[2,16,40,768]{3,2,1,0:T(8,128)} %fusion.8, bf16[2,1536,768]{2,1,0:T(8,128)(2,1)} %param.31, bf16[16,2,40,1536]{3,2,1,0:T(8,128)(2,1)} %copy-done.6), kind=kOutput, calls=%fused_computation.22 | convolution fusion | flops 6044712960 | bytes 21233664 | tf_op jit(solution)/shard_map/sjcf,jfd->sjcd/dot_general | solution.py:237
  312.7 2.6 copy.176
  315.3 51.5 %all_to_all.42 = bf16[16,2,40,1536]{3,2,1,0:T(8,128)(2,1)S(1)} all-to-all(bf16[16,2,40,1536]{3,2,1,0:T(8,128)(2,1)S(1)} %copy.176), channel_id=1, replica_groups=mesh['row'=8,'col'=16] {'col'}, dimensions={0} | all-to-all | bytes 7864320 | tf_op jit(solution)/shard_map/all_to_all | solution.py:240
  367.5 1.6 fusion.28
  (129 shorter events, 16.5 us)
Async XLA Ops:
  6.5 33.8 %copy-start = (bf16[4,16,2048]{2,1,0:T(8,128)(2,1)S(1)}, bf16[4,16,2048]{2,1,0:T(8,128)(2,1)}, u32[]{:S(2)}) copy-start(bf16[4,16,2048]{2,1,0:T(8,128)(2,1)} %param.28) | copy-start | bytes 786436
  6.5 25.4 %copy-start.14 = (bf16[192,96]{1,0:T(8,128)(2,1)S(1)}, bf16[192,96]{1,0:T(8,128)(2,1)}, u32[]{:S(2)}) copy-start(bf16[192,96]{1,0:T(8,128)(2,1)} %param.25) | copy-start | bytes 110596
  6.5 31.8 %copy-start.18 = (s32[8,4]{0,1:T(4,128)S(1)}, s32[8,4]{0,1:T(4,128)}, u32[]{:S(2)}) copy-start(s32[8,4]{0,1:T(4,128)} %param.19) | copy-start | bytes 388
  6.5 31.8 %copy-start.17 = (s32[8,4]{0,1:T(4,128)S(1)}, s32[8,4]{0,1:T(4,128)}, u32[]{:S(2)}) copy-start(s32[8,4]{0,1:T(4,128)} %param.20) | copy-start | bytes 388
  6.5 32.0 %copy-start.9 = (bf16[4,16,1536]{2,1,0:T(8,128)(2,1)S(1)}, bf16[4,16,1536]{2,1,0:T(8,128)(2,1)}, u32[]{:S(2)}) copy-start(bf16[4,16,1536]{2,1,0:T(8,128)(2,1)} %param.27) | copy-start | bytes 589828
  6.5 32.6 %copy-start.10 = (bf16[4,16,1536]{2,1,0:T(8,128)(2,1)S(1)}, bf16[4,16,1536]{2,1,0:T(8,128)(2,1)}, u32[]{:S(2)}) copy-start(bf16[4,16,1536]{2,1,0:T(8,128)(2,1)} %param.29) | copy-start | bytes 589828
  8.4 31.3 %copy-start.11 = (bf16[4,16,1536]{2,1,0:T(8,128)(2,1)S(1)}, bf16[4,16,1536]{2,1,0:T(8,128)(2,1)}, u32[]{:S(2)}) copy-start(bf16[4,16,1536]{2,1,0:T(8,128)(2,1)} %param.30) | copy-start | bytes 589828
  8.5 22.5 %all-to-all-start = ((bf16[16,192,128]{2,1,0:T(8,128)(2,1)}), bf16[16,192,128]{2,1,0:T(8,128)(2,1)S(1)}, u32[]{:S(2)}, u32[]{:S(2)}) async-start(bf16[16,192,128]{2,1,0:T(8,128)(2,1)} %broadcast_in_dim.183), calls=%async_computation | async-start | bytes 1572864 | tf_op jit(solution)/shard_map/all_to_all | solution.py:95
  17.0 63.5 %all-gather.3.cloned.1.call-start = ((), (), s32[]{:S(2)}) async-start(), calls=%async_computation.7 | async-start | bytes 3538944 | tf_op jit(solution)/shard_map/all_gather | solution.py:101
  33.1 58.8 %all-to-all-start.4 = ((bf16[16,192,96]{2,1,0:T(8,128)(2,1)}), bf16[16,192,96]{2,1,0:T(8,128)(2,1)}, u32[]{:S(2)}, u32[]{:S(2)}) async-start(bf16[16,192,96]{2,1,0:T(8,128)(2,1)} %broadcast_in_dim.200), calls=%async_computation.4 | async-start | bytes 1572864 | tf_op jit(solution)/shard_map/all_to_all | solution.py:95
  80.5 81.3 %collective-permute-start = (bf16[1536,1024]{1,0:T(8,128)(2,1)}, bf16[1536,1024]{1,0:T(8,128)(2,1)}, u32[]{:S(2)}, u32[]{:S(2)}) collective-permute-start(bf16[1536,1024]{1,0:T(8,128)(2,1)} %all-gather.3.cloned.1.call-done), channel_id=1, source_target_pairs={{0,1},{1,0},{2,3},{3,2},{4,5},{5,4},{6,7},{7,6},{8,9},{9,8},{10,11... | collective-permute-start | bytes 9437192 | tf_op jit(solution)/shard_map/ppermute | solution.py:102
  83.1 15.9 %copy-start.15 = (bf16[1536]{0:T(1024)(128)(2,1)S(1)}, bf16[1536]{0:T(1024)(128)(2,1)}, u32[]{:S(2)}) copy-start(bf16[1536]{0:T(1024)(128)(2,1)} %param.22) | copy-start | bytes 9220
  90.0 12.9 %copy-start.13 = (s32[128,4]{0,1:T(4,128)S(1)}, s32[128,4]{0,1:T(4,128)}, u32[]{:S(2)}) copy-start(s32[128,4]{0,1:T(4,128)} %param.21) | copy-start | bytes 6148
  91.8 21.3 %all-to-all-start.1 = ((bf16[16,2,13312]{2,1,0:T(2,128)(2,1)}), bf16[16,2,13312]{2,1,0:T(2,128)(2,1)S(1)}, u32[]{:S(2)}, u32[]{:S(2)}) async-start(bf16[16,2,13312]{2,1,0:T(2,128)(2,1)} %reshape.458), calls=%async_computation.1 | async-start | bytes 1703936 | tf_op jit(solution)/shard_map/all_to_all | solution.py:135
  98.4 81.1 %all-gather.5.cloned.1.call-start = ((), (), s32[]{:S(2)}) async-start(), calls=%async_computation.8 | async-start | bytes 2654208 | tf_op jit(solution)/shard_map/all_gather | solution.py:101
  102.7 19.5 %copy-start.8 = (f32[128,64]{0,1:T(8,128)}, f32[128,64]{0,1:T(8,128)S(1)}, u32[]{:S(2)}) copy-start(f32[128,64]{0,1:T(8,128)S(1)} %get-tuple-element.17) | copy-start | bytes 98308
  115.5 13.2 %copy-start.3 = (bf16[128,1536]{1,0:T(8,128)(2,1)S(1)}, bf16[128,1536]{1,0:T(8,128)(2,1)}, u32[]{:S(2)}) copy-start(bf16[128,1536]{1,0:T(8,128)(2,1)} %param.18) | copy-start | bytes 1179652
  123.7 28.0 %all-to-all-start.2 = ((bf16[16,2,13312]{2,1,0:T(2,128)(2,1)}), bf16[16,2,13312]{2,1,0:T(2,128)(2,1)S(1)}, u32[]{:S(2)}, u32[]{:S(2)}) async-start(bf16[16,2,13312]{2,1,0:T(2,128)(2,1)} %reshape.460), calls=%async_computation.2 | async-start | bytes 1703936 | tf_op jit(solution)/shard_map/all_to_all | solution.py:137
  166.2 2.5 copy-start.5
  166.4 6.7 %copy-start.16 = (bf16[1536]{0:T(1024)(128)(2,1)S(1)}, bf16[1536]{0:T(1024)(128)(2,1)}, u32[]{:S(2)}) copy-start(bf16[1536]{0:T(1024)(128)(2,1)} %param.23) | copy-start | bytes 9220
  168.8 32.6 %all-to-all-start.3 = ((bf16[16,128,512]{1,2,0:T(8,128)(2,1)}), bf16[16,128,512]{1,2,0:T(8,128)(2,1)S(1)}, u32[]{:S(2)}, u32[]{:S(2)}) async-start(bf16[16,128,512]{1,2,0:T(8,128)(2,1)} %broadcast_in_dim.196), calls=%async_computation.3 | async-start | bytes 4194304 | tf_op jit(solution)/shard_map/all_to_all | solution.py:171
  173.0 6.9 %slice-start = ((f32[128,2048]{1,0:T(8,128)}), f32[128,1536]{1,0:T(8,128)S(1)}, s32[]{:S(2)}) async-start(f32[128,2048]{1,0:T(8,128)} %copy-done.5), calls=%async_computation.9 | async-start | bytes 1572864 | tf_op jit(solution)/shard_map/slice | solution.py:152
  179.5 51.2 %collective-permute-start.1 = (bf16[1536,768]{1,0:T(8,128)(2,1)}, bf16[1536,768]{1,0:T(8,128)(2,1)}, u32[]{:S(2)}, u32[]{:S(2)}) collective-permute-start(bf16[1536,768]{1,0:T(8,128)(2,1)} %all-gather.5.cloned.1.call-done), channel_id=1, source_target_pairs={{0,1},{1,0},{2,3},{3,2},{4,5},{5,4},{6,7},{7,6},{8,9},{9,8},{10,11... | collective-permute-start | bytes 7077896 | tf_op jit(solution)/shard_map/ppermute | solution.py:102
  201.7 3.4 copy-start.4
  215.2 8.3 %copy-start.2 = (f32[2,768,2048]{2,1,0:T(8,128)S(1)}, f32[2,768,2048]{2,1,0:T(8,128)}, u32[]{:S(2)}) copy-start(f32[2,768,2048]{2,1,0:T(8,128)} %get-tuple-element.23) | copy-start | bytes 37748740
  215.2 8.5 %copy-start.7 = (bf16[2048,2,128]{2,0,1:T(8,128)(2,1)S(1)}, bf16[2048,2,128]{2,0,1:T(8,128)(2,1)}, u32[]{:S(2)}) copy-start(bf16[2048,2,128]{2,0,1:T(8,128)(2,1)} %copy.164) | copy-start | bytes 3145732
  228.5 6.1 %copy-start.12 = (bf16[1536,32]{0,1:T(8,128)(2,1)S(1)}, bf16[1536,32]{0,1:T(8,128)(2,1)}, u32[]{:S(2)}) copy-start(bf16[1536,32]{0,1:T(8,128)(2,1)} %param.26) | copy-start | bytes 294916
  239.5 55.4 %slice-start.1 = ((s8[4718592]{0:T(1024)(128)(4,1)}), s8[4194304]{0:T(1024)(128)(4,1)S(1)}, s32[]{:S(2)}) async-start(s8[4718592]{0:T(1024)(128)(4,1)} %bitcast.163), calls=%async_computation.10 | async-start | bytes 8388608
  240.8 54.2 %slice-start.2 = ((s8[4718592]{0:T(1024)(128)(4,1)}), s8[524288]{0:T(1024)(128)(4,1)S(1)}, s32[]{:S(2)}) async-start(s8[4718592]{0:T(1024)(128)(4,1)} %bitcast.163), calls=%async_computation.11 | async-start | bytes 1048576
  293.0 1.9 copy-start.6
  366.8 2.3 copy-start.1
Sparse Core Ops, SparseCore 0:
  32.0 48.4 all-gather.2
  102.6 42.3 all-gather.4

commit v4 on v3

--- a/solution.py
+++ b/solution.py
@@ -87,6 +87,26 @@
     adapter_row = lax.dynamic_index_in_dim(prompt_adapter, row_index, 0, keepdims=False)
     tok_index = col_index * token_rows + jnp.arange(token_rows, dtype=jnp.int32)
     prompt_of, within_prompt, token_positions = prompt_layout(lengths_row, tok_index)
+    local_adapters = adapter_projection_down.shape[0]
+    owner_column = adapter_row // local_adapters
+    nearby_slot = adapter_row % local_adapters
+    owned_here = (owner_column == col_index)[:, None, None]
+    tables = (adapter_projection_down, adapter_projection_up, adapter_output_down, adapter_output_up)
+    picked = jnp.concatenate(
+        [
+            jnp.where(owned_here, jnp.take(table, nearby_slot, axis=0), jnp.zeros((), table.dtype))
+            for table in tables
+        ],
+        axis=-1,
+    )
+    picked_shape = picked.shape
+    lane = 128
+    chunks = picked.reshape(columns, -1, lane)
+    received = lax.all_to_all(chunks, "col", 0, 0, tiled=True)
+    reduced = jnp.sum(received.astype(jnp.float32), axis=0).astype(jnp.bfloat16)
+    spread = lax.all_to_all(
+        jnp.broadcast_to(reduced[None], (columns,) + reduced.shape), "col", 0, 0, tiled=True
+    )
     core_index = col_index % 2
     partner = [(c, c ^ 1) for c in range(columns)]
 
@@ -96,6 +116,7 @@
             jnp.broadcast_to(block[None], (columns, rows_here, cols_here)), "col", 0, 0, tiled=True
         )
         slab = slab.transpose(1, 0, 2).reshape(rows_here, columns * cols_here)
+        slab, _ = lax.optimization_barrier((slab, received))
         half = slab.shape[1] // 2
         own = lax.dynamic_slice_in_dim(slab, core_index * half, half, axis=1)
         own = lax.all_gather(own, "row", axis=0, tiled=True)
@@ -118,25 +139,6 @@
 
     qkv_halves = gather_halves(projection_weight)
     out_halves = gather_halves(output_weight)
-    local_adapters = adapter_projection_down.shape[0]
-    owner_column = adapter_row // local_adapters
-    nearby_slot = adapter_row % local_adapters
-    owned_here = (owner_column == col_index)[:, None, None]
-    tables = (adapter_projection_down, adapter_projection_up, adapter_output_down, adapter_output_up)
-    picked = jnp.concatenate(
-        [
-            jnp.where(owned_here, jnp.take(table, nearby_slot, axis=0), jnp.zeros((), table.dtype))
-            for table in tables
-        ],
-        axis=-1,
-    )
-    picked_shape = picked.shape
-    chunks = picked.reshape(columns, -1)
-    received = lax.all_to_all(chunks, "col", 0, 0, tiled=True)
-    reduced = jnp.sum(received.astype(jnp.float32), axis=0).astype(jnp.bfloat16)
-    spread = lax.all_to_all(
-        jnp.broadcast_to(reduced[None], (columns, reduced.shape[0])), "col", 0, 0, tiled=True
-    )
     maps = spread.reshape(picked_shape)
     widths = [table.shape[-1] for table in tables]
     bounds = [sum(widths[:i]) for i in range(len(widths) + 1)]

time: 383 us -> 365 us (0.953); the launches traced: 376 us -> 364 us
  other arithmetic: 36.1 us -> 23.6 us
  local copies, waits for them, and re-layouts: 37.5 us -> 46.7 us
  waiting for transfers between devices: 104 us -> 97.2 us
    all_to_all x1, waiting for transfers between devices: 18.1 us -> 2.47 us  [local(): lax.all_to_all(jnp.broadcast_to(key_value_piece[None], (columns,) + key_v...]
    all_to_all x2 -> x0, other arithmetic: 11 us -> none  [the longest x1 5.82 us: local(): received = lax.all_to_all(chunks, 'col', 0, 0, tiled=True)]
    broadcast_in_dim x1 -> x0, other arithmetic: 5.82 us -> none  [local(): jnp.broadcast_to(reduced[None], (columns, reduced.shape[0]))]
    all_to_all x2, waiting for transfers between devices: 13.9 us -> 18.6 us  [gather_halves(): lax.all_to_all(jnp.broadcast_to(block[None], (columns, rows_here, cols_he...]
    all_to_all x1, waiting for transfers between devices: 9.99 us -> 14.6 us  [local(): received = lax.all_to_all(chunks, 'col', 0, 0, tiled=True)]
  transfers between devices with their start and end apart: 9 -> 9, of which waited for: 5 -> 6; matrix products, arithmetic and copies ran while one was open for 22% -> 21% of each run, Pallas kernels for 0% -> 0%
where the time goes in v4:
time: 365 us; the launch traced here: 364 us
  blocking collectives  104 us (28%)
  waiting for transfers between devices  97.2 us (27%)
  local copies, waits for them, and re-layouts  46.7 us (13%)
  matrix products  45.6 us (12%)
  starting transfers between devices  32.4 us (9%)
  other arithmetic  23.6 us (6%)
  between operations  14.1 us (4%)
    all_to_all x1, blocking collectives, local(): lax.all_to_all(sending, 'col', split_axis=0, concat_axis=0, tiled=True)  52.7 us
    all_to_all x1, blocking collectives, local(): lax.all_to_all(answered, 'col', split_axis=0, concat_axis=0, tiled=True)  51.5 us
    all_gather x2, waiting for transfers between devices, gather_halves(): own = lax.all_gather(own, 'row', axis=0, tiled=True)  40.2 us
    all_to_all x1, waiting for transfers between devices, local(): lax.all_to_all(jnp.broadcast_to(reduced[None], (columns,) + reduced.shape...  21.3 us
    all_to_all x2, waiting for transfers between devices, gather_halves(): lax.all_to_all(jnp.broadcast_to(block[None], (columns, rows_here, cols_he...  18.6 us
    all_to_all x2, starting transfers between devices, gather_halves(): lax.all_to_all(jnp.broadcast_to(block[None], (columns, rows_here, cols_he...  15 us
    all_to_all x1, waiting for transfers between devices, local(): received = lax.all_to_all(chunks, 'col', 0, 0, tiled=True)  14.6 us
    dot_general x1, matrix products, local(): jnp.einsum('sjcf,jfd->sjcd', hidden_vals, expert_down_weight, preferred_e...  12.6 us
  transfers between devices with their start and end apart: 9, of which 6 were waited for; matrix products, arithmetic and copies ran while one was open for 21% of the time, Pallas kernels for 0%

profile of v4, /device:TPU:1, one launch (start us, length us, event | category | flops | bytes accessed | tf_op | source)
XLA Modules:
  0.0 363.7 jit_solution(4043901123092742651)
XLA Ops:
  6.5 1.9 broadcast_in_dim.183
  8.4 8.4 %all-to-all-start = ((bf16[16,192,128]{2,1,0:T(8,128)(2,1)}), bf16[16,192,128]{2,1,0:T(8,128)(2,1)S(1)}, u32[]{:S(2)}, u32[]{:S(2)}) async-start(bf16[16,192,128]{2,1,0:T(8,128)(2,1)} %broadcast_in_dim.183), calls=%async_computation | async-start | bytes 1572864 | tf_op jit(solution)/shard_map/all_to_all | solution.py:115
  17.8 1.5 gather_fusion.2
  19.3 1.5 gather_fusion.3
  20.8 1.5 gather_fusion.4
  23.2 2.0 reshape.375
  25.2 5.6 %all-to-all-done = bf16[16,192,128]{2,1,0:T(8,128)(2,1)S(1)} async-done(((bf16[16,192,128]{2,1,0:T(8,128)(2,1)}), bf16[16,192,128]{2,1,0:T(8,128)(2,1)S(1)}, u32[]{:S(2)}, u32[]{:S(2)}) %all-to-all-start) | async-done | bytes 786464 | tf_op jit(solution)/shard_map/all_to_all | solution.py:115
  30.8 4.7 %all-to-all-start.1 = ((bf16[16,208,128]{2,1,0:T(8,128)(2,1)}), bf16[16,208,128]{2,1,0:T(8,128)(2,1)S(1)}, u32[]{:S(2)}, u32[]{:S(2)}) async-start(bf16[16,208,128]{2,1,0:T(8,128)(2,1)} %reshape.375), calls=%async_computation.1 | async-start | bytes 1703936 | tf_op jit(solution)/shard_map/all_to_all | solution.py:105
  35.7 14.6 %all-to-all-done.1 = bf16[16,208,128]{2,1,0:T(8,128)(2,1)S(1)} async-done(((bf16[16,208,128]{2,1,0:T(8,128)(2,1)}), bf16[16,208,128]{2,1,0:T(8,128)(2,1)S(1)}, u32[]{:S(2)}, u32[]{:S(2)}) %all-to-all-start.1) | async-done | bytes 852000 | tf_op jit(solution)/shard_map/all_to_all | solution.py:105
  51.1 40.2 %all-gather.3.cloned.1.call-done = bf16[1536,1024]{1,0:T(8,128)(2,1)} async-done(((bf16[192,1024]{1,0:T(8,128)(2,1)}), bf16[1536,1024]{1,0:T(8,128)(2,1)}) %all-gather.3.cloned.1.call-update) | async-done | bytes 3145744 | tf_op jit(solution)/shard_map/all_gather | solution.py:122
  91.3 3.0 collective-permute-start
  95.4 6.5 %all-to-all-start.4 = ((bf16[16,192,96]{2,1,0:T(8,128)(2,1)}), bf16[16,192,96]{2,1,0:T(8,128)(2,1)S(1)}, u32[]{:S(2)}, u32[]{:S(2)}) async-start(bf16[16,192,96]{2,1,0:T(8,128)(2,1)} %broadcast_in_dim.200), calls=%async_computation.4 | async-start | bytes 1572864 | tf_op jit(solution)/shard_map/all_to_all | solution.py:115
  102.9 13.0 %all-to-all-done.4 = bf16[16,192,96]{2,1,0:T(8,128)(2,1)S(1)} async-done(((bf16[16,192,96]{2,1,0:T(8,128)(2,1)}), bf16[16,192,96]{2,1,0:T(8,128)(2,1)S(1)}, u32[]{:S(2)}, u32[]{:S(2)}) %all-to-all-start.4) | async-done | bytes 589856 | tf_op jit(solution)/shard_map/all_to_all | solution.py:115
  120.3 4.7 %all-to-all-start.2 = ((bf16[16,208,128]{2,1,0:T(8,128)(2,1)}), bf16[16,208,128]{2,1,0:T(8,128)(2,1)S(1)}, u32[]{:S(2)}, u32[]{:S(2)}) async-start(bf16[16,208,128]{2,1,0:T(8,128)(2,1)} %broadcast_in_dim.191), calls=%async_computation.2 | async-start | bytes 1703936 | tf_op jit(solution)/shard_map/all_to_all | solution.py:107
  125.9 21.3 %all-to-all-done.2 = bf16[16,208,128]{2,1,0:T(8,128)(2,1)S(1)} async-done(((bf16[16,208,128]{2,1,0:T(8,128)(2,1)}), bf16[16,208,128]{2,1,0:T(8,128)(2,1)S(1)}, u32[]{:S(2)}, u32[]{:S(2)}) %all-to-all-start.2) | async-done | bytes 852000 | tf_op jit(solution)/shard_map/all_to_all | solution.py:107
  148.2 2.8 convolution_dynamic-update-slice_fusion.1
  151.0 2.6 convolution_dynamic-update-slice_fusion
  155.3 1.7 broadcast_in_dim.196
  157.0 4.7 %all-to-all-start.3 = ((bf16[16,128,512]{1,2,0:T(8,128)(2,1)}), bf16[16,128,512]{1,2,0:T(8,128)(2,1)S(1)}, u32[]{:S(2)}, u32[]{:S(2)}) async-start(bf16[16,128,512]{1,2,0:T(8,128)(2,1)} %broadcast_in_dim.196), calls=%async_computation.3 | async-start | bytes 4194304 | tf_op jit(solution)/shard_map/all_to_all | solution.py:173
  161.7 1.5 eq.97
  165.6 3.2 reduce-window.11
  168.8 1.7 slice_reduce_fusion
  170.5 1.3 reduce-window.14
  172.4 1.5 fusion.72
  173.9 1.4 reduce_sum.111
  175.3 1.5 copy.141
  178.8 1.3 multiply_add_fusion
  180.1 3.1 fusion.4
  184.4 1.4 copy.127
  187.7 2.5 all-to-all-done.3
  190.5 1.1 fusion.92
  191.6 2.3 copy.133
  193.8 7.4 %select_reduce_fusion = (f32[2,768]{1,0:T(2,128)S(1)}, f32[2,768,2048]{2,1,0:T(8,128)}) fusion(pred[768,2048]{1,0:T(8,128)(4,1)S(1)} %copy-done.4, bf16[2,768,128]{2,1,0:T(8,128)(2,1)S(1)} %bitcast.157, bf16[2048,2,128]{2,0,1:T(8,128)(2,1)} %copy.133), kind=kOutput, calls=%fused_computation.6 | convolution fusion | flops 814742016 | bytes 15603712 | tf_op jit(solution)/shard_map/hqd,hkd->hqk/dot_general | solution.py:190
  201.3 1.3 copy.134
  202.6 7.9 %fusion = f32[2,768]{1,0:T(2,128)S(1)} fusion(f32[2,768,2048]{2,1,0:T(8,128)} %get-tuple-element.27, f32[2,768]{1,0:T(2,128)S(1)} %broadcast_maximum_fusion, pred[768,2048]{1,0:T(8,128)(4,1)S(1)} %copy-done.4), kind=kLoop, calls=%fused_computation.7 | loop fusion | flops 12581376 | bytes 14168064 | tf_op jit(solution)/shard_map/reduce_sum | solution.py:196
  211.1 4.5 %fusion.50 = bf16[2,768,128]{2,1,0:T(8,128)(2,1)S(1)} fusion(bf16[2048,2,128]{2,0,1:T(8,128)(2,1)S(1)} %copy-done.7, f32[2,768,2048]{2,1,0:T(8,128)S(1)} %copy-done.2, f32[2,768]{1,0:T(2,128)S(1)} %broadcast_maximum_fusion, pred[768,2048]{1,0:T(8,128)(4,1)S(1)} %copy-done.4, f32[2,768]{1,0:T(2,128)S(1)} %fusion), kind=kOutput, calls=%fused_computation.57 | convolution fusion | flops 818282496 | bytes 15609856 | tf_op jit(solution)/shard_map/hqk,hkd->hqd/dot_general | solution.py:197
  215.9 2.2 convolution_dynamic-update-slice_fusion.3
  218.2 2.2 convolution_dynamic-update-slice_fusion.2
  220.4 1.6 multiply_reduce_fusion
  222.3 3.8 %gather_fusion.1 = f32[512]{0:T(512)S(1)} fusion(f32[128,32]{0,1:T(8,128)S(1)} %fusion.87, s32[512]{0:T(512)S(1)} %reshape.421), kind=kCustom, calls=%fused_computation.4 | custom fusion | bytes 8192 | tf_op jit(solution)/shard_map/jit(take_along_axis)/gather | solution.py:217
  227.0 1.3 convolution_convert_fusion
  228.3 52.7 %all_to_all.35 = bf16[16,2,40,1536]{3,2,1,0:T(8,128)(2,1)S(1)} all-to-all(bf16[16,2,40,1536]{3,2,1,0:T(8,128)(2,1)S(1)} %bitcast.147), channel_id=1, replica_groups=mesh['row'=8,'col'=16] {'col'}, dimensions={0} | all-to-all | bytes 7864320 | tf_op jit(solution)/shard_map/all_to_all | solution.py:231
  280.9 1.9 copy-done.5
  282.8 5.1 %fusion.8 = f32[2,16,40,768]{3,2,1,0:T(8,128)} fusion(bf16[2,1536,768]{2,1,0:T(8,128)(2,1)S(1)} %bitcast.165, bf16[16,2,40,1536]{3,2,1,0:T(8,128)(2,1)S(1)} %all_to_all.35), kind=kOutput, calls=%fused_computation.16 | convolution fusion | flops 3019898880 | bytes 12582912 | tf_op jit(solution)/shard_map/sjcd,jdf->sjcf/dot_general | solution.py:235
  288.0 12.6 %fusion.15 = bf16[16,2,40,1536]{3,2,0,1:T(8,128)(2,1)} fusion(bf16[2,768,1536]{2,1,0:T(8,128)(2,1)} %param.33, f32[2,16,40,768]{3,2,1,0:T(8,128)} %fusion.8, bf16[2,1536,768]{2,1,0:T(8,128)(2,1)} %param.31, bf16[16,2,40,1536]{3,2,1,0:T(8,128)(2,1)} %copy-done.5), kind=kOutput, calls=%fused_computation.22 | convolution fusion | flops 6044712960 | bytes 21233664 | tf_op jit(solution)/shard_map/sjcf,jfd->sjcd/dot_general | solution.py:239
  300.6 2.6 copy.146
  303.2 51.5 %all_to_all.36 = bf16[16,2,40,1536]{3,2,1,0:T(8,128)(2,1)S(1)} all-to-all(bf16[16,2,40,1536]{3,2,1,0:T(8,128)(2,1)S(1)} %copy.146), channel_id=1, replica_groups=mesh['row'=8,'col'=16] {'col'}, dimensions={0} | all-to-all | bytes 7864320 | tf_op jit(solution)/shard_map/all_to_all | solution.py:242
  355.4 1.5 fusion.28
  (126 shorter events, 23.7 us)
Async XLA Ops:
  6.5 15.8 %copy-start = (bf16[4,16,2048]{2,1,0:T(8,128)(2,1)S(1)}, bf16[4,16,2048]{2,1,0:T(8,128)(2,1)}, u32[]{:S(2)}) copy-start(bf16[4,16,2048]{2,1,0:T(8,128)(2,1)} %param.28) | copy-start | bytes 786436
  8.4 22.4 %all-to-all-start = ((bf16[16,192,128]{2,1,0:T(8,128)(2,1)}), bf16[16,192,128]{2,1,0:T(8,128)(2,1)S(1)}, u32[]{:S(2)}, u32[]{:S(2)}) async-start(bf16[16,192,128]{2,1,0:T(8,128)(2,1)} %broadcast_in_dim.183), calls=%async_computation | async-start | bytes 1572864 | tf_op jit(solution)/shard_map/all_to_all | solution.py:115
  23.1 71.2 %copy-start.14 = (bf16[192,96]{1,0:T(8,128)(2,1)S(1)}, bf16[192,96]{1,0:T(8,128)(2,1)}, u32[]{:S(2)}) copy-start(bf16[192,96]{1,0:T(8,128)(2,1)} %param.25) | copy-start | bytes 110596
  23.2 78.7 %copy-start.16 = (bf16[1536]{0:T(1024)(128)(2,1)S(1)}, bf16[1536]{0:T(1024)(128)(2,1)}, u32[]{:S(2)}) copy-start(bf16[1536]{0:T(1024)(128)(2,1)} %param.22) | copy-start | bytes 9220
  30.8 19.4 %all-to-all-start.1 = ((bf16[16,208,128]{2,1,0:T(8,128)(2,1)}), bf16[16,208,128]{2,1,0:T(8,128)(2,1)S(1)}, u32[]{:S(2)}, u32[]{:S(2)}) async-start(bf16[16,208,128]{2,1,0:T(8,128)(2,1)} %reshape.375), calls=%async_computation.1 | async-start | bytes 1703936 | tf_op jit(solution)/shard_map/all_to_all | solution.py:105
  35.5 55.8 %all-gather.3.cloned.1.call-start = ((), (), s32[]{:S(2)}) async-start(), calls=%async_computation.7 | async-start | bytes 3538944 | tf_op jit(solution)/shard_map/all_gather | solution.py:122
  35.7 83.2 %copy-start.13 = (s32[128,4]{0,1:T(4,128)S(1)}, s32[128,4]{0,1:T(4,128)}, u32[]{:S(2)}) copy-start(s32[128,4]{0,1:T(4,128)} %param.21) | copy-start | bytes 6148
  91.3 59.7 %collective-permute-start = (bf16[1536,1024]{1,0:T(8,128)(2,1)}, bf16[1536,1024]{1,0:T(8,128)(2,1)}, u32[]{:S(2)}, u32[]{:S(2)}) collective-permute-start(bf16[1536,1024]{1,0:T(8,128)(2,1)} %all-gather.3.cloned.1.call-done), channel_id=1, source_target_pairs={{0,1},{1,0},{2,3},{3,2},{4,5},{5,4},{6,7},{7,6},{8,9},{9,8},{10,11... | collective-permute-start | bytes 9437192 | tf_op jit(solution)/shard_map/ppermute | solution.py:123
  95.4 20.5 %all-to-all-start.4 = ((bf16[16,192,96]{2,1,0:T(8,128)(2,1)}), bf16[16,192,96]{2,1,0:T(8,128)(2,1)S(1)}, u32[]{:S(2)}, u32[]{:S(2)}) async-start(bf16[16,192,96]{2,1,0:T(8,128)(2,1)} %broadcast_in_dim.200), calls=%async_computation.4 | async-start | bytes 1572864 | tf_op jit(solution)/shard_map/all_to_all | solution.py:115
  101.9 23.1 %copy-start.3 = (bf16[128,1536]{1,0:T(8,128)(2,1)S(1)}, bf16[128,1536]{1,0:T(8,128)(2,1)}, u32[]{:S(2)}) copy-start(bf16[128,1536]{1,0:T(8,128)(2,1)} %param.18) | copy-start | bytes 1179652
  101.9 81.3 %all-gather.5.cloned.1.call-start = ((), (), s32[]{:S(2)}) async-start(), calls=%async_computation.8 | async-start | bytes 2654208 | tf_op jit(solution)/shard_map/all_gather | solution.py:122
  102.2 0.5 copy-start.19
  102.3 22.7 %copy-start.20 = (s32[128]{0:T(128)}, s32[128]{0:T(128)S(1)}, u32[]{:S(2)}) copy-start(s32[128]{0:T(128)S(1)} %iota_add_fusion) | copy-start | bytes 1540
  102.4 22.8 %copy-start.21 = (s32[128]{0:T(128)}, s32[128]{0:T(128)S(1)}, u32[]{:S(2)}) copy-start(s32[128]{0:T(128)S(1)} %convert_reduce_fusion.2) | copy-start | bytes 1540
  118.2 0.6 copy-start.10
  118.2 0.6 copy-start.11
  119.1 31.9 %copy-start.8 = (s32[128,4]{1,0:T(8,128)}, s32[128,4]{1,0:T(8,128)S(1)}, u32[]{:S(2)}) copy-start(s32[128,4]{1,0:T(8,128)S(1)} %copy.138) | copy-start | bytes 6148
  120.3 26.8 %all-to-all-start.2 = ((bf16[16,208,128]{2,1,0:T(8,128)(2,1)}), bf16[16,208,128]{2,1,0:T(8,128)(2,1)S(1)}, u32[]{:S(2)}, u32[]{:S(2)}) async-start(bf16[16,208,128]{2,1,0:T(8,128)(2,1)} %broadcast_in_dim.191), calls=%async_computation.2 | async-start | bytes 1703936 | tf_op jit(solution)/shard_map/all_to_all | solution.py:107
  125.2 28.4 %copy-start.17 = (pred[128,4]{0,1:T(4,128)(4,1)}, pred[128,4]{0,1:T(4,128)(4,1)S(1)}, u32[]{:S(2)}) copy-start(pred[128,4]{0,1:T(4,128)(4,1)S(1)} %iota_compare_fusion.5) | copy-start | bytes 1540
  148.1 5.5 %copy-start.6 = (bf16[4,16,6656]{2,1,0:T(8,128)(2,1)}, bf16[4,16,6656]{2,1,0:T(8,128)(2,1)S(1)}, u32[]{:S(2)}) copy-start(bf16[4,16,6656]{2,1,0:T(8,128)(2,1)S(1)} %reshape.376) | copy-start | bytes 2555908
  157.0 33.1 %all-to-all-start.3 = ((bf16[16,128,512]{1,2,0:T(8,128)(2,1)}), bf16[16,128,512]{1,2,0:T(8,128)(2,1)S(1)}, u32[]{:S(2)}, u32[]{:S(2)}) async-start(bf16[16,128,512]{1,2,0:T(8,128)(2,1)} %broadcast_in_dim.196), calls=%async_computation.3 | async-start | bytes 4194304 | tf_op jit(solution)/shard_map/all_to_all | solution.py:173
  183.2 34.9 %collective-permute-start.1 = (bf16[1536,768]{1,0:T(8,128)(2,1)}, bf16[1536,768]{1,0:T(8,128)(2,1)}, u32[]{:S(2)}, u32[]{:S(2)}) collective-permute-start(bf16[1536,768]{1,0:T(8,128)(2,1)} %all-gather.5.cloned.1.call-done), channel_id=1, source_target_pairs={{0,1},{1,0},{2,3},{3,2},{4,5},{5,4},{6,7},{7,6},{8,9},{9,8},{10,11... | collective-permute-start | bytes 7077896 | tf_op jit(solution)/shard_map/ppermute | solution.py:123
  190.4 3.4 copy-start.4
  190.4 3.4 copy-start.9
  202.6 8.3 %copy-start.2 = (f32[2,768,2048]{2,1,0:T(8,128)S(1)}, f32[2,768,2048]{2,1,0:T(8,128)}, u32[]{:S(2)}) copy-start(f32[2,768,2048]{2,1,0:T(8,128)} %get-tuple-element.27) | copy-start | bytes 37748740
  202.6 8.5 %copy-start.7 = (bf16[2048,2,128]{2,0,1:T(8,128)(2,1)S(1)}, bf16[2048,2,128]{2,0,1:T(8,128)(2,1)}, u32[]{:S(2)}) copy-start(bf16[2048,2,128]{2,0,1:T(8,128)(2,1)} %copy.134) | copy-start | bytes 3145732
  215.6 4.8 %copy-start.18 = (pred[128,4]{0,1:T(4,128)(4,1)S(1)}, pred[128,4]{0,1:T(4,128)(4,1)}, u32[]{:S(2)}) copy-start(pred[128,4]{0,1:T(4,128)(4,1)} %copy-done.17) | copy-start | bytes 1540
  215.9 6.1 %copy-start.12 = (bf16[1536,32]{0,1:T(8,128)(2,1)S(1)}, bf16[1536,32]{0,1:T(8,128)(2,1)}, u32[]{:S(2)}) copy-start(bf16[1536,32]{0,1:T(8,128)(2,1)} %param.26) | copy-start | bytes 294916
  222.3 4.0 %copy-start.15 = (s32[128,4]{0,1:T(4,128)S(1)}, s32[128,4]{0,1:T(4,128)}, u32[]{:S(2)}) copy-start(s32[128,4]{0,1:T(4,128)} %multiply_add_fusion) | copy-start | bytes 6148
  227.0 55.9 %slice-start = ((s8[4718592]{0:T(1024)(128)(4,1)}), s8[4194304]{0:T(1024)(128)(4,1)S(1)}, s32[]{:S(2)}) async-start(s8[4718592]{0:T(1024)(128)(4,1)} %bitcast.164), calls=%async_computation.9 | async-start | bytes 8388608
  228.2 54.6 %slice-start.1 = ((s8[4718592]{0:T(1024)(128)(4,1)}), s8[524288]{0:T(1024)(128)(4,1)S(1)}, s32[]{:S(2)}) async-start(s8[4718592]{0:T(1024)(128)(4,1)} %bitcast.164), calls=%async_computation.10 | async-start | bytes 1048576
  280.9 1.9 copy-start.5
  354.7 2.2 copy-start.1
Sparse Core Ops, SparseCore 0:
  51.2 40.0 all-gather.2
  118.2 40.7 all-gather.4

commit v5 on v4

--- a/solution.py
+++ b/solution.py
@@ -102,7 +102,21 @@
     picked_shape = picked.shape
     lane = 128
     chunks = picked.reshape(columns, -1, lane)
-    received = lax.all_to_all(chunks, "col", 0, 0, tiled=True)
+    blocks = (projection_weight, output_weight)
+    flat_blocks = [block.reshape(-1, lane) for block in blocks]
+    sizes = [chunks.shape[1]] + [flat.shape[0] for flat in flat_blocks]
+    starts = [sum(sizes[:i]) for i in range(len(sizes) + 1)]
+    bundle = jnp.concatenate(
+        [chunks] + [jnp.broadcast_to(flat[None], (columns,) + flat.shape) for flat in flat_blocks],
+        axis=1,
+    )
+    bundle = lax.all_to_all(bundle, "col", 0, 0, tiled=True)
+    received = bundle[:, starts[0] : starts[1]]
+    slabs = []
+    for i, block in enumerate(blocks):
+        rows_here, cols_here = block.shape
+        piece = bundle[:, starts[i + 1] : starts[i + 2]].reshape(columns, rows_here, cols_here)
+        slabs.append(piece.transpose(1, 0, 2).reshape(rows_here, columns * cols_here))
     reduced = jnp.sum(received.astype(jnp.float32), axis=0).astype(jnp.bfloat16)
     spread = lax.all_to_all(
         jnp.broadcast_to(reduced[None], (columns,) + reduced.shape), "col", 0, 0, tiled=True
@@ -110,13 +124,7 @@
     core_index = col_index % 2
     partner = [(c, c ^ 1) for c in range(columns)]
 
-    def gather_halves(block):
-        rows_here, cols_here = block.shape
-        slab = lax.all_to_all(
-            jnp.broadcast_to(block[None], (columns, rows_here, cols_here)), "col", 0, 0, tiled=True
-        )
-        slab = slab.transpose(1, 0, 2).reshape(rows_here, columns * cols_here)
-        slab, _ = lax.optimization_barrier((slab, received))
+    def gather_halves(slab):
         half = slab.shape[1] // 2
         own = lax.dynamic_slice_in_dim(slab, core_index * half, half, axis=1)
         own = lax.all_gather(own, "row", axis=0, tiled=True)
@@ -137,8 +145,8 @@
             1,
         )
 
-    qkv_halves = gather_halves(projection_weight)
-    out_halves = gather_halves(output_weight)
+    qkv_halves = gather_halves(slabs[0])
+    out_halves = gather_halves(slabs[1])
     maps = spread.reshape(picked_shape)
     widths = [table.shape[-1] for table in tables]
     bounds = [sum(widths[:i]) for i in range(len(widths) + 1)]

time: 365 us -> 358 us (0.981)
  waiting for transfers between devices: 97.2 us -> 112 us
  starting transfers between devices: 32.4 us -> 22.7 us
  local copies, waits for them, and re-layouts: 46.7 us -> 38.3 us
  other arithmetic: 23.6 us -> 19.4 us
    all_to_all x1, waiting for transfers between devices: 2.47 us -> 18.3 us  [local(): lax.all_to_all(jnp.broadcast_to(key_value_piece[None], (columns,) + key_v...]
    all_to_all x3 -> x1, starting transfers between devices: 19.6 us -> 8.57 us  [local(): bundle = lax.all_to_all(bundle, 'col', 0, 0, tiled=True)]
    all_to_all x3 -> x1, waiting for transfers between devices: 33.2 us -> 29.7 us  [local(): bundle = lax.all_to_all(bundle, 'col', 0, 0, tiled=True)]
  transfers between devices with their start and end apart: 9 -> 7, of which waited for: 6 -> 4; matrix products, arithmetic and copies ran while one was open for 21% -> 17% of each run, Pallas kernels for 0% -> 0%
where the time goes in v5:
time: 358 us; the launch traced here: 357 us
  waiting for transfers between devices  112 us (31%)
  blocking collectives  103 us (29%)
  matrix products  47.8 us (13%)
  local copies, waits for them, and re-layouts  38.3 us (11%)
  starting transfers between devices  22.7 us (6%)
  other arithmetic  19.4 us (5%)
  between operations  14 us (4%)
    all_to_all x1, blocking collectives, local(): lax.all_to_all(sending, 'col', split_axis=0, concat_axis=0, tiled=True)  52 us
    all_to_all x1, blocking collectives, local(): lax.all_to_all(answered, 'col', split_axis=0, concat_axis=0, tiled=True)  51.5 us
    all_gather x2, waiting for transfers between devices, gather_halves(): own = lax.all_gather(own, 'row', axis=0, tiled=True)  40.7 us
    all_to_all x1, waiting for transfers between devices, local(): bundle = lax.all_to_all(bundle, 'col', 0, 0, tiled=True)  29.7 us
    all_to_all x1, waiting for transfers between devices, local(): lax.all_to_all(jnp.broadcast_to(reduced[None], (columns,) + reduced.shape...  22.8 us
    all_to_all x1, waiting for transfers between devices, local(): lax.all_to_all(jnp.broadcast_to(key_value_piece[None], (columns,) + key_v...  18.3 us
    dot_general x1, matrix products, local(): jnp.einsum('sjcf,jfd->sjcd', hidden_vals, expert_down_weight, preferred_e...  12.6 us
    dot_general x1, matrix products, local(): jnp.einsum('hqd,hkd->hqk', grouped, key_lines, preferred_element_type=jnp...  8.74 us
  transfers between devices with their start and end apart: 7, of which 4 were waited for; matrix products, arithmetic and copies ran while one was open for 17% of the time, Pallas kernels for 0%

profile of v5, /device:TPU:1, one launch (start us, length us, event | category | flops | bytes accessed | tf_op | source)
XLA Modules:
  0.0 357.3 jit_solution(6653918058650758425)
XLA Ops:
  6.5 0.9 dynamic-slice_reduce_fusion
  7.5 1.5 gather_fusion.2
  9.0 1.5 gather_fusion.3
  10.5 1.5 gather_fusion.4
  12.9 1.1 reshape.377
  14.4 1.5 pad_maximum_fusion
  16.0 8.6 %all-to-all-start = ((bf16[16,544,128]{2,1,0:T(8,128)(2,1)}), bf16[16,544,128]{2,1,0:T(8,128)(2,1)S(1)}, u32[]{:S(2)}, u32[]{:S(2)}) async-start(bf16[16,544,128]{2,1,0:T(8,128)(2,1)} %pad_maximum_fusion), calls=%async_computation | async-start | bytes 4456448 | tf_op jit(solution)/shard_map/all_to_all | solution.py:113
  24.6 29.7 %all-to-all-done = bf16[16,544,128]{2,1,0:T(8,128)(2,1)S(1)} async-done(((bf16[16,544,128]{2,1,0:T(8,128)(2,1)}), bf16[16,544,128]{2,1,0:T(8,128)(2,1)S(1)}, u32[]{:S(2)}, u32[]{:S(2)}) %all-to-all-start) | async-done | bytes 2228256 | tf_op jit(solution)/shard_map/all_to_all | solution.py:113
  54.4 0.8 constant_dynamic-slice_fusion.1
  55.2 40.7 %all-gather.3.cloned.1.call-done = bf16[1536,1024]{1,0:T(8,128)(2,1)} async-done(((bf16[192,1024]{1,0:T(8,128)(2,1)}), bf16[1536,1024]{1,0:T(8,128)(2,1)}) %all-gather.3.cloned.1.call-update) | async-done | bytes 3145744 | tf_op jit(solution)/shard_map/all_gather | solution.py:130
  96.0 3.0 collective-permute-start
  100.8 1.4 reshape.387
  102.2 2.6 copy.136
  104.7 2.0 reshape.388
  106.7 0.7 constant_dynamic-slice_fusion
  107.6 1.0 broadcast_in_dim.194
  108.6 6.5 %all-to-all-start.1 = ((bf16[16,208,128]{2,1,0:T(8,128)(2,1)}), bf16[16,208,128]{2,1,0:T(8,128)(2,1)S(1)}, u32[]{:S(2)}, u32[]{:S(2)}) async-start(bf16[16,208,128]{2,1,0:T(8,128)(2,1)} %broadcast_in_dim.194), calls=%async_computation.1 | async-start | bytes 1703936 | tf_op jit(solution)/shard_map/all_to_all | solution.py:121
  116.0 22.8 %all-to-all-done.1 = bf16[16,208,128]{2,1,0:T(8,128)(2,1)S(1)} async-done(((bf16[16,208,128]{2,1,0:T(8,128)(2,1)}), bf16[16,208,128]{2,1,0:T(8,128)(2,1)S(1)}, u32[]{:S(2)}, u32[]{:S(2)}) %all-to-all-start.1) | async-done | bytes 852000 | tf_op jit(solution)/shard_map/all_to_all | solution.py:121
  138.8 1.8 reshape.379
  140.7 2.5 convolution_dynamic-update-slice_fusion.1
  143.3 2.6 convolution_dynamic-update-slice_fusion
  145.9 1.9 fusion.25
  148.6 1.8 broadcast_in_dim.199
  150.3 4.3 %all-to-all-start.2 = ((bf16[16,128,512]{1,2,0:T(8,128)(2,1)}), bf16[16,128,512]{1,2,0:T(8,128)(2,1)S(1)}, u32[]{:S(2)}, u32[]{:S(2)}) async-start(bf16[16,128,512]{1,2,0:T(8,128)(2,1)} %broadcast_in_dim.199), calls=%async_computation.2 | async-start | bytes 4194304 | tf_op jit(solution)/shard_map/all_to_all | solution.py:181
  155.0 2.3 reduce-window.11
  158.0 3.2 fusion.4
  161.4 1.2 copy.127
  162.5 1.2 subtract_convert_fusion.1
  163.8 0.9 copy.128
  164.7 18.3 %all-to-all-done.2 = bf16[16,128,512]{1,2,0:T(8,128)(2,1)S(1)} async-done(((bf16[16,128,512]{1,2,0:T(8,128)(2,1)}), bf16[16,128,512]{1,2,0:T(8,128)(2,1)S(1)}, u32[]{:S(2)}, u32[]{:S(2)}) %all-to-all-start.2) | async-done | bytes 2097184 | tf_op jit(solution)/shard_map/all_to_all | solution.py:181
  183.4 1.1 fusion.92
  184.5 2.3 copy.133
  186.8 8.7 %select_reduce_fusion = (f32[2,768]{1,0:T(2,128)S(1)}, f32[2,768,2048]{2,1,0:T(8,128)}) fusion(pred[768,2048]{1,0:T(8,128)(4,1)S(1)} %copy-done.4, bf16[2,768,128]{2,1,0:T(8,128)(2,1)} %bitcast.157, bf16[2048,2,128]{2,0,1:T(8,128)(2,1)} %copy.133), kind=kOutput, calls=%fused_computation.6 | convolution fusion | flops 814742016 | bytes 15603712 | tf_op jit(solution)/shard_map/hqd,hkd->hqk/dot_general | solution.py:198
  195.5 1.3 copy.134
  196.9 7.9 %fusion = f32[2,768]{1,0:T(2,128)S(1)} fusion(f32[2,768,2048]{2,1,0:T(8,128)} %get-tuple-element.23, f32[2,768]{1,0:T(2,128)S(1)} %broadcast_maximum_fusion, pred[768,2048]{1,0:T(8,128)(4,1)S(1)} %copy-done.4), kind=kLoop, calls=%fused_computation.7 | loop fusion | flops 12581376 | bytes 14168064 | tf_op jit(solution)/shard_map/reduce_sum | solution.py:204
  205.4 4.4 %fusion.50 = bf16[2,768,128]{2,1,0:T(8,128)(2,1)S(1)} fusion(bf16[2048,2,128]{2,0,1:T(8,128)(2,1)S(1)} %copy-done.7, f32[2,768,2048]{2,1,0:T(8,128)S(1)} %copy-done.2, f32[2,768]{1,0:T(2,128)S(1)} %broadcast_maximum_fusion, pred[768,2048]{1,0:T(8,128)(4,1)S(1)} %copy-done.4, f32[2,768]{1,0:T(2,128)S(1)} %fusion), kind=kOutput, calls=%fused_computation.58 | convolution fusion | flops 818282496 | bytes 15609856 | tf_op jit(solution)/shard_map/hqk,hkd->hqd/dot_general | solution.py:205
  210.2 2.2 convolution_dynamic-update-slice_fusion.3
  212.4 2.2 convolution_dynamic-update-slice_fusion.2
  214.6 1.6 multiply_reduce_fusion
  216.5 3.8 %gather_fusion.1 = f32[512]{0:T(512)S(1)} fusion(f32[128,32]{0,1:T(8,128)S(1)} %fusion.87, s32[512]{0:T(512)S(1)} %reshape.425), kind=kCustom, calls=%fused_computation.4 | custom fusion | bytes 8192 | tf_op jit(solution)/shard_map/jit(take_along_axis)/gather | solution.py:225
  221.2 1.3 convolution_convert_fusion
  222.4 52.0 %all_to_all.25 = bf16[16,2,40,1536]{3,2,1,0:T(8,128)(2,1)S(1)} all-to-all(bf16[16,2,40,1536]{3,2,1,0:T(8,128)(2,1)S(1)} %bitcast.147), channel_id=1, replica_groups=mesh['row'=8,'col'=16] {'col'}, dimensions={0} | all-to-all | bytes 7864320 | tf_op jit(solution)/shard_map/all_to_all | solution.py:239
  274.4 1.9 copy-done.6
  276.3 5.2 %fusion.8 = f32[2,16,40,768]{3,2,1,0:T(8,128)} fusion(bf16[2,1536,768]{2,1,0:T(8,128)(2,1)S(1)} %bitcast.165, bf16[16,2,40,1536]{3,2,1,0:T(8,128)(2,1)S(1)} %all_to_all.25), kind=kOutput, calls=%fused_computation.16 | convolution fusion | flops 3019898880 | bytes 12582912 | tf_op jit(solution)/shard_map/sjcd,jdf->sjcf/dot_general | solution.py:243
  281.5 12.6 %fusion.15 = bf16[16,2,40,1536]{3,2,0,1:T(8,128)(2,1)} fusion(bf16[2,768,1536]{2,1,0:T(8,128)(2,1)} %param.33, f32[2,16,40,768]{3,2,1,0:T(8,128)} %fusion.8, bf16[2,1536,768]{2,1,0:T(8,128)(2,1)} %param.31, bf16[16,2,40,1536]{3,2,1,0:T(8,128)(2,1)} %copy-done.6), kind=kOutput, calls=%fused_computation.22 | convolution fusion | flops 6044712960 | bytes 21233664 | tf_op jit(solution)/shard_map/sjcf,jfd->sjcd/dot_general | solution.py:247
  294.1 2.6 copy.146
  296.7 51.5 %all_to_all.26 = bf16[16,2,40,1536]{3,2,1,0:T(8,128)(2,1)S(1)} all-to-all(bf16[16,2,40,1536]{3,2,1,0:T(8,128)(2,1)S(1)} %copy.146), channel_id=1, replica_groups=mesh['row'=8,'col'=16] {'col'}, dimensions={0} | all-to-all | bytes 7864320 | tf_op jit(solution)/shard_map/all_to_all | solution.py:250
  348.9 1.6 fusion.28
  (115 shorter events, 9.3 us)
Async XLA Ops:
  6.5 5.5 %copy-start = (bf16[4,16,2048]{2,1,0:T(8,128)(2,1)S(1)}, bf16[4,16,2048]{2,1,0:T(8,128)(2,1)}, u32[]{:S(2)}) copy-start(bf16[4,16,2048]{2,1,0:T(8,128)(2,1)} %param.28) | copy-start | bytes 786436
  6.5 7.5 %copy-start.13 = (bf16[192,96]{1,0:T(8,128)(2,1)S(1)}, bf16[192,96]{1,0:T(8,128)(2,1)}, u32[]{:S(2)}) copy-start(bf16[192,96]{1,0:T(8,128)(2,1)} %param.25) | copy-start | bytes 110596
  6.5 7.6 %copy-start.12 = (bf16[192,128]{1,0:T(8,128)(2,1)S(1)}, bf16[192,128]{1,0:T(8,128)(2,1)}, u32[]{:S(2)}) copy-start(bf16[192,128]{1,0:T(8,128)(2,1)} %param.24) | copy-start | bytes 147460
  16.0 83.0 %copy-start.14 = (bf16[1536]{0:T(1024)(128)(2,1)S(1)}, bf16[1536]{0:T(1024)(128)(2,1)}, u32[]{:S(2)}) copy-start(bf16[1536]{0:T(1024)(128)(2,1)} %param.22) | copy-start | bytes 9220
  16.0 84.6 %copy-start.11 = (s32[128,4]{0,1:T(4,128)S(1)}, s32[128,4]{0,1:T(4,128)}, u32[]{:S(2)}) copy-start(s32[128,4]{0,1:T(4,128)} %param.21) | copy-start | bytes 6148
  16.0 38.3 %all-to-all-start = ((bf16[16,544,128]{2,1,0:T(8,128)(2,1)}), bf16[16,544,128]{2,1,0:T(8,128)(2,1)S(1)}, u32[]{:S(2)}, u32[]{:S(2)}) async-start(bf16[16,544,128]{2,1,0:T(8,128)(2,1)} %pad_maximum_fusion), calls=%async_computation | async-start | bytes 4456448 | tf_op jit(solution)/shard_map/all_to_all | solution.py:113
  24.5 71.4 %all-gather.3.cloned.1.call-start = ((), (), s32[]{:S(2)}) async-start(), calls=%async_computation.5 | async-start | bytes 3538944 | tf_op jit(solution)/shard_map/all_gather | solution.py:130
  55.2 106.0 %all-gather.5.cloned.1.call-start = ((), (), s32[]{:S(2)}) async-start(), calls=%async_computation.6 | async-start | bytes 2654208 | tf_op jit(solution)/shard_map/all_gather | solution.py:130
  96.0 47.3 %collective-permute-start = (bf16[1536,1024]{1,0:T(8,128)(2,1)}, bf16[1536,1024]{1,0:T(8,128)(2,1)}, u32[]{:S(2)}, u32[]{:S(2)}) collective-permute-start(bf16[1536,1024]{1,0:T(8,128)(2,1)} %all-gather.3.cloned.1.call-done), channel_id=1, source_target_pairs={{0,1},{1,0},{2,3},{3,2},{4,5},{5,4},{6,7},{7,6},{8,9},{9,8},{10,11... | collective-permute-start | bytes 9437192 | tf_op jit(solution)/shard_map/ppermute | solution.py:131
  99.7 8.9 %copy-start.8 = (f32[128,64]{0,1:T(8,128)}, f32[128,64]{0,1:T(8,128)S(1)}, u32[]{:S(2)}) copy-start(f32[128,64]{0,1:T(8,128)S(1)} %get-tuple-element.17) | copy-start | bytes 98308
  102.2 13.0 %copy-start.3 = (bf16[128,1536]{1,0:T(8,128)(2,1)S(1)}, bf16[128,1536]{1,0:T(8,128)(2,1)}, u32[]{:S(2)}) copy-start(bf16[128,1536]{1,0:T(8,128)(2,1)} %param.18) | copy-start | bytes 1179652
  108.6 30.2 %all-to-all-start.1 = ((bf16[16,208,128]{2,1,0:T(8,128)(2,1)}), bf16[16,208,128]{2,1,0:T(8,128)(2,1)S(1)}, u32[]{:S(2)}, u32[]{:S(2)}) async-start(bf16[16,208,128]{2,1,0:T(8,128)(2,1)} %broadcast_in_dim.194), calls=%async_computation.1 | async-start | bytes 1703936 | tf_op jit(solution)/shard_map/all_to_all | solution.py:121
  143.3 4.6 %copy-start.9 = (f32[128,64]{1,0:T(8,128)S(1)}, f32[128,64]{1,0:T(8,128)}, u32[]{:S(2)}) copy-start(f32[128,64]{1,0:T(8,128)} %copy.130) | copy-start | bytes 98308
  147.8 2.6 copy-start.5
  147.9 6.8 %copy-start.15 = (bf16[1536]{0:T(1024)(128)(2,1)S(1)}, bf16[1536]{0:T(1024)(128)(2,1)}, u32[]{:S(2)}) copy-start(bf16[1536]{0:T(1024)(128)(2,1)} %param.23) | copy-start | bytes 9220
  150.3 32.7 %all-to-all-start.2 = ((bf16[16,128,512]{1,2,0:T(8,128)(2,1)}), bf16[16,128,512]{1,2,0:T(8,128)(2,1)S(1)}, u32[]{:S(2)}, u32[]{:S(2)}) async-start(bf16[16,128,512]{1,2,0:T(8,128)(2,1)} %broadcast_in_dim.199), calls=%async_computation.2 | async-start | bytes 4194304 | tf_op jit(solution)/shard_map/all_to_all | solution.py:181
  154.6 6.8 %slice-start = ((f32[128,2048]{1,0:T(8,128)}), f32[128,1536]{1,0:T(8,128)S(1)}, s32[]{:S(2)}) async-start(f32[128,2048]{1,0:T(8,128)} %copy-done.5), calls=%async_computation.7 | async-start | bytes 1572864 | tf_op jit(solution)/shard_map/slice | solution.py:162
  161.1 51.2 %collective-permute-start.1 = (bf16[1536,768]{1,0:T(8,128)(2,1)}, bf16[1536,768]{1,0:T(8,128)(2,1)}, u32[]{:S(2)}, u32[]{:S(2)}) collective-permute-start(bf16[1536,768]{1,0:T(8,128)(2,1)} %all-gather.5.cloned.1.call-done), channel_id=1, source_target_pairs={{0,1},{1,0},{2,3},{3,2},{4,5},{5,4},{6,7},{7,6},{8,9},{9,8},{10,11... | collective-permute-start | bytes 7077896 | tf_op jit(solution)/shard_map/ppermute | solution.py:131
  183.4 3.4 copy-start.4
  196.9 8.3 %copy-start.2 = (f32[2,768,2048]{2,1,0:T(8,128)S(1)}, f32[2,768,2048]{2,1,0:T(8,128)}, u32[]{:S(2)}) copy-start(f32[2,768,2048]{2,1,0:T(8,128)} %get-tuple-element.23) | copy-start | bytes 37748740
  196.9 8.5 %copy-start.7 = (bf16[2048,2,128]{2,0,1:T(8,128)(2,1)S(1)}, bf16[2048,2,128]{2,0,1:T(8,128)(2,1)}, u32[]{:S(2)}) copy-start(bf16[2048,2,128]{2,0,1:T(8,128)(2,1)} %copy.134) | copy-start | bytes 3145732
  210.2 6.1 %copy-start.10 = (bf16[1536,32]{0,1:T(8,128)(2,1)S(1)}, bf16[1536,32]{0,1:T(8,128)(2,1)}, u32[]{:S(2)}) copy-start(bf16[1536,32]{0,1:T(8,128)(2,1)} %param.26) | copy-start | bytes 294916
  221.2 55.2 %slice-start.1 = ((s8[4718592]{0:T(1024)(128)(4,1)}), s8[4194304]{0:T(1024)(128)(4,1)S(1)}, s32[]{:S(2)}) async-start(s8[4718592]{0:T(1024)(128)(4,1)} %bitcast.164), calls=%async_computation.8 | async-start | bytes 8388608
  222.4 53.9 %slice-start.2 = ((s8[4718592]{0:T(1024)(128)(4,1)}), s8[524288]{0:T(1024)(128)(4,1)S(1)}, s32[]{:S(2)}) async-start(s8[4718592]{0:T(1024)(128)(4,1)} %bitcast.164), calls=%async_computation.9 | async-start | bytes 1048576
  274.4 1.9 copy-start.6
  348.2 2.3 copy-start.1
Sparse Core Ops, SparseCore 0:
  55.3 40.6 all-gather.2
  107.6 42.7 all-gather.4

commit v6 on v5

--- a/solution.py
+++ b/solution.py
@@ -106,21 +106,20 @@
     flat_blocks = [block.reshape(-1, lane) for block in blocks]
     sizes = [chunks.shape[1]] + [flat.shape[0] for flat in flat_blocks]
     starts = [sum(sizes[:i]) for i in range(len(sizes) + 1)]
+    received = lax.all_to_all(chunks, "col", 0, 0, tiled=True)
+    reduced = jnp.sum(received.astype(jnp.float32), axis=0).astype(jnp.bfloat16)
     bundle = jnp.concatenate(
-        [chunks] + [jnp.broadcast_to(flat[None], (columns,) + flat.shape) for flat in flat_blocks],
+        [jnp.broadcast_to(reduced[None], (columns,) + reduced.shape)]
+        + [jnp.broadcast_to(flat[None], (columns,) + flat.shape) for flat in flat_blocks],
         axis=1,
     )
     bundle = lax.all_to_all(bundle, "col", 0, 0, tiled=True)
-    received = bundle[:, starts[0] : starts[1]]
+    spread = bundle[:, starts[0] : starts[1]]
     slabs = []
     for i, block in enumerate(blocks):
         rows_here, cols_here = block.shape
         piece = bundle[:, starts[i + 1] : starts[i + 2]].reshape(columns, rows_here, cols_here)
         slabs.append(piece.transpose(1, 0, 2).reshape(rows_here, columns * cols_here))
-    reduced = jnp.sum(received.astype(jnp.float32), axis=0).astype(jnp.bfloat16)
-    spread = lax.all_to_all(
-        jnp.broadcast_to(reduced[None], (columns,) + reduced.shape), "col", 0, 0, tiled=True
-    )
     core_index = col_index % 2
     partner = [(c, c ^ 1) for c in range(columns)]
 

time: 358 us -> 362 us (1.011)
  waiting for transfers between devices: 112 us -> 97.3 us
  local copies, waits for them, and re-layouts: 38.3 us -> 48 us
  other arithmetic: 19.4 us -> 25.7 us
    all_to_all x1, waiting for transfers between devices: 18.3 us -> 7.01 us  [local(): lax.all_to_all(jnp.broadcast_to(key_value_piece[None], (columns,) + key_v...]
    all_to_all x1, waiting for transfers between devices: 22.8 us -> 14.5 us  [local(): received = lax.all_to_all(chunks, 'col', 0, 0, tiled=True)]
    all_gather x2, waiting for transfers between devices: 40.7 us -> 45.9 us  [gather_halves(): own = lax.all_gather(own, 'row', axis=0, tiled=True)]
    all_to_all x1, starting transfers between devices: 8.57 us -> 4.91 us  [local(): bundle = lax.all_to_all(bundle, 'col', 0, 0, tiled=True)]
  transfers between devices with their start and end apart: 7 -> 7, of which waited for: 4 -> 5; matrix products, arithmetic and copies ran while one was open for 17% -> 20% of each run, Pallas kernels for 0% -> 0%
where the time goes in v6:
time: 362 us; the launch traced here: 360 us
  blocking collectives  103 us (28%)
  waiting for transfers between devices  97.3 us (27%)
  local copies, waits for them, and re-layouts  48 us (13%)
  matrix products  46.3 us (13%)
  starting transfers between devices  26.1 us (7%)
  other arithmetic  25.7 us (7%)
  between operations  14.1 us (4%)
    all_to_all x1, blocking collectives, local(): lax.all_to_all(answered, 'col', split_axis=0, concat_axis=0, tiled=True)  51.5 us
    all_to_all x1, blocking collectives, local(): lax.all_to_all(sending, 'col', split_axis=0, concat_axis=0, tiled=True)  51.4 us
    all_gather x2, waiting for transfers between devices, gather_halves(): own = lax.all_gather(own, 'row', axis=0, tiled=True)  45.9 us
    all_to_all x1, waiting for transfers between devices, local(): bundle = lax.all_to_all(bundle, 'col', 0, 0, tiled=True)  29.8 us
    all_to_all x1, waiting for transfers between devices, local(): received = lax.all_to_all(chunks, 'col', 0, 0, tiled=True)  14.5 us
    dot_general x1, matrix products, local(): jnp.einsum('sjcf,jfd->sjcd', hidden_vals, expert_down_weight, preferred_e...  12.6 us
    all_to_all x1, starting transfers between devices, local(): received = lax.all_to_all(chunks, 'col', 0, 0, tiled=True)  8.44 us
    reduce_sum x1, other arithmetic, local(): running_new = jnp.sum(weights, axis=-1)  7.89 us
  transfers between devices with their start and end apart: 7, of which 5 were waited for; matrix products, arithmetic and copies ran while one was open for 20% of the time, Pallas kernels for 0%

profile of v6, /device:TPU:1, one launch (start us, length us, event | category | flops | bytes accessed | tf_op | source)
XLA Modules:
  0.0 360.4 jit_solution(6945402585934366756)
XLA Ops:
  7.5 1.5 gather_fusion.2
  9.0 1.5 gather_fusion.3
  10.5 1.5 gather_fusion.4
  12.9 2.0 reshape.377
  15.0 8.4 %all-to-all-start = ((bf16[16,208,128]{2,1,0:T(8,128)(2,1)}), bf16[16,208,128]{2,1,0:T(8,128)(2,1)S(1)}, u32[]{:S(2)}, u32[]{:S(2)}) async-start(bf16[16,208,128]{2,1,0:T(8,128)(2,1)} %reshape.377), calls=%async_computation | async-start | bytes 1703936 | tf_op jit(solution)/shard_map/all_to_all | solution.py:109
  23.5 14.5 %all-to-all-done = bf16[16,208,128]{2,1,0:T(8,128)(2,1)S(1)} async-done(((bf16[16,208,128]{2,1,0:T(8,128)(2,1)}), bf16[16,208,128]{2,1,0:T(8,128)(2,1)S(1)}, u32[]{:S(2)}, u32[]{:S(2)}) %all-to-all-start) | async-done | bytes 852000 | tf_op jit(solution)/shard_map/all_to_all | solution.py:109
  38.6 1.5 pad_maximum_fusion
  40.1 4.9 %all-to-all-start.1 = ((bf16[16,544,128]{2,1,0:T(8,128)(2,1)}), bf16[16,544,128]{2,1,0:T(8,128)(2,1)S(1)}, u32[]{:S(2)}, u32[]{:S(2)}) async-start(bf16[16,544,128]{2,1,0:T(8,128)(2,1)} %pad_maximum_fusion), calls=%async_computation.1 | async-start | bytes 4456448 | tf_op jit(solution)/shard_map/all_to_all | solution.py:116
  45.1 29.8 %all-to-all-done.1 = bf16[16,544,128]{2,1,0:T(8,128)(2,1)S(1)} async-done(((bf16[16,544,128]{2,1,0:T(8,128)(2,1)}), bf16[16,544,128]{2,1,0:T(8,128)(2,1)S(1)}, u32[]{:S(2)}, u32[]{:S(2)}) %all-to-all-start.1) | async-done | bytes 2228256 | tf_op jit(solution)/shard_map/all_to_all | solution.py:116
  75.8 40.7 %all-gather.3.cloned.1.call-done = bf16[1536,1024]{1,0:T(8,128)(2,1)} async-done(((bf16[192,1024]{1,0:T(8,128)(2,1)}), bf16[1536,1024]{1,0:T(8,128)(2,1)}) %all-gather.3.cloned.1.call-update) | async-done | bytes 3145744 | tf_op jit(solution)/shard_map/all_gather | solution.py:129
  116.5 3.0 collective-permute-start
  121.4 1.7 reshape.387
  123.1 1.4 copy.136
  124.5 2.0 reshape.388
  131.7 2.7 convolution_dynamic-update-slice_fusion.1
  134.4 2.6 convolution_dynamic-update-slice_fusion
  137.1 1.5 fusion.25
  139.4 1.7 broadcast_in_dim.199
  141.1 6.5 %all-to-all-start.2 = ((bf16[16,128,512]{1,2,0:T(8,128)(2,1)}), bf16[16,128,512]{1,2,0:T(8,128)(2,1)S(1)}, u32[]{:S(2)}, u32[]{:S(2)}) async-start(bf16[16,128,512]{1,2,0:T(8,128)(2,1)} %broadcast_in_dim.199), calls=%async_computation.2 | async-start | bytes 4194304 | tf_op jit(solution)/shard_map/all_to_all | solution.py:180
  147.7 1.5 eq.97
  151.6 3.2 reduce-window.11
  154.8 1.7 slice_reduce_fusion
  156.5 1.3 reduce-window.14
  158.4 1.5 fusion.72
  160.0 1.4 reduce_sum.111
  161.4 1.5 copy.141
  166.1 3.1 fusion.4
  169.2 5.2 %all-gather.5.cloned.1.call-done = bf16[1536,768]{1,0:T(8,128)(2,1)} async-done(((bf16[192,768]{1,0:T(8,128)(2,1)}), bf16[1536,768]{1,0:T(8,128)(2,1)}) %all-gather.5.cloned.1.call-update) | async-done | bytes 2359312 | tf_op jit(solution)/shard_map/all_gather | solution.py:129
  174.4 3.1 collective-permute-start.1
  178.5 1.4 copy.127
  181.1 7.0 %all-to-all-done.2 = bf16[16,128,512]{1,2,0:T(8,128)(2,1)S(1)} async-done(((bf16[16,128,512]{1,2,0:T(8,128)(2,1)}), bf16[16,128,512]{1,2,0:T(8,128)(2,1)S(1)}, u32[]{:S(2)}, u32[]{:S(2)}) %all-to-all-start.2) | async-done | bytes 2097184 | tf_op jit(solution)/shard_map/all_to_all | solution.py:180
  189.5 2.3 copy.133
  191.8 7.5 %select_reduce_fusion = (f32[2,768]{1,0:T(2,128)S(1)}, f32[2,768,2048]{2,1,0:T(8,128)}) fusion(pred[768,2048]{1,0:T(8,128)(4,1)S(1)} %copy-done.4, bf16[2,768,128]{2,1,0:T(8,128)(2,1)S(1)} %bitcast.157, bf16[2048,2,128]{2,0,1:T(8,128)(2,1)} %copy.133), kind=kOutput, calls=%fused_computation.6 | convolution fusion | flops 814742016 | bytes 15603712 | tf_op jit(solution)/shard_map/hqd,hkd->hqk/dot_general | solution.py:197
  199.2 1.3 copy.134
  200.6 7.9 %fusion = f32[2,768]{1,0:T(2,128)S(1)} fusion(f32[2,768,2048]{2,1,0:T(8,128)} %get-tuple-element.23, f32[2,768]{1,0:T(2,128)S(1)} %broadcast_maximum_fusion, pred[768,2048]{1,0:T(8,128)(4,1)S(1)} %copy-done.4), kind=kLoop, calls=%fused_computation.7 | loop fusion | flops 12581376 | bytes 14168064 | tf_op jit(solution)/shard_map/reduce_sum | solution.py:203
  209.1 4.5 %fusion.50 = bf16[2,768,128]{2,1,0:T(8,128)(2,1)S(1)} fusion(bf16[2048,2,128]{2,0,1:T(8,128)(2,1)S(1)} %copy-done.7, f32[2,768,2048]{2,1,0:T(8,128)S(1)} %copy-done.2, f32[2,768]{1,0:T(2,128)S(1)} %broadcast_maximum_fusion, pred[768,2048]{1,0:T(8,128)(4,1)S(1)} %copy-done.4, f32[2,768]{1,0:T(2,128)S(1)} %fusion), kind=kOutput, calls=%fused_computation.58 | convolution fusion | flops 818282496 | bytes 15609856 | tf_op jit(solution)/shard_map/hqk,hkd->hqd/dot_general | solution.py:204
  213.9 2.2 convolution_dynamic-update-slice_fusion.3
  216.1 2.2 convolution_dynamic-update-slice_fusion.2
  218.3 1.6 multiply_reduce_fusion
  220.3 3.8 %gather_fusion.1 = f32[512]{0:T(512)S(1)} fusion(f32[128,32]{0,1:T(8,128)S(1)} %fusion.87, s32[512]{0:T(512)S(1)} %reshape.425), kind=kCustom, calls=%fused_computation.4 | custom fusion | bytes 8192 | tf_op jit(solution)/shard_map/jit(take_along_axis)/gather | solution.py:224
  224.9 1.3 convolution_convert_fusion
  226.2 51.4 %all_to_all.25 = bf16[16,2,40,1536]{3,2,1,0:T(8,128)(2,1)S(1)} all-to-all(bf16[16,2,40,1536]{3,2,1,0:T(8,128)(2,1)S(1)} %bitcast.147), channel_id=1, replica_groups=mesh['row'=8,'col'=16] {'col'}, dimensions={0} | all-to-all | bytes 7864320 | tf_op jit(solution)/shard_map/all_to_all | solution.py:238
  277.6 1.9 copy-done.5
  279.5 5.2 %fusion.8 = f32[2,16,40,768]{3,2,1,0:T(8,128)} fusion(bf16[2,1536,768]{2,1,0:T(8,128)(2,1)S(1)} %bitcast.165, bf16[16,2,40,1536]{3,2,1,0:T(8,128)(2,1)S(1)} %all_to_all.25), kind=kOutput, calls=%fused_computation.16 | convolution fusion | flops 3019898880 | bytes 12582912 | tf_op jit(solution)/shard_map/sjcd,jdf->sjcf/dot_general | solution.py:242
  284.7 12.6 %fusion.15 = bf16[16,2,40,1536]{3,2,0,1:T(8,128)(2,1)} fusion(bf16[2,768,1536]{2,1,0:T(8,128)(2,1)} %param.33, f32[2,16,40,768]{3,2,1,0:T(8,128)} %fusion.8, bf16[2,1536,768]{2,1,0:T(8,128)(2,1)} %param.31, bf16[16,2,40,1536]{3,2,1,0:T(8,128)(2,1)} %copy-done.5), kind=kOutput, calls=%fused_computation.22 | convolution fusion | flops 6044712960 | bytes 21233664 | tf_op jit(solution)/shard_map/sjcf,jfd->sjcd/dot_general | solution.py:246
  297.3 2.6 copy.146
  299.9 51.5 %all_to_all.26 = bf16[16,2,40,1536]{3,2,1,0:T(8,128)(2,1)S(1)} all-to-all(bf16[16,2,40,1536]{3,2,1,0:T(8,128)(2,1)S(1)} %copy.146), channel_id=1, replica_groups=mesh['row'=8,'col'=16] {'col'}, dimensions={0} | all-to-all | bytes 7864320 | tf_op jit(solution)/shard_map/all_to_all | solution.py:249
  352.0 1.5 fusion.28
  (133 shorter events, 23.7 us)
Async XLA Ops:
  6.5 5.5 %copy-start = (bf16[4,16,2048]{2,1,0:T(8,128)(2,1)S(1)}, bf16[4,16,2048]{2,1,0:T(8,128)(2,1)}, u32[]{:S(2)}) copy-start(bf16[4,16,2048]{2,1,0:T(8,128)(2,1)} %param.28) | copy-start | bytes 786436
  10.5 12.9 %copy-start.16 = (bf16[192,96]{1,0:T(8,128)(2,1)S(1)}, bf16[192,96]{1,0:T(8,128)(2,1)}, u32[]{:S(2)}) copy-start(bf16[192,96]{1,0:T(8,128)(2,1)} %param.25) | copy-start | bytes 110596
  12.7 25.6 %copy-start.15 = (bf16[192,128]{1,0:T(8,128)(2,1)S(1)}, bf16[192,128]{1,0:T(8,128)(2,1)}, u32[]{:S(2)}) copy-start(bf16[192,128]{1,0:T(8,128)(2,1)} %param.24) | copy-start | bytes 147460
  15.0 23.1 %all-to-all-start = ((bf16[16,208,128]{2,1,0:T(8,128)(2,1)}), bf16[16,208,128]{2,1,0:T(8,128)(2,1)S(1)}, u32[]{:S(2)}, u32[]{:S(2)}) async-start(bf16[16,208,128]{2,1,0:T(8,128)(2,1)} %reshape.377), calls=%async_computation | async-start | bytes 1703936 | tf_op jit(solution)/shard_map/all_to_all | solution.py:109
  40.1 79.5 %copy-start.19 = (bf16[1536]{0:T(1024)(128)(2,1)S(1)}, bf16[1536]{0:T(1024)(128)(2,1)}, u32[]{:S(2)}) copy-start(bf16[1536]{0:T(1024)(128)(2,1)} %param.22) | copy-start | bytes 9220
  40.1 34.7 %all-to-all-start.1 = ((bf16[16,544,128]{2,1,0:T(8,128)(2,1)}), bf16[16,544,128]{2,1,0:T(8,128)(2,1)S(1)}, u32[]{:S(2)}, u32[]{:S(2)}) async-start(bf16[16,544,128]{2,1,0:T(8,128)(2,1)} %pad_maximum_fusion), calls=%async_computation.1 | async-start | bytes 4456448 | tf_op jit(solution)/shard_map/all_to_all | solution.py:116
  45.0 71.5 %all-gather.3.cloned.1.call-start = ((), (), s32[]{:S(2)}) async-start(), calls=%async_computation.5 | async-start | bytes 3538944 | tf_op jit(solution)/shard_map/all_gather | solution.py:129
  74.9 54.0 %copy-start.14 = (s32[128,4]{0,1:T(4,128)S(1)}, s32[128,4]{0,1:T(4,128)}, u32[]{:S(2)}) copy-start(s32[128,4]{0,1:T(4,128)} %param.21) | copy-start | bytes 6148
  74.9 54.2 %copy-start.3 = (bf16[128,1536]{1,0:T(8,128)(2,1)S(1)}, bf16[128,1536]{1,0:T(8,128)(2,1)}, u32[]{:S(2)}) copy-start(bf16[128,1536]{1,0:T(8,128)(2,1)} %param.18) | copy-start | bytes 1179652
  75.8 98.6 %all-gather.5.cloned.1.call-start = ((), (), s32[]{:S(2)}) async-start(), calls=%async_computation.6 | async-start | bytes 2654208 | tf_op jit(solution)/shard_map/all_gather | solution.py:129
  116.5 17.9 %collective-permute-start = (bf16[1536,1024]{1,0:T(8,128)(2,1)}, bf16[1536,1024]{1,0:T(8,128)(2,1)}, u32[]{:S(2)}, u32[]{:S(2)}) collective-permute-start(bf16[1536,1024]{1,0:T(8,128)(2,1)} %all-gather.3.cloned.1.call-done), channel_id=1, source_target_pairs={{0,1},{1,0},{2,3},{3,2},{4,5},{5,4},{6,7},{7,6},{8,9},{9,8},{10,11... | collective-permute-start | bytes 9437192 | tf_op jit(solution)/shard_map/ppermute | solution.py:130
  119.9 0.6 copy-start.22
  119.9 10.0 %copy-start.23 = (s32[128]{0:T(128)}, s32[128]{0:T(128)S(1)}, u32[]{:S(2)}) copy-start(s32[128]{0:T(128)S(1)} %iota_add_fusion) | copy-start | bytes 1540
  120.0 9.9 %copy-start.24 = (s32[128]{0:T(128)}, s32[128]{0:T(128)S(1)}, u32[]{:S(2)}) copy-start(s32[128]{0:T(128)S(1)} %convert_reduce_fusion.2) | copy-start | bytes 1540
  127.4 0.7 copy-start.9
  127.4 0.7 copy-start.10
  129.0 0.9 copy-start.8
  129.9 4.5 %copy-start.18 = (f32[128]{0:T(128)}, f32[128]{0:T(128)S(1)}, u32[]{:S(2)}) copy-start(f32[128]{0:T(128)S(1)} %add_rsqrt_fusion.1) | copy-start | bytes 1540
  131.6 5.5 %copy-start.6 = (bf16[4,16,6656]{2,1,0:T(8,128)(2,1)}, bf16[4,16,6656]{2,1,0:T(8,128)(2,1)S(1)}, u32[]{:S(2)}) copy-start(bf16[4,16,6656]{2,1,0:T(8,128)(2,1)S(1)} %reshape.379) | copy-start | bytes 2555908
  131.7 5.4 %copy-start.20 = (pred[128,4]{0,1:T(4,128)(4,1)S(1)}, pred[128,4]{0,1:T(4,128)(4,1)}, u32[]{:S(2)}) copy-start(pred[128,4]{0,1:T(4,128)(4,1)} %iota_compare_fusion.5) | copy-start | bytes 1540
  134.4 4.3 %copy-start.11 = (f32[128,64]{1,0:T(8,128)S(1)}, f32[128,64]{1,0:T(8,128)}, u32[]{:S(2)}) copy-start(f32[128,64]{1,0:T(8,128)} %copy.129) | copy-start | bytes 98308
  134.4 4.3 %copy-start.12 = (f32[128,64]{1,0:T(8,128)S(1)}, f32[128,64]{1,0:T(8,128)}, u32[]{:S(2)}) copy-start(f32[128,64]{1,0:T(8,128)} %copy.130) | copy-start | bytes 98308
  141.1 47.0 %all-to-all-start.2 = ((bf16[16,128,512]{1,2,0:T(8,128)(2,1)}), bf16[16,128,512]{1,2,0:T(8,128)(2,1)S(1)}, u32[]{:S(2)}, u32[]{:S(2)}) async-start(bf16[16,128,512]{1,2,0:T(8,128)(2,1)} %broadcast_in_dim.199), calls=%async_computation.2 | async-start | bytes 4194304 | tf_op jit(solution)/shard_map/all_to_all | solution.py:180
  174.4 41.7 %collective-permute-start.1 = (bf16[1536,768]{1,0:T(8,128)(2,1)}, bf16[1536,768]{1,0:T(8,128)(2,1)}, u32[]{:S(2)}, u32[]{:S(2)}) collective-permute-start(bf16[1536,768]{1,0:T(8,128)(2,1)} %all-gather.5.cloned.1.call-done), channel_id=1, source_target_pairs={{0,1},{1,0},{2,3},{3,2},{4,5},{5,4},{6,7},{7,6},{8,9},{9,8},{10,11... | collective-permute-start | bytes 7077896 | tf_op jit(solution)/shard_map/ppermute | solution.py:130
  188.4 3.4 copy-start.4
  200.5 8.3 %copy-start.2 = (f32[2,768,2048]{2,1,0:T(8,128)S(1)}, f32[2,768,2048]{2,1,0:T(8,128)}, u32[]{:S(2)}) copy-start(f32[2,768,2048]{2,1,0:T(8,128)} %get-tuple-element.23) | copy-start | bytes 37748740
  200.5 8.5 %copy-start.7 = (bf16[2048,2,128]{2,0,1:T(8,128)(2,1)S(1)}, bf16[2048,2,128]{2,0,1:T(8,128)(2,1)}, u32[]{:S(2)}) copy-start(bf16[2048,2,128]{2,0,1:T(8,128)(2,1)} %copy.134) | copy-start | bytes 3145732
  213.5 4.8 %copy-start.21 = (pred[128,4]{0,1:T(4,128)(4,1)S(1)}, pred[128,4]{0,1:T(4,128)(4,1)}, u32[]{:S(2)}) copy-start(pred[128,4]{0,1:T(4,128)(4,1)} %iota_compare_fusion.5) | copy-start | bytes 1540
  213.9 6.1 %copy-start.13 = (bf16[1536,32]{0,1:T(8,128)(2,1)S(1)}, bf16[1536,32]{0,1:T(8,128)(2,1)}, u32[]{:S(2)}) copy-start(bf16[1536,32]{0,1:T(8,128)(2,1)} %param.26) | copy-start | bytes 294916
  220.3 4.0 %copy-start.17 = (s32[128,4]{0,1:T(4,128)S(1)}, s32[128,4]{0,1:T(4,128)}, u32[]{:S(2)}) copy-start(s32[128,4]{0,1:T(4,128)} %multiply_add_fusion) | copy-start | bytes 6148
  224.9 54.6 %slice-start = ((s8[4718592]{0:T(1024)(128)(4,1)}), s8[4194304]{0:T(1024)(128)(4,1)S(1)}, s32[]{:S(2)}) async-start(s8[4718592]{0:T(1024)(128)(4,1)} %bitcast.164), calls=%async_computation.7 | async-start | bytes 8388608
  226.2 53.3 %slice-start.1 = ((s8[4718592]{0:T(1024)(128)(4,1)}), s8[524288]{0:T(1024)(128)(4,1)S(1)}, s32[]{:S(2)}) async-start(s8[4718592]{0:T(1024)(128)(4,1)} %bitcast.164), calls=%async_computation.8 | async-start | bytes 1048576
  277.6 1.9 copy-start.5
  351.3 2.2 copy-start.1
Sparse Core Ops, SparseCore 0:
  75.9 40.6 all-gather.2
  127.3 47.0 all-gather.4

commit v7 on v5

--- a/solution.py
+++ b/solution.py
@@ -8,6 +8,7 @@
 HEAD_SIZE = 128
 QUERY_PER_KEY = 6
 CAP = 40
+LONGEST_PROMPT = 1536
 
 
 norm_eps = 1e-06
@@ -185,12 +186,16 @@
         0,
         tiled=True,
     ).reshape(columns * token_rows, key_value_piece.shape[1])
+    block_tokens = key_value.shape[0]
+    window = min(block_tokens, LONGEST_PROMPT + token_rows)
+    window_start = jnp.clip((col_index + 1) * token_rows - window, 0, block_tokens - window)
+    key_value = lax.dynamic_slice_in_dim(key_value, window_start, window, axis=0)
     segments = (key_value[:, : KEY_HEADS * HEAD_SIZE], key_value[:, KEY_HEADS * HEAD_SIZE :])
     best_experts = jnp.full((KEY_HEADS, QUERY_PER_KEY * token_rows), -1e30, jnp.float32)
     segment_length = segments[0].shape[0]
     key_lines = segments[0].reshape(segment_length, KEY_HEADS, HEAD_SIZE).transpose(1, 0, 2)
     value_lines = segments[1].reshape(segment_length, KEY_HEADS, HEAD_SIZE).transpose(1, 0, 2)
-    key_index = jnp.arange(segment_length, dtype=jnp.int32)
+    key_index = window_start + jnp.arange(segment_length, dtype=jnp.int32)
     key_prompt = prompt_layout(lengths_row, key_index)[0]
     allowed = (key_prompt[None, :] == query_prompt[:, None]) & (
         key_index[None, :] <= query_index[:, None]

time: 358 us -> 354 us (0.989)
  transfers between devices with their start and end apart: 7 -> 7, of which waited for: 4 -> 4; matrix products, arithmetic and copies ran while one was open for 17% -> 16% of each run, Pallas kernels for 0% -> 0%
where the time goes in v7:
time: 354 us
  waiting for transfers between devices  113 us (32%)
  blocking collectives  103 us (29%)
  matrix products  44.6 us (13%)
  local copies, waits for them, and re-layouts  38.9 us (11%)
  starting transfers between devices  22.8 us (6%)
  other arithmetic  17.1 us (5%)
  between operations  14.1 us (4%)
    all_to_all x1, blocking collectives, local(): lax.all_to_all(sending, 'col', split_axis=0, concat_axis=0, tiled=True)  52 us
    all_to_all x1, blocking collectives, local(): lax.all_to_all(answered, 'col', split_axis=0, concat_axis=0, tiled=True)  51.5 us
    all_gather x2, waiting for transfers between devices, gather_halves(): own = lax.all_gather(own, 'row', axis=0, tiled=True)  40.7 us
    all_to_all x1, waiting for transfers between devices, local(): bundle = lax.all_to_all(bundle, 'col', 0, 0, tiled=True)  29.7 us
    all_to_all x1, waiting for transfers between devices, local(): lax.all_to_all(jnp.broadcast_to(reduced[None], (columns,) + reduced.shape...  22.5 us
    all_to_all x1, waiting for transfers between devices, local(): lax.all_to_all(jnp.broadcast_to(key_value_piece[None], (columns,) + key_v...  19.6 us
    dot_general x1, matrix products, local(): jnp.einsum('sjcf,jfd->sjcd', hidden_vals, expert_down_weight, preferred_e...  12.6 us
    all_to_all x1, starting transfers between devices, local(): bundle = lax.all_to_all(bundle, 'col', 0, 0, tiled=True)  8.57 us
  transfers between devices with their start and end apart: 7, of which 4 were waited for; matrix products, arithmetic and copies ran while one was open for 16% of the time, Pallas kernels for 0%

profile of v7, /device:TPU:1, one launch (start us, length us, event | category | flops | bytes accessed | tf_op | source)
XLA Modules:
  0.0 353.6 jit_solution(6263122237845206974)
XLA Ops:
  6.5 0.9 constant_dynamic-slice_fusion.4
  7.5 1.5 gather_fusion.2
  9.0 1.5 gather_fusion.3
  10.5 1.5 gather_fusion.4
  12.9 1.1 reshape.393
  14.4 1.5 pad_maximum_fusion
  16.0 8.6 %all-to-all-start = ((bf16[16,544,128]{2,1,0:T(8,128)(2,1)}), bf16[16,544,128]{2,1,0:T(8,128)(2,1)S(1)}, u32[]{:S(2)}, u32[]{:S(2)}) async-start(bf16[16,544,128]{2,1,0:T(8,128)(2,1)} %pad_maximum_fusion), calls=%async_computation | async-start | bytes 4456448 | tf_op jit(solution)/shard_map/all_to_all | solution.py:114
  24.6 29.7 %all-to-all-done = bf16[16,544,128]{2,1,0:T(8,128)(2,1)S(1)} async-done(((bf16[16,544,128]{2,1,0:T(8,128)(2,1)}), bf16[16,544,128]{2,1,0:T(8,128)(2,1)S(1)}, u32[]{:S(2)}, u32[]{:S(2)}) %all-to-all-start) | async-done | bytes 2228256 | tf_op jit(solution)/shard_map/all_to_all | solution.py:114
  54.4 0.8 constant_dynamic-slice_fusion.2
  55.2 40.7 %all-gather.3.cloned.1.call-done = bf16[1536,1024]{1,0:T(8,128)(2,1)} async-done(((bf16[192,1024]{1,0:T(8,128)(2,1)}), bf16[1536,1024]{1,0:T(8,128)(2,1)}) %all-gather.3.cloned.1.call-update) | async-done | bytes 3145744 | tf_op jit(solution)/shard_map/all_gather | solution.py:131
  96.0 3.0 collective-permute-start
  100.0 1.4 reshape.403
  101.4 2.6 copy.136
  104.0 2.0 reshape.404
  105.9 0.7 constant_dynamic-slice_fusion.1
  107.6 1.2 reduce-window.11
  108.9 1.0 broadcast_in_dim.194
  109.9 6.5 %all-to-all-start.1 = ((bf16[16,208,128]{2,1,0:T(8,128)(2,1)}), bf16[16,208,128]{2,1,0:T(8,128)(2,1)S(1)}, u32[]{:S(2)}, u32[]{:S(2)}) async-start(bf16[16,208,128]{2,1,0:T(8,128)(2,1)} %broadcast_in_dim.194), calls=%async_computation.1 | async-start | bytes 1703936 | tf_op jit(solution)/shard_map/all_to_all | solution.py:122
  116.7 22.5 %all-to-all-done.1 = bf16[16,208,128]{2,1,0:T(8,128)(2,1)S(1)} async-done(((bf16[16,208,128]{2,1,0:T(8,128)(2,1)}), bf16[16,208,128]{2,1,0:T(8,128)(2,1)S(1)}, u32[]{:S(2)}, u32[]{:S(2)}) %all-to-all-start.1) | async-done | bytes 852000 | tf_op jit(solution)/shard_map/all_to_all | solution.py:122
  139.1 1.9 reshape.395
  141.1 2.6 convolution_dynamic-update-slice_fusion.1
  143.7 2.5 convolution_dynamic-update-slice_fusion
  146.2 1.9 fusion.24
  148.9 1.8 broadcast_in_dim.199
  150.7 4.4 %all-to-all-start.2 = ((bf16[16,128,512]{1,2,0:T(8,128)(2,1)}), bf16[16,128,512]{1,2,0:T(8,128)(2,1)S(1)}, u32[]{:S(2)}, u32[]{:S(2)}) async-start(bf16[16,128,512]{1,2,0:T(8,128)(2,1)} %broadcast_in_dim.199), calls=%async_computation.2 | async-start | bytes 4194304 | tf_op jit(solution)/shard_map/all_to_all | solution.py:182
  156.6 0.8 convert_reduce_fusion.1
  158.8 2.2 compare_and_fusion
  161.2 1.2 copy.127
  162.4 1.2 subtract_convert_fusion.1
  163.9 19.6 %all-to-all-done.2 = bf16[16,128,512]{1,2,0:T(8,128)(2,1)S(1)} async-done(((bf16[16,128,512]{1,2,0:T(8,128)(2,1)}), bf16[16,128,512]{1,2,0:T(8,128)(2,1)S(1)}, u32[]{:S(2)}, u32[]{:S(2)}) %all-to-all-start.2) | async-done | bytes 2097184 | tf_op jit(solution)/shard_map/all_to_all | solution.py:182
  183.8 1.7 fusion.88
  185.6 2.2 copy.133
  187.7 6.4 %select_reduce_fusion = (f32[2,768]{1,0:T(2,128)S(1)}, f32[2,768,1664]{2,1,0:T(8,128)}) fusion(pred[768,1664]{1,0:T(8,128)(4,1)S(1)} %copy-done.4, bf16[2,768,128]{2,1,0:T(8,128)(2,1)S(1)} %bitcast.153, bf16[1664,2,128]{2,0,1:T(8,128)(2,1)} %copy.133), kind=kOutput, calls=%fused_computation.6 | convolution fusion | flops 661977600 | bytes 12752896 | tf_op jit(solution)/shard_map/hqd,hkd->hqk/dot_general | solution.py:203
  194.1 1.2 copy.134
  195.4 7.0 %fusion = f32[2,768]{1,0:T(2,128)S(1)} fusion(f32[2,768,1664]{2,1,0:T(8,128)} %get-tuple-element.23, f32[2,768]{1,0:T(2,128)S(1)} %broadcast_maximum_fusion, pred[768,1664]{1,0:T(8,128)(4,1)S(1)} %copy-done.4), kind=kLoop, calls=%fused_computation.7 | loop fusion | flops 10222080 | bytes 11513856 | tf_op jit(solution)/shard_map/reduce_sum | solution.py:209
  202.5 3.6 %fusion.44 = bf16[2,768,128]{2,1,0:T(8,128)(2,1)S(1)} fusion(f32[2,768,1664]{2,1,0:T(8,128)S(1)} %copy-done.2, f32[2,768]{1,0:T(2,128)S(1)} %broadcast_maximum_fusion, pred[768,1664]{1,0:T(8,128)(4,1)S(1)} %copy-done.4, bf16[1664,2,128]{2,0,1:T(8,128)(2,1)S(1)} %copy-done.7, f32[2,768]{1,0:T(2,128)S(1)} %fusion), kind=kOutput, calls=%fused_computation.54 | convolution fusion | flops 664928256 | bytes 12759040 | tf_op jit(solution)/shard_map/hqk,hkd->hqd/dot_general | solution.py:210
  206.4 2.2 convolution_dynamic-update-slice_fusion.3
  208.6 2.2 convolution_dynamic-update-slice_fusion.2
  210.8 1.6 multiply_reduce_fusion
  212.8 3.8 %gather_fusion.1 = f32[512]{0:T(512)S(1)} fusion(f32[128,32]{0,1:T(8,128)S(1)} %fusion.83, s32[512]{0:T(512)S(1)} %reshape.441), kind=kCustom, calls=%fused_computation.4 | custom fusion | bytes 8192 | tf_op jit(solution)/shard_map/jit(take_along_axis)/gather | solution.py:230
  217.4 1.3 convolution_convert_fusion
  218.7 52.0 %all_to_all.25 = bf16[16,2,40,1536]{3,2,1,0:T(8,128)(2,1)S(1)} all-to-all(bf16[16,2,40,1536]{3,2,1,0:T(8,128)(2,1)S(1)} %bitcast.143), channel_id=1, replica_groups=mesh['row'=8,'col'=16] {'col'}, dimensions={0} | all-to-all | bytes 7864320 | tf_op jit(solution)/shard_map/all_to_all | solution.py:244
  270.7 1.9 copy-done.6
  272.6 5.2 %fusion.7 = f32[2,16,40,768]{3,2,1,0:T(8,128)} fusion(bf16[2,1536,768]{2,1,0:T(8,128)(2,1)S(1)} %bitcast.161, bf16[16,2,40,1536]{3,2,1,0:T(8,128)(2,1)S(1)} %all_to_all.25), kind=kOutput, calls=%fused_computation.15 | convolution fusion | flops 3019898880 | bytes 12582912 | tf_op jit(solution)/shard_map/sjcd,jdf->sjcf/dot_general | solution.py:248
  277.7 12.6 %fusion.14 = bf16[16,2,40,1536]{3,2,0,1:T(8,128)(2,1)} fusion(bf16[2,768,1536]{2,1,0:T(8,128)(2,1)} %param.33, f32[2,16,40,768]{3,2,1,0:T(8,128)} %fusion.7, bf16[2,1536,768]{2,1,0:T(8,128)(2,1)} %param.31, bf16[16,2,40,1536]{3,2,1,0:T(8,128)(2,1)} %copy-done.6), kind=kOutput, calls=%fused_computation.21 | convolution fusion | flops 6044712960 | bytes 21233664 | tf_op jit(solution)/shard_map/sjcf,jfd->sjcd/dot_general | solution.py:252
  290.4 2.6 copy.146
  293.0 51.5 %all_to_all.26 = bf16[16,2,40,1536]{3,2,1,0:T(8,128)(2,1)S(1)} all-to-all(bf16[16,2,40,1536]{3,2,1,0:T(8,128)(2,1)S(1)} %copy.146), channel_id=1, replica_groups=mesh['row'=8,'col'=16] {'col'}, dimensions={0} | all-to-all | bytes 7864320 | tf_op jit(solution)/shard_map/all_to_all | solution.py:255
  345.2 1.6 fusion.27
  (124 shorter events, 10.3 us)
Async XLA Ops:
  6.5 5.5 %copy-start = (bf16[4,16,2048]{2,1,0:T(8,128)(2,1)S(1)}, bf16[4,16,2048]{2,1,0:T(8,128)(2,1)}, u32[]{:S(2)}) copy-start(bf16[4,16,2048]{2,1,0:T(8,128)(2,1)} %param.28) | copy-start | bytes 786436
  6.5 7.5 %copy-start.13 = (bf16[192,96]{1,0:T(8,128)(2,1)S(1)}, bf16[192,96]{1,0:T(8,128)(2,1)}, u32[]{:S(2)}) copy-start(bf16[192,96]{1,0:T(8,128)(2,1)} %param.25) | copy-start | bytes 110596
  6.5 7.6 %copy-start.12 = (bf16[192,128]{1,0:T(8,128)(2,1)S(1)}, bf16[192,128]{1,0:T(8,128)(2,1)}, u32[]{:S(2)}) copy-start(bf16[192,128]{1,0:T(8,128)(2,1)} %param.24) | copy-start | bytes 147460
  16.0 83.3 %copy-start.11 = (s32[128,4]{0,1:T(4,128)S(1)}, s32[128,4]{0,1:T(4,128)}, u32[]{:S(2)}) copy-start(s32[128,4]{0,1:T(4,128)} %param.21) | copy-start | bytes 6148
  16.0 38.3 %all-to-all-start = ((bf16[16,544,128]{2,1,0:T(8,128)(2,1)}), bf16[16,544,128]{2,1,0:T(8,128)(2,1)S(1)}, u32[]{:S(2)}, u32[]{:S(2)}) async-start(bf16[16,544,128]{2,1,0:T(8,128)(2,1)} %pad_maximum_fusion), calls=%async_computation | async-start | bytes 4456448 | tf_op jit(solution)/shard_map/all_to_all | solution.py:114
  24.5 71.4 %all-gather.3.cloned.1.call-start = ((), (), s32[]{:S(2)}) async-start(), calls=%async_computation.5 | async-start | bytes 3538944 | tf_op jit(solution)/shard_map/all_gather | solution.py:131
  54.4 52.6 %copy-start.14 = (bf16[1536]{0:T(1024)(128)(2,1)S(1)}, bf16[1536]{0:T(1024)(128)(2,1)}, u32[]{:S(2)}) copy-start(bf16[1536]{0:T(1024)(128)(2,1)} %param.22) | copy-start | bytes 9220
  55.2 105.8 %all-gather.5.cloned.1.call-start = ((), (), s32[]{:S(2)}) async-start(), calls=%async_computation.6 | async-start | bytes 2654208 | tf_op jit(solution)/shard_map/all_gather | solution.py:131
  96.0 47.7 %collective-permute-start = (bf16[1536,1024]{1,0:T(8,128)(2,1)}, bf16[1536,1024]{1,0:T(8,128)(2,1)}, u32[]{:S(2)}, u32[]{:S(2)}) collective-permute-start(bf16[1536,1024]{1,0:T(8,128)(2,1)} %all-gather.3.cloned.1.call-done), channel_id=1, source_target_pairs={{0,1},{1,0},{2,3},{3,2},{4,5},{5,4},{6,7},{7,6},{8,9},{9,8},{10,11... | collective-permute-start | bytes 9437192 | tf_op jit(solution)/shard_map/ppermute | solution.py:132
  99.3 0.6 copy-start.17
  99.5 10.4 %copy-start.18 = (s32[128]{0:T(128)}, s32[128]{0:T(128)S(1)}, u32[]{:S(2)}) copy-start(s32[128]{0:T(128)S(1)} %iota_add_fusion.1) | copy-start | bytes 1540
  99.6 17.0 %copy-start.19 = (s32[128]{0:T(128)}, s32[128]{0:T(128)S(1)}, u32[]{:S(2)}) copy-start(s32[128]{0:T(128)S(1)} %convert_reduce_fusion.2) | copy-start | bytes 1540
  101.4 15.1 %copy-start.3 = (bf16[128,1536]{1,0:T(8,128)(2,1)S(1)}, bf16[128,1536]{1,0:T(8,128)(2,1)}, u32[]{:S(2)}) copy-start(bf16[128,1536]{1,0:T(8,128)(2,1)} %param.18) | copy-start | bytes 1179652
  106.9 0.6 copy-start.8
  106.9 0.6 copy-start.9
  109.9 29.2 %all-to-all-start.1 = ((bf16[16,208,128]{2,1,0:T(8,128)(2,1)}), bf16[16,208,128]{2,1,0:T(8,128)(2,1)S(1)}, u32[]{:S(2)}, u32[]{:S(2)}) async-start(bf16[16,208,128]{2,1,0:T(8,128)(2,1)} %broadcast_in_dim.194), calls=%async_computation.1 | async-start | bytes 1703936 | tf_op jit(solution)/shard_map/all_to_all | solution.py:122
  116.6 29.6 %copy-start.15 = (pred[128,4]{0,1:T(4,128)(4,1)}, pred[128,4]{0,1:T(4,128)(4,1)S(1)}, u32[]{:S(2)}) copy-start(pred[128,4]{0,1:T(4,128)(4,1)S(1)} %iota_compare_fusion.3) | copy-start | bytes 1540
  148.1 2.5 copy-start.5
  150.7 32.8 %all-to-all-start.2 = ((bf16[16,128,512]{1,2,0:T(8,128)(2,1)}), bf16[16,128,512]{1,2,0:T(8,128)(2,1)S(1)}, u32[]{:S(2)}, u32[]{:S(2)}) async-start(bf16[16,128,512]{1,2,0:T(8,128)(2,1)} %broadcast_in_dim.199), calls=%async_computation.2 | async-start | bytes 4194304 | tf_op jit(solution)/shard_map/all_to_all | solution.py:182
  155.1 6.1 %slice-start = ((f32[128,2048]{1,0:T(8,128)}), f32[128,1536]{1,0:T(8,128)S(1)}, s32[]{:S(2)}) async-start(f32[128,2048]{1,0:T(8,128)} %copy-done.5), calls=%async_computation.7 | async-start | bytes 1572864 | tf_op jit(solution)/shard_map/slice | solution.py:163
  161.0 47.7 %collective-permute-start.1 = (bf16[1536,768]{1,0:T(8,128)(2,1)}, bf16[1536,768]{1,0:T(8,128)(2,1)}, u32[]{:S(2)}, u32[]{:S(2)}) collective-permute-start(bf16[1536,768]{1,0:T(8,128)(2,1)} %all-gather.5.cloned.1.call-done), channel_id=1, source_target_pairs={{0,1},{1,0},{2,3},{3,2},{4,5},{5,4},{6,7},{7,6},{8,9},{9,8},{10,11... | collective-permute-start | bytes 7077896 | tf_op jit(solution)/shard_map/ppermute | solution.py:132
  183.8 3.9 %copy-start.4 = (pred[768,1664]{1,0:T(8,128)(4,1)S(1)}, pred[768,1664]{1,0:T(8,128)(4,1)}, u32[]{:S(2)}) copy-start(pred[768,1664]{1,0:T(8,128)(4,1)} %compare_and_fusion) | copy-start | bytes 3833860
  195.4 7.0 %copy-start.2 = (f32[2,768,1664]{2,1,0:T(8,128)S(1)}, f32[2,768,1664]{2,1,0:T(8,128)}, u32[]{:S(2)}) copy-start(f32[2,768,1664]{2,1,0:T(8,128)} %get-tuple-element.23) | copy-start | bytes 30670852
  195.4 7.1 %copy-start.7 = (bf16[1664,2,128]{2,0,1:T(8,128)(2,1)S(1)}, bf16[1664,2,128]{2,0,1:T(8,128)(2,1)}, u32[]{:S(2)}) copy-start(bf16[1664,2,128]{2,0,1:T(8,128)(2,1)} %copy.134) | copy-start | bytes 2555908
  206.1 4.7 %copy-start.16 = (pred[128,4]{0,1:T(4,128)(4,1)S(1)}, pred[128,4]{0,1:T(4,128)(4,1)}, u32[]{:S(2)}) copy-start(pred[128,4]{0,1:T(4,128)(4,1)} %copy-done.15) | copy-start | bytes 1540
  206.4 6.1 %copy-start.10 = (bf16[1536,32]{0,1:T(8,128)(2,1)S(1)}, bf16[1536,32]{0,1:T(8,128)(2,1)}, u32[]{:S(2)}) copy-start(bf16[1536,32]{0,1:T(8,128)(2,1)} %param.26) | copy-start | bytes 294916
  217.4 55.2 %slice-start.1 = ((s8[4718592]{0:T(1024)(128)(4,1)}), s8[4194304]{0:T(1024)(128)(4,1)S(1)}, s32[]{:S(2)}) async-start(s8[4718592]{0:T(1024)(128)(4,1)} %bitcast.160), calls=%async_computation.8 | async-start | bytes 8388608
  218.7 53.9 %slice-start.2 = ((s8[4718592]{0:T(1024)(128)(4,1)}), s8[524288]{0:T(1024)(128)(4,1)S(1)}, s32[]{:S(2)}) async-start(s8[4718592]{0:T(1024)(128)(4,1)} %bitcast.160), calls=%async_computation.9 | async-start | bytes 1048576
  270.7 1.9 copy-start.6
  344.4 2.3 copy-start.1
Sparse Core Ops, SparseCore 0:
  55.3 40.6 all-gather.2
  106.8 44.6 all-gather.4

commit v8 on v7

--- a/solution.py
+++ b/solution.py
@@ -241,18 +241,21 @@
         picks.T.astype(jnp.bfloat16), normed_two, preferred_element_type=jnp.float32
     ).astype(jnp.bfloat16)
     sending = dispatch_rows.reshape(columns, local_experts, CAP, model_width)
-    arrived = lax.all_to_all(sending, "col", split_axis=0, concat_axis=0, tiled=True)
-    gate_vals = jnp.einsum(
-        "sjcd,jdf->sjcf", arrived, expert_gate_weight, preferred_element_type=jnp.float32
-    )
-    up_vals = jnp.einsum(
-        "sjcd,jdf->sjcf", arrived, expert_up_weight, preferred_element_type=jnp.float32
-    )
-    hidden_vals = (jnp.maximum(gate_vals, 0.0) * up_vals).astype(jnp.bfloat16)
-    answered = jnp.einsum(
-        "sjcf,jfd->sjcd", hidden_vals, expert_down_weight, preferred_element_type=jnp.float32
-    ).astype(jnp.bfloat16)
-    returned = lax.all_to_all(answered, "col", split_axis=0, concat_axis=0, tiled=True)
+    answers = []
+    for j in range(local_experts):
+        arrived = lax.all_to_all(sending[:, j], "col", split_axis=0, concat_axis=0, tiled=True)
+        gate_vals = jnp.einsum(
+            "scd,df->scf", arrived, expert_gate_weight[j], preferred_element_type=jnp.float32
+        )
+        up_vals = jnp.einsum(
+            "scd,df->scf", arrived, expert_up_weight[j], preferred_element_type=jnp.float32
+        )
+        hidden_vals = (jnp.maximum(gate_vals, 0.0) * up_vals).astype(jnp.bfloat16)
+        answered = jnp.einsum(
+            "scf,fd->scd", hidden_vals, expert_down_weight[j], preferred_element_type=jnp.float32
+        ).astype(jnp.bfloat16)
+        answers.append(lax.all_to_all(answered, "col", split_axis=0, concat_axis=0, tiled=True))
+    returned = jnp.stack(answers, axis=1)
     returned_rows = returned.reshape(slot_total, model_width)
     mix_matrix = jnp.sum(jnp.where(matches, mixing[:, :, None], 0.0), axis=1)
     mix_high = mix_matrix.astype(jnp.bfloat16)

time: 354 us -> 359 us (1.014)
  blocking collectives: 103 us -> 62.1 us
  waiting for transfers between devices: 113 us -> 141 us
  matrix products: 44.6 us -> 54.7 us
  starting transfers between devices: 22.8 us -> 32 us
    all_to_all x0 -> x2, waiting for transfers between devices: none -> 26.2 us  [the longest x1 13.1 us: local(): lax.all_to_all(answered, 'col', split_axis=0, concat_axis=0, tiled=True)]
    all_to_all x1, blocking collectives: 52 us -> 30.9 us  [local(): lax.all_to_all(sending[:, j], 'col', split_axis=0, concat_axis=0, tiled=T...]
    all_to_all x1, blocking collectives: 51.5 us -> 31.2 us  [local(): lax.all_to_all(answered, 'col', split_axis=0, concat_axis=0, tiled=True)]
    dot_general x2 -> x4, matrix products: 17.8 us -> 27.9 us  [the longest x2 17.4 us: local(): jnp.einsum('scf,fd->scd', hidden_vals, expert_down_weight[j], preferred_e...]
    all_to_all x0 -> x2, starting transfers between devices: none -> 9.29 us  [the longest x1 4.76 us: local(): lax.all_to_all(sending[:, j], 'col', split_axis=0, concat_axis=0, tiled=T...]
  transfers between devices with their start and end apart: 7 -> 9, of which waited for: 4 -> 6; matrix products, arithmetic and copies ran while one was open for 16% -> 22% of each run, Pallas kernels for 0% -> 0%
where the time goes in v8:
time: 359 us; the launch traced here: 358 us
  waiting for transfers between devices  141 us (39%)
  blocking collectives  62.1 us (17%)
  matrix products  54.7 us (15%)
  local copies, waits for them, and re-layouts  37.1 us (10%)
  starting transfers between devices  32 us (9%)
  other arithmetic  17 us (5%)
  between operations  14.2 us (4%)
    all_gather x2, waiting for transfers between devices, gather_halves(): own = lax.all_gather(own, 'row', axis=0, tiled=True)  40.7 us
    all_to_all x1, blocking collectives, local(): lax.all_to_all(answered, 'col', split_axis=0, concat_axis=0, tiled=True)  31.2 us
    all_to_all x1, blocking collectives, local(): lax.all_to_all(sending[:, j], 'col', split_axis=0, concat_axis=0, tiled=T...  30.9 us
    all_to_all x1, waiting for transfers between devices, local(): bundle = lax.all_to_all(bundle, 'col', 0, 0, tiled=True)  29.7 us
    all_to_all x1, waiting for transfers between devices, local(): lax.all_to_all(jnp.broadcast_to(reduced[None], (columns,) + reduced.shape...  22.4 us
    all_to_all x1, waiting for transfers between devices, local(): lax.all_to_all(jnp.broadcast_to(key_value_piece[None], (columns,) + key_v...  22.2 us
    dot_general x2, matrix products, local(): jnp.einsum('scf,fd->scd', hidden_vals, expert_down_weight[j], preferred_e...  17.4 us
    all_to_all x1, waiting for transfers between devices, local(): lax.all_to_all(answered, 'col', split_axis=0, concat_axis=0, tiled=True)  13.1 us
  transfers between devices with their start and end apart: 9, of which 6 were waited for; matrix products, arithmetic and copies ran while one was open for 22% of the time, Pallas kernels for 0%

profile of v8, /device:TPU:1, one launch (start us, length us, event | category | flops | bytes accessed | tf_op | source)
XLA Modules:
  0.0 358.4 jit_solution(18221772386517095247)
XLA Ops:
  7.5 1.5 gather_fusion.2
  9.0 1.5 gather_fusion.3
  10.5 1.5 gather_fusion.4
  14.4 1.5 pad_maximum_fusion.1
  16.0 8.4 %all-to-all-start = ((bf16[16,544,128]{2,1,0:T(8,128)(2,1)}), bf16[16,544,128]{2,1,0:T(8,128)(2,1)S(1)}, u32[]{:S(2)}, u32[]{:S(2)}) async-start(bf16[16,544,128]{2,1,0:T(8,128)(2,1)} %pad_maximum_fusion.1), calls=%async_computation | async-start | bytes 4456448 | tf_op jit(solution)/shard_map/all_to_all | solution.py:114
  24.5 29.7 %all-to-all-done = bf16[16,544,128]{2,1,0:T(8,128)(2,1)S(1)} async-done(((bf16[16,544,128]{2,1,0:T(8,128)(2,1)}), bf16[16,544,128]{2,1,0:T(8,128)(2,1)S(1)}, u32[]{:S(2)}, u32[]{:S(2)}) %all-to-all-start) | async-done | bytes 2228256 | tf_op jit(solution)/shard_map/all_to_all | solution.py:114
  55.1 40.7 %all-gather.3.cloned.1.call-done = bf16[1536,1024]{1,0:T(8,128)(2,1)} async-done(((bf16[192,1024]{1,0:T(8,128)(2,1)}), bf16[1536,1024]{1,0:T(8,128)(2,1)}) %all-gather.3.cloned.1.call-update) | async-done | bytes 3145744 | tf_op jit(solution)/shard_map/all_gather | solution.py:131
  95.8 3.0 collective-permute-start
  100.1 1.4 reshape.403
  101.5 2.5 copy.137
  104.0 2.0 reshape.404
  110.0 6.5 %all-to-all-start.1 = ((bf16[16,208,128]{2,1,0:T(8,128)(2,1)}), bf16[16,208,128]{2,1,0:T(8,128)(2,1)S(1)}, u32[]{:S(2)}, u32[]{:S(2)}) async-start(bf16[16,208,128]{2,1,0:T(8,128)(2,1)} %broadcast_in_dim.194), calls=%async_computation.1 | async-start | bytes 1703936 | tf_op jit(solution)/shard_map/all_to_all | solution.py:122
  116.7 22.4 %all-to-all-done.1 = bf16[16,208,128]{2,1,0:T(8,128)(2,1)S(1)} async-done(((bf16[16,208,128]{2,1,0:T(8,128)(2,1)}), bf16[16,208,128]{2,1,0:T(8,128)(2,1)S(1)}, u32[]{:S(2)}, u32[]{:S(2)}) %all-to-all-start.1) | async-done | bytes 852000 | tf_op jit(solution)/shard_map/all_to_all | solution.py:122
  139.2 1.8 reshape.395
  141.1 2.6 convolution_dynamic-update-slice_fusion.1
  143.7 2.5 convolution_dynamic-update-slice_fusion
  146.2 1.9 fusion.10
  148.9 1.8 broadcast_in_dim.199
  150.7 4.4 %all-to-all-start.2 = ((bf16[16,128,512]{1,2,0:T(8,128)(2,1)}), bf16[16,128,512]{1,2,0:T(8,128)(2,1)S(1)}, u32[]{:S(2)}, u32[]{:S(2)}) async-start(bf16[16,128,512]{1,2,0:T(8,128)(2,1)} %broadcast_in_dim.199), calls=%async_computation.2 | async-start | bytes 4194304 | tf_op jit(solution)/shard_map/all_to_all | solution.py:182
  156.2 2.2 compare_and_fusion
  158.6 1.2 copy.128
  159.8 1.2 subtract_convert_fusion.1
  161.3 22.2 %all-to-all-done.2 = bf16[16,128,512]{1,2,0:T(8,128)(2,1)S(1)} async-done(((bf16[16,128,512]{1,2,0:T(8,128)(2,1)}), bf16[16,128,512]{1,2,0:T(8,128)(2,1)S(1)}, u32[]{:S(2)}, u32[]{:S(2)}) %all-to-all-start.2) | async-done | bytes 2097184 | tf_op jit(solution)/shard_map/all_to_all | solution.py:182
  183.9 1.7 fusion.88
  185.6 2.2 copy.134
  187.8 6.4 %select_reduce_fusion = (f32[2,768]{1,0:T(2,128)S(1)}, f32[2,768,1664]{2,1,0:T(8,128)}) fusion(pred[768,1664]{1,0:T(8,128)(4,1)S(1)} %copy-done.5, bf16[2,768,128]{2,1,0:T(8,128)(2,1)S(1)} %bitcast.173, bf16[1664,2,128]{2,0,1:T(8,128)(2,1)} %copy.134), kind=kOutput, calls=%fused_computation.6 | convolution fusion | flops 661977600 | bytes 12752896 | tf_op jit(solution)/shard_map/hqd,hkd->hqk/dot_general | solution.py:203
  194.2 1.3 copy.135
  195.5 7.0 %fusion = f32[2,768]{1,0:T(2,128)S(1)} fusion(f32[2,768,1664]{2,1,0:T(8,128)} %get-tuple-element.25, f32[2,768]{1,0:T(2,128)S(1)} %broadcast_maximum_fusion, pred[768,1664]{1,0:T(8,128)(4,1)S(1)} %copy-done.5), kind=kLoop, calls=%fused_computation.7 | loop fusion | flops 10222080 | bytes 11513856 | tf_op jit(solution)/shard_map/reduce_sum | solution.py:209
  202.6 3.6 %fusion.39 = bf16[2,768,128]{2,1,0:T(8,128)(2,1)S(1)} fusion(f32[2,768,1664]{2,1,0:T(8,128)S(1)} %copy-done.2, f32[2,768]{1,0:T(2,128)S(1)} %broadcast_maximum_fusion, pred[768,1664]{1,0:T(8,128)(4,1)S(1)} %copy-done.5, bf16[1664,2,128]{2,0,1:T(8,128)(2,1)S(1)} %copy-done.8, f32[2,768]{1,0:T(2,128)S(1)} %fusion), kind=kOutput, calls=%fused_computation.64 | convolution fusion | flops 664928256 | bytes 12759040 | tf_op jit(solution)/shard_map/hqk,hkd->hqd/dot_general | solution.py:210
  206.5 2.2 convolution_dynamic-update-slice_fusion.3
  208.7 2.2 convolution_dynamic-update-slice_fusion.2
  210.9 1.6 multiply_reduce_fusion
  212.9 3.8 %gather_fusion.1 = f32[512]{0:T(512)S(1)} fusion(f32[128,32]{0,1:T(8,128)S(1)} %fusion.83, s32[512]{0:T(512)S(1)} %reshape.441), kind=kCustom, calls=%fused_computation.4 | custom fusion | bytes 8192 | tf_op jit(solution)/shard_map/jit(take_along_axis)/gather | solution.py:230
  216.9 1.5 select_reduce_fusion.1
  218.4 1.3 convolution_convert_fusion
  219.6 1.5 slice_bitcast_fusion.1
  221.2 30.9 %all_to_all.35 = bf16[16,40,1536]{2,1,0:T(8,128)(2,1)} all-to-all(bf16[16,40,1536]{2,1,0:T(8,128)(2,1)S(1)} %get-tuple-element.10), channel_id=1, replica_groups=mesh['row'=8,'col'=16] {'col'}, dimensions={0} | all-to-all | bytes 3932160 | tf_op jit(solution)/shard_map/all_to_all | solution.py:246
  252.0 4.8 %all-to-all-start.5 = ((bf16[16,40,1536]{2,1,0:T(8,128)(2,1)}), bf16[16,40,1536]{2,1,0:T(8,128)(2,1)S(1)}, u32[]{:S(2)}, u32[]{:S(2)}) async-start(bf16[16,40,1536]{2,1,0:T(8,128)(2,1)} %get-tuple-element.11), calls=%async_computation.5 | async-start | bytes 3932160 | tf_op jit(solution)/shard_map/all_to_all | solution.py:246
  256.8 5.2 %fusion.20 = f32[16,40,768]{2,1,0:T(8,128)} fusion(bf16[16,40,1536]{2,1,0:T(8,128)(2,1)} %all_to_all.35, bf16[2,1536,768]{2,1,0:T(8,128)(2,1)} %param.32), kind=kOutput, calls=%fused_computation.37 | convolution fusion | flops 1509949440 | bytes 6291456 | tf_op jit(solution)/shard_map/scd,df->scf/dot_general | solution.py:250
  262.0 8.7 %convolution_convert_fusion.2 = bf16[16,40,1536]{2,1,0:T(8,128)(2,1)} fusion(bf16[2,768,1536]{2,1,0:T(8,128)(2,1)} %param.33, f32[16,40,768]{2,1,0:T(8,128)} %fusion.20, bf16[16,40,1536]{2,1,0:T(8,128)(2,1)} %all_to_all.35, bf16[2,1536,768]{2,1,0:T(8,128)(2,1)} %param.31), kind=kOutput, calls=%fused_computation.15 | convolution fusion | flops 3022356480 | bytes 10616832 | tf_op jit(solution)/shard_map/scf,fd->scd/dot_general | solution.py:254
  270.8 13.0 %all-to-all-done.5 = bf16[16,40,1536]{2,1,0:T(8,128)(2,1)S(1)} async-done(((bf16[16,40,1536]{2,1,0:T(8,128)(2,1)}), bf16[16,40,1536]{2,1,0:T(8,128)(2,1)S(1)}, u32[]{:S(2)}, u32[]{:S(2)}) %all-to-all-start.5) | async-done | bytes 1966112 | tf_op jit(solution)/shard_map/all_to_all | solution.py:246
  283.8 1.3 copy-done.7
  285.1 4.5 %all-to-all-start.4 = ((bf16[16,40,1536]{2,1,0:T(8,128)(2,1)}), bf16[16,40,1536]{2,1,0:T(8,128)(2,1)S(1)}, u32[]{:S(2)}, u32[]{:S(2)}) async-start(bf16[16,40,1536]{2,1,0:T(8,128)(2,1)} %convolution_convert_fusion.2), calls=%async_computation.4 | async-start | bytes 3932160 | tf_op jit(solution)/shard_map/all_to_all | solution.py:257
  289.6 5.2 %fusion.15 = f32[16,40,768]{2,1,0:T(8,128)} fusion(bf16[16,40,1536]{2,1,0:T(8,128)(2,1)} %copy-done.7, bf16[2,1536,768]{2,1,0:T(8,128)(2,1)} %param.32), kind=kOutput, calls=%fused_computation.32 | convolution fusion | flops 1509949440 | bytes 6291456 | tf_op jit(solution)/shard_map/scd,df->scf/dot_general | solution.py:250
  294.9 8.7 %convolution_convert_fusion.1 = bf16[16,40,1536]{2,1,0:T(8,128)(2,1)} fusion(bf16[2,768,1536]{2,1,0:T(8,128)(2,1)} %param.33, f32[16,40,768]{2,1,0:T(8,128)} %fusion.15, bf16[16,40,1536]{2,1,0:T(8,128)(2,1)} %copy-done.7, bf16[2,1536,768]{2,1,0:T(8,128)(2,1)} %param.31), kind=kOutput, calls=%fused_computation.14 | convolution fusion | flops 3022356480 | bytes 10616832 | tf_op jit(solution)/shard_map/scf,fd->scd/dot_general | solution.py:254
  303.6 13.1 %all-to-all-done.4 = bf16[16,40,1536]{2,1,0:T(8,128)(2,1)S(1)} async-done(((bf16[16,40,1536]{2,1,0:T(8,128)(2,1)}), bf16[16,40,1536]{2,1,0:T(8,128)(2,1)S(1)}, u32[]{:S(2)}, u32[]{:S(2)}) %all-to-all-start.4) | async-done | bytes 1966112 | tf_op jit(solution)/shard_map/all_to_all | solution.py:257
  316.7 31.2 %all_to_all.36 = bf16[16,40,1536]{2,1,0:T(8,128)(2,1)S(1)} all-to-all(bf16[16,40,1536]{2,1,0:T(8,128)(2,1)} %convolution_convert_fusion.1), channel_id=1, replica_groups=mesh['row'=8,'col'=16] {'col'}, dimensions={0} | all-to-all | bytes 3932160 | tf_op jit(solution)/shard_map/all_to_all | solution.py:257
  350.0 1.5 fusion.13
  (137 shorter events, 15.2 us)
Async XLA Ops:
  6.5 5.5 %copy-start = (bf16[4,16,2048]{2,1,0:T(8,128)(2,1)S(1)}, bf16[4,16,2048]{2,1,0:T(8,128)(2,1)}, u32[]{:S(2)}) copy-start(bf16[4,16,2048]{2,1,0:T(8,128)(2,1)} %param.28) | copy-start | bytes 786436
  12.7 1.4 copy-start.14
  12.7 1.5 copy-start.13
  16.0 38.2 %all-to-all-start = ((bf16[16,544,128]{2,1,0:T(8,128)(2,1)}), bf16[16,544,128]{2,1,0:T(8,128)(2,1)S(1)}, u32[]{:S(2)}, u32[]{:S(2)}) async-start(bf16[16,544,128]{2,1,0:T(8,128)(2,1)} %pad_maximum_fusion.1), calls=%async_computation | async-start | bytes 4456448 | tf_op jit(solution)/shard_map/all_to_all | solution.py:114
  24.4 74.8 %copy-start.12 = (s32[128,4]{0,1:T(4,128)S(1)}, s32[128,4]{0,1:T(4,128)}, u32[]{:S(2)}) copy-start(s32[128,4]{0,1:T(4,128)} %param.21) | copy-start | bytes 6148
  24.4 71.4 %all-gather.3.cloned.1.call-start = ((), (), s32[]{:S(2)}) async-start(), calls=%async_computation.7 | async-start | bytes 3538944 | tf_op jit(solution)/shard_map/all_gather | solution.py:131
  55.0 103.4 %all-gather.5.cloned.1.call-start = ((), (), s32[]{:S(2)}) async-start(), calls=%async_computation.8 | async-start | bytes 2654208 | tf_op jit(solution)/shard_map/all_gather | solution.py:131
  95.8 47.9 %collective-permute-start = (bf16[1536,1024]{1,0:T(8,128)(2,1)}, bf16[1536,1024]{1,0:T(8,128)(2,1)}, u32[]{:S(2)}, u32[]{:S(2)}) collective-permute-start(bf16[1536,1024]{1,0:T(8,128)(2,1)} %all-gather.3.cloned.1.call-done), channel_id=1, source_target_pairs={{0,1},{1,0},{2,3},{3,2},{4,5},{5,4},{6,7},{7,6},{8,9},{9,8},{10,11... | collective-permute-start | bytes 9437192 | tf_op jit(solution)/shard_map/ppermute | solution.py:132
  99.1 0.9 copy-start.19
  99.4 0.5 copy-start.21
  99.5 17.2 %copy-start.23 = (s32[128]{0:T(128)}, s32[128]{0:T(128)S(1)}, u32[]{:S(2)}) copy-start(s32[128]{0:T(128)S(1)} %convert_reduce_fusion.2) | copy-start | bytes 1540
  100.1 6.9 %copy-start.15 = (bf16[1536]{0:T(1024)(128)(2,1)S(1)}, bf16[1536]{0:T(1024)(128)(2,1)}, u32[]{:S(2)}) copy-start(bf16[1536]{0:T(1024)(128)(2,1)} %param.22) | copy-start | bytes 9220
  105.9 10.6 %copy-start.3 = (bf16[128,1536]{1,0:T(8,128)(2,1)S(1)}, bf16[128,1536]{1,0:T(8,128)(2,1)}, u32[]{:S(2)}) copy-start(bf16[128,1536]{1,0:T(8,128)(2,1)} %param.18) | copy-start | bytes 1179652
  106.9 0.6 copy-start.9
  106.9 0.6 copy-start.10
  110.0 29.2 %all-to-all-start.1 = ((bf16[16,208,128]{2,1,0:T(8,128)(2,1)}), bf16[16,208,128]{2,1,0:T(8,128)(2,1)S(1)}, u32[]{:S(2)}, u32[]{:S(2)}) async-start(bf16[16,208,128]{2,1,0:T(8,128)(2,1)} %broadcast_in_dim.194), calls=%async_computation.1 | async-start | bytes 1703936 | tf_op jit(solution)/shard_map/all_to_all | solution.py:122
  116.7 29.6 %copy-start.17 = (pred[128,4]{0,1:T(4,128)(4,1)}, pred[128,4]{0,1:T(4,128)(4,1)S(1)}, u32[]{:S(2)}) copy-start(pred[128,4]{0,1:T(4,128)(4,1)S(1)} %iota_compare_fusion.3) | copy-start | bytes 1540
  148.2 2.5 copy-start.6
  150.7 4.8 %copy-start.16 = (bf16[1536]{0:T(1024)(128)(2,1)S(1)}, bf16[1536]{0:T(1024)(128)(2,1)}, u32[]{:S(2)}) copy-start(bf16[1536]{0:T(1024)(128)(2,1)} %param.23) | copy-start | bytes 9220
  150.7 5.3 %copy-start.20 = (s32[4,1]{0,1:T(1,128)S(1)}, s32[4,1]{0,1:T(1,128)}, u32[]{:S(2)}) copy-start(s32[4,1]{0,1:T(1,128)} %copy-done.19) | copy-start | bytes 52
  150.7 5.5 %copy-start.24 = (s32[128]{0:T(128)S(1)}, s32[128]{0:T(128)}, u32[]{:S(2)}) copy-start(s32[128]{0:T(128)} %copy-done.23) | copy-start | bytes 1540
  150.7 5.5 %copy-start.22 = (s32[128]{0:T(128)S(1)}, s32[128]{0:T(128)}, u32[]{:S(2)}) copy-start(s32[128]{0:T(128)} %copy-done.21) | copy-start | bytes 1540
  150.7 32.9 %all-to-all-start.2 = ((bf16[16,128,512]{1,2,0:T(8,128)(2,1)}), bf16[16,128,512]{1,2,0:T(8,128)(2,1)S(1)}, u32[]{:S(2)}, u32[]{:S(2)}) async-start(bf16[16,128,512]{1,2,0:T(8,128)(2,1)} %broadcast_in_dim.199), calls=%async_computation.2 | async-start | bytes 4194304 | tf_op jit(solution)/shard_map/all_to_all | solution.py:182
  155.1 3.5 slice-start
  158.4 50.3 %collective-permute-start.1 = (bf16[1536,768]{1,0:T(8,128)(2,1)}, bf16[1536,768]{1,0:T(8,128)(2,1)}, u32[]{:S(2)}, u32[]{:S(2)}) collective-permute-start(bf16[1536,768]{1,0:T(8,128)(2,1)} %all-gather.5.cloned.1.call-done), channel_id=1, source_target_pairs={{0,1},{1,0},{2,3},{3,2},{4,5},{5,4},{6,7},{7,6},{8,9},{9,8},{10,11... | collective-permute-start | bytes 7077896 | tf_op jit(solution)/shard_map/ppermute | solution.py:132
  183.9 3.9 %copy-start.5 = (pred[768,1664]{1,0:T(8,128)(4,1)S(1)}, pred[768,1664]{1,0:T(8,128)(4,1)}, u32[]{:S(2)}) copy-start(pred[768,1664]{1,0:T(8,128)(4,1)} %compare_and_fusion) | copy-start | bytes 3833860
  195.5 7.0 %copy-start.2 = (f32[2,768,1664]{2,1,0:T(8,128)S(1)}, f32[2,768,1664]{2,1,0:T(8,128)}, u32[]{:S(2)}) copy-start(f32[2,768,1664]{2,1,0:T(8,128)} %get-tuple-element.25) | copy-start | bytes 30670852
  195.5 7.1 %copy-start.8 = (bf16[1664,2,128]{2,0,1:T(8,128)(2,1)S(1)}, bf16[1664,2,128]{2,0,1:T(8,128)(2,1)}, u32[]{:S(2)}) copy-start(bf16[1664,2,128]{2,0,1:T(8,128)(2,1)} %copy.135) | copy-start | bytes 2555908
  208.6 2.3 copy-start.18
  208.7 3.9 %copy-start.11 = (bf16[1536,32]{0,1:T(8,128)(2,1)S(1)}, bf16[1536,32]{0,1:T(8,128)(2,1)}, u32[]{:S(2)}) copy-start(bf16[1536,32]{0,1:T(8,128)(2,1)} %param.26) | copy-start | bytes 294916
  252.0 31.8 %all-to-all-start.5 = ((bf16[16,40,1536]{2,1,0:T(8,128)(2,1)}), bf16[16,40,1536]{2,1,0:T(8,128)(2,1)S(1)}, u32[]{:S(2)}, u32[]{:S(2)}) async-start(bf16[16,40,1536]{2,1,0:T(8,128)(2,1)} %get-tuple-element.11), calls=%async_computation.5 | async-start | bytes 3932160 | tf_op jit(solution)/shard_map/all_to_all | solution.py:246
  283.8 1.3 copy-start.7
  285.1 31.6 %all-to-all-start.4 = ((bf16[16,40,1536]{2,1,0:T(8,128)(2,1)}), bf16[16,40,1536]{2,1,0:T(8,128)(2,1)S(1)}, u32[]{:S(2)}, u32[]{:S(2)}) async-start(bf16[16,40,1536]{2,1,0:T(8,128)(2,1)} %convolution_convert_fusion.2), calls=%async_computation.4 | async-start | bytes 3932160 | tf_op jit(solution)/shard_map/all_to_all | solution.py:257
  348.3 1.1 copy-start.4
  349.3 2.2 copy-start.1
Sparse Core Ops, SparseCore 0:
  55.2 40.6 all-gather.2
  106.8 44.6 all-gather.4

commit v9 on v7

--- a/solution.py
+++ b/solution.py
@@ -125,12 +125,19 @@
     core_index = col_index % 2
     partner = [(c, c ^ 1) for c in range(columns)]
 
-    def gather_halves(slab):
-        half = slab.shape[1] // 2
-        own = lax.dynamic_slice_in_dim(slab, core_index * half, half, axis=1)
-        own = lax.all_gather(own, "row", axis=0, tiled=True)
-        other = lax.ppermute(own, "col", partner)
-        return own, other
+    def gather_halves(slab_list):
+        owns = []
+        for slab in slab_list:
+            half = slab.shape[1] // 2
+            owns.append(lax.dynamic_slice_in_dim(slab, core_index * half, half, axis=1))
+        widths_own = [own.shape[1] for own in owns]
+        joined = lax.all_gather(jnp.concatenate(owns, axis=1), "row", axis=0, tiled=True)
+        swapped = lax.ppermute(joined, "col", partner)
+        cuts = [sum(widths_own[:i]) for i in range(len(widths_own) + 1)]
+        return [
+            (joined[:, cuts[i] : cuts[i + 1]], swapped[:, cuts[i] : cuts[i + 1]])
+            for i in range(len(owns))
+        ]
 
     def times_halves(inputs, halves):
         own, other = halves
@@ -146,8 +153,7 @@
             1,
         )
 
-    qkv_halves = gather_halves(slabs[0])
-    out_halves = gather_halves(slabs[1])
+    qkv_halves, out_halves = gather_halves(slabs)
     maps = spread.reshape(picked_shape)
     widths = [table.shape[-1] for table in tables]
     bounds = [sum(widths[:i]) for i in range(len(widths) + 1)]

time: 354 us -> 366 us (1.034)
  waiting for transfers between devices: 113 us -> 130 us
    all_gather x2 -> x1, waiting for transfers between devices: 40.7 us -> 63.8 us  [gather_halves(): lax.all_gather(jnp.concatenate(owns, axis=1), 'row', axis=0, tiled=True)]
    all_to_all x1, waiting for transfers between devices: 22.5 us -> 14.5 us  [local(): lax.all_to_all(jnp.broadcast_to(reduced[None], (columns,) + reduced.shape...]
  transfers between devices with their start and end apart: 7 -> 5, of which waited for: 4 -> 4; matrix products, arithmetic and copies ran while one was open for 16% -> 4% of each run, Pallas kernels for 0% -> 0%
where the time goes in v9:
time: 366 us; the launch traced here: 365 us
  waiting for transfers between devices  130 us (36%)
  blocking collectives  104 us (28%)
  matrix products  46 us (13%)
  local copies, waits for them, and re-layouts  35.6 us (10%)
  starting transfers between devices  20.6 us (6%)
  other arithmetic  15.1 us (4%)
  between operations  14.2 us (4%)
    all_gather x1, waiting for transfers between devices, gather_halves(): lax.all_gather(jnp.concatenate(owns, axis=1), 'row', axis=0, tiled=True)  63.8 us
    all_to_all x1, blocking collectives, local(): lax.all_to_all(sending, 'col', split_axis=0, concat_axis=0, tiled=True)  52.2 us
    all_to_all x1, blocking collectives, local(): lax.all_to_all(answered, 'col', split_axis=0, concat_axis=0, tiled=True)  51.5 us
    all_to_all x1, waiting for transfers between devices, local(): bundle = lax.all_to_all(bundle, 'col', 0, 0, tiled=True)  29.7 us
    all_to_all x1, waiting for transfers between devices, local(): lax.all_to_all(jnp.broadcast_to(key_value_piece[None], (columns,) + key_v...  21.7 us
    all_to_all x1, waiting for transfers between devices, local(): lax.all_to_all(jnp.broadcast_to(reduced[None], (columns,) + reduced.shape...  14.5 us
    dot_general x1, matrix products, local(): jnp.einsum('sjcf,jfd->sjcd', hidden_vals, expert_down_weight, preferred_e...  12.6 us
    all_to_all x1, starting transfers between devices, local(): bundle = lax.all_to_all(bundle, 'col', 0, 0, tiled=True)  8.44 us
  transfers between devices with their start and end apart: 5, of which 4 were waited for; matrix products, arithmetic and copies ran while one was open for 4% of the time, Pallas kernels for 0%

profile of v9, /device:TPU:1, one launch (start us, length us, event | category | flops | bytes accessed | tf_op | source)
XLA Modules:
  0.0 364.9 jit_solution(163386391294002305)
XLA Ops:
  6.5 0.9 constant_dynamic-slice_fusion.4
  7.5 1.5 gather_fusion.2
  9.0 1.5 gather_fusion.3
  10.5 1.5 gather_fusion.4
  12.9 1.1 reshape.393
  14.4 1.5 pad_maximum_fusion
  16.0 8.4 %all-to-all-start = ((bf16[16,544,128]{2,1,0:T(8,128)(2,1)}), bf16[16,544,128]{2,1,0:T(8,128)(2,1)S(1)}, u32[]{:S(2)}, u32[]{:S(2)}) async-start(bf16[16,544,128]{2,1,0:T(8,128)(2,1)} %pad_maximum_fusion), calls=%async_computation | async-start | bytes 4456448 | tf_op jit(solution)/shard_map/all_to_all | solution.py:114
  24.5 29.7 %all-to-all-done = bf16[16,544,128]{2,1,0:T(8,128)(2,1)S(1)} async-done(((bf16[16,544,128]{2,1,0:T(8,128)(2,1)}), bf16[16,544,128]{2,1,0:T(8,128)(2,1)S(1)}, u32[]{:S(2)}, u32[]{:S(2)}) %all-to-all-start) | async-done | bytes 2228256 | tf_op jit(solution)/shard_map/all_to_all | solution.py:114
  54.1 0.8 slice.100
  55.0 1.7 reshape.395
  56.7 1.4 copy.127
  58.1 2.0 reshape.396
  60.2 0.9 pad_maximum_fusion.2
  61.2 63.8 %all-gather.2.cloned.1.call-done = bf16[1536,1792]{1,0:T(8,128)(2,1)} async-done(((bf16[192,1792]{1,0:T(8,128)(2,1)}), bf16[1536,1792]{1,0:T(8,128)(2,1)}) %all-gather.2.cloned.1.call-update) | async-done | bytes 5505040 | tf_op jit(solution)/shard_map/all_gather | solution.py:134
  125.0 0.8 collective-permute-start
  127.1 0.7 copy.131
  128.1 1.2 reduce-window.11
  129.4 1.0 broadcast_in_dim.194
  130.4 6.5 %all-to-all-start.1 = ((bf16[16,208,128]{2,1,0:T(8,128)(2,1)}), bf16[16,208,128]{2,1,0:T(8,128)(2,1)S(1)}, u32[]{:S(2)}, u32[]{:S(2)}) async-start(bf16[16,208,128]{2,1,0:T(8,128)(2,1)} %broadcast_in_dim.194), calls=%async_computation.1 | async-start | bytes 1703936 | tf_op jit(solution)/shard_map/all_to_all | solution.py:122
  137.2 14.5 %all-to-all-done.1 = bf16[16,208,128]{2,1,0:T(8,128)(2,1)S(1)} async-done(((bf16[16,208,128]{2,1,0:T(8,128)(2,1)}), bf16[16,208,128]{2,1,0:T(8,128)(2,1)S(1)}, u32[]{:S(2)}, u32[]{:S(2)}) %all-to-all-start.1) | async-done | bytes 852000 | tf_op jit(solution)/shard_map/all_to_all | solution.py:122
  151.6 1.8 reshape.397
  153.6 2.6 fusion.47
  156.2 2.5 fusion.50
  158.8 1.9 fusion.28
  161.5 1.8 broadcast_in_dim.199
  163.2 4.8 %all-to-all-start.2 = ((bf16[16,128,512]{1,2,0:T(8,128)(2,1)}), bf16[16,128,512]{1,2,0:T(8,128)(2,1)S(1)}, u32[]{:S(2)}, u32[]{:S(2)}) async-start(bf16[16,128,512]{1,2,0:T(8,128)(2,1)} %broadcast_in_dim.199), calls=%async_computation.2 | async-start | bytes 4194304 | tf_op jit(solution)/shard_map/all_to_all | solution.py:188
  169.1 2.2 compare_and_fusion
  171.3 1.0 slice.106
  172.3 1.4 copy.128
  173.8 0.9 copy.129
  174.8 21.7 %all-to-all-done.2 = bf16[16,128,512]{1,2,0:T(8,128)(2,1)S(1)} async-done(((bf16[16,128,512]{1,2,0:T(8,128)(2,1)}), bf16[16,128,512]{1,2,0:T(8,128)(2,1)S(1)}, u32[]{:S(2)}, u32[]{:S(2)}) %all-to-all-start.2) | async-done | bytes 2097184 | tf_op jit(solution)/shard_map/all_to_all | solution.py:188
  196.8 0.9 fusion.108
  198.2 7.8 %select_reduce_fusion = (f32[2,768]{1,0:T(2,128)S(1)}, f32[2,768,1664]{2,1,0:T(8,128)}) fusion(pred[768,1664]{1,0:T(8,128)(4,1)} %compare_and_fusion, bf16[2,768,128]{2,1,0:T(8,128)(2,1)} %bitcast.149, bf16[1664,2,128]{2,0,1:T(8,128)(2,1)S(1)} %copy.134), kind=kOutput, calls=%fused_computation.6 | convolution fusion | flops 661977600 | bytes 12752896 | tf_op jit(solution)/shard_map/hqd,hkd->hqk/dot_general | solution.py:209
  206.7 6.5 %fusion = f32[2,768]{1,0:T(2,128)S(1)} fusion(f32[2,768,1664]{2,1,0:T(8,128)} %get-tuple-element.23, f32[2,768]{1,0:T(2,128)S(1)} %broadcast_maximum_fusion, pred[768,1664]{1,0:T(8,128)(4,1)S(1)} %copy-done.3), kind=kLoop, calls=%fused_computation.7 | loop fusion | flops 10222080 | bytes 11513856 | tf_op jit(solution)/shard_map/reduce_sum | solution.py:215
  213.6 3.6 fusion.64
  217.5 2.2 fusion.53
  219.8 2.2 fusion.56
  221.9 1.6 multiply_reduce_fusion
  223.9 3.8 %gather_fusion.1 = f32[512]{0:T(512)S(1)} fusion(f32[128,32]{0,1:T(8,128)S(1)} %fusion.103, s32[512]{0:T(512)S(1)} %reshape.441), kind=kCustom, calls=%fused_computation.4 | custom fusion | bytes 8192 | tf_op jit(solution)/shard_map/jit(take_along_axis)/gather | solution.py:236
  228.5 1.3 convolution_convert_fusion
  229.8 52.2 %all_to_all.25 = bf16[16,2,40,1536]{3,2,1,0:T(8,128)(2,1)S(1)} all-to-all(bf16[16,2,40,1536]{3,2,1,0:T(8,128)(2,1)S(1)} %bitcast.139), channel_id=1, replica_groups=mesh['row'=8,'col'=16] {'col'}, dimensions={0} | all-to-all | bytes 7864320 | tf_op jit(solution)/shard_map/all_to_all | solution.py:250
  282.0 1.9 copy-done.4
  283.9 5.2 %fusion.7 = f32[2,16,40,768]{3,2,1,0:T(8,128)} fusion(bf16[2,1536,768]{2,1,0:T(8,128)(2,1)S(1)} %bitcast.157, bf16[16,2,40,1536]{3,2,1,0:T(8,128)(2,1)S(1)} %all_to_all.25), kind=kOutput, calls=%fused_computation.15 | convolution fusion | flops 3019898880 | bytes 12582912 | tf_op jit(solution)/shard_map/sjcd,jdf->sjcf/dot_general | solution.py:254
  289.1 12.6 %fusion.14 = bf16[16,2,40,1536]{3,2,0,1:T(8,128)(2,1)} fusion(bf16[2,768,1536]{2,1,0:T(8,128)(2,1)} %param.33, f32[2,16,40,768]{3,2,1,0:T(8,128)} %fusion.7, bf16[2,1536,768]{2,1,0:T(8,128)(2,1)} %param.31, bf16[16,2,40,1536]{3,2,1,0:T(8,128)(2,1)} %copy-done.4), kind=kOutput, calls=%fused_computation.21 | convolution fusion | flops 6044712960 | bytes 21233664 | tf_op jit(solution)/shard_map/sjcf,jfd->sjcd/dot_general | solution.py:258
  301.7 2.6 copy.146
  304.3 51.5 %all_to_all.26 = bf16[16,2,40,1536]{3,2,1,0:T(8,128)(2,1)S(1)} all-to-all(bf16[16,2,40,1536]{3,2,1,0:T(8,128)(2,1)S(1)} %copy.146), channel_id=1, replica_groups=mesh['row'=8,'col'=16] {'col'}, dimensions={0} | all-to-all | bytes 7864320 | tf_op jit(solution)/shard_map/all_to_all | solution.py:261
  355.8 0.7 fusion.83
  356.5 1.6 fusion.31
  (121 shorter events, 8.6 us)
Async XLA Ops:
  6.5 5.5 %copy-start = (bf16[4,16,2048]{2,1,0:T(8,128)(2,1)S(1)}, bf16[4,16,2048]{2,1,0:T(8,128)(2,1)}, u32[]{:S(2)}) copy-start(bf16[4,16,2048]{2,1,0:T(8,128)(2,1)} %param.28) | copy-start | bytes 786436
  6.5 7.5 %copy-start.12 = (bf16[192,96]{1,0:T(8,128)(2,1)S(1)}, bf16[192,96]{1,0:T(8,128)(2,1)}, u32[]{:S(2)}) copy-start(bf16[192,96]{1,0:T(8,128)(2,1)} %param.25) | copy-start | bytes 110596
  6.5 7.6 %copy-start.11 = (bf16[192,128]{1,0:T(8,128)(2,1)S(1)}, bf16[192,128]{1,0:T(8,128)(2,1)}, u32[]{:S(2)}) copy-start(bf16[192,128]{1,0:T(8,128)(2,1)} %param.24) | copy-start | bytes 147460
  16.0 38.2 %all-to-all-start = ((bf16[16,544,128]{2,1,0:T(8,128)(2,1)}), bf16[16,544,128]{2,1,0:T(8,128)(2,1)S(1)}, u32[]{:S(2)}, u32[]{:S(2)}) async-start(bf16[16,544,128]{2,1,0:T(8,128)(2,1)} %pad_maximum_fusion), calls=%async_computation | async-start | bytes 4456448 | tf_op jit(solution)/shard_map/all_to_all | solution.py:114
  24.4 100.6 %all-gather.2.cloned.1.call-start = ((), (), s32[]{:S(2)}) async-start(), calls=%async_computation.5 | async-start | bytes 6193152 | tf_op jit(solution)/shard_map/all_gather | solution.py:134
  56.7 69.2 %copy-start.13 = (bf16[1536]{0:T(1024)(128)(2,1)S(1)}, bf16[1536]{0:T(1024)(128)(2,1)}, u32[]{:S(2)}) copy-start(bf16[1536]{0:T(1024)(128)(2,1)} %param.22) | copy-start | bytes 9220
  56.7 71.2 %copy-start.10 = (s32[128,4]{0,1:T(4,128)S(1)}, s32[128,4]{0,1:T(4,128)}, u32[]{:S(2)}) copy-start(s32[128,4]{0,1:T(4,128)} %param.21) | copy-start | bytes 6148
  60.1 76.9 %copy-start.5 = (bf16[128,1536]{1,0:T(8,128)(2,1)S(1)}, bf16[128,1536]{1,0:T(8,128)(2,1)}, u32[]{:S(2)}) copy-start(bf16[128,1536]{1,0:T(8,128)(2,1)} %param.18) | copy-start | bytes 1179652
  125.0 31.2 %collective-permute-start = (bf16[1536,1792]{1,0:T(8,128)(2,1)}, bf16[1536,1792]{1,0:T(8,128)(2,1)}, u32[]{:S(2)}, u32[]{:S(2)}) collective-permute-start(bf16[1536,1792]{1,0:T(8,128)(2,1)} %all-gather.2.cloned.1.call-done), channel_id=1, source_target_pairs={{0,1},{1,0},{2,3},{3,2},{4,5},{5,4},{6,7},{7,6},{8,9},{9,8},{10,11... | collective-permute-start | bytes 16515080 | tf_op jit(solution)/shard_map/ppermute | solution.py:135
  126.1 1.9 copy-start.17
  126.2 0.6 copy-start.15
  126.3 29.9 %copy-start.19 = (s32[128]{0:T(128)}, s32[128]{0:T(128)S(1)}, u32[]{:S(2)}) copy-start(s32[128]{0:T(128)S(1)} %convert_reduce_fusion.2) | copy-start | bytes 1540
  130.4 21.2 %all-to-all-start.1 = ((bf16[16,208,128]{2,1,0:T(8,128)(2,1)}), bf16[16,208,128]{2,1,0:T(8,128)(2,1)S(1)}, u32[]{:S(2)}, u32[]{:S(2)}) async-start(bf16[16,208,128]{2,1,0:T(8,128)(2,1)} %broadcast_in_dim.194), calls=%async_computation.1 | async-start | bytes 1703936 | tf_op jit(solution)/shard_map/all_to_all | solution.py:122
  153.6 5.2 %copy-start.6 = (bf16[128,1536]{1,0:T(8,128)(2,1)S(1)}, bf16[128,1536]{1,0:T(8,128)(2,1)}, u32[]{:S(2)}) copy-start(bf16[128,1536]{1,0:T(8,128)(2,1)} %param.18) | copy-start | bytes 1179652
  156.2 4.6 %copy-start.8 = (f32[128,64]{1,0:T(8,128)S(1)}, f32[128,64]{1,0:T(8,128)}, u32[]{:S(2)}) copy-start(f32[128,64]{1,0:T(8,128)} %copy.131) | copy-start | bytes 98308
  160.8 7.6 %copy-start.14 = (bf16[1536]{0:T(1024)(128)(2,1)S(1)}, bf16[1536]{0:T(1024)(128)(2,1)}, u32[]{:S(2)}) copy-start(bf16[1536]{0:T(1024)(128)(2,1)} %param.23) | copy-start | bytes 9220
  161.1 7.8 %copy-start.18 = (s32[4,1]{0,1:T(1,128)S(1)}, s32[4,1]{0,1:T(1,128)}, u32[]{:S(2)}) copy-start(s32[4,1]{0,1:T(1,128)} %copy-done.17) | copy-start | bytes 52
  161.1 7.9 %copy-start.20 = (s32[128]{0:T(128)S(1)}, s32[128]{0:T(128)}, u32[]{:S(2)}) copy-start(s32[128]{0:T(128)} %copy-done.19) | copy-start | bytes 1540
  161.1 7.9 %copy-start.16 = (s32[128]{0:T(128)S(1)}, s32[128]{0:T(128)}, u32[]{:S(2)}) copy-start(s32[128]{0:T(128)} %copy-done.15) | copy-start | bytes 1540
  163.2 33.2 %all-to-all-start.2 = ((bf16[16,128,512]{1,2,0:T(8,128)(2,1)}), bf16[16,128,512]{1,2,0:T(8,128)(2,1)S(1)}, u32[]{:S(2)}, u32[]{:S(2)}) async-start(bf16[16,128,512]{1,2,0:T(8,128)(2,1)} %broadcast_in_dim.199), calls=%async_computation.2 | async-start | bytes 4194304 | tf_op jit(solution)/shard_map/all_to_all | solution.py:188
  198.2 8.5 %copy-start.3 = (pred[768,1664]{1,0:T(8,128)(4,1)S(1)}, pred[768,1664]{1,0:T(8,128)(4,1)}, u32[]{:S(2)}) copy-start(pred[768,1664]{1,0:T(8,128)(4,1)} %compare_and_fusion) | copy-start | bytes 3833860
  206.7 6.9 %copy-start.2 = (f32[2,768,1664]{2,1,0:T(8,128)S(1)}, f32[2,768,1664]{2,1,0:T(8,128)}, u32[]{:S(2)}) copy-start(f32[2,768,1664]{2,1,0:T(8,128)} %get-tuple-element.23) | copy-start | bytes 30670852
  217.2 4.7 %copy-start.7 = (bf16[128,1536]{1,0:T(8,128)(2,1)S(1)}, bf16[128,1536]{1,0:T(8,128)(2,1)}, u32[]{:S(2)}) copy-start(bf16[128,1536]{1,0:T(8,128)(2,1)} %param.18) | copy-start | bytes 1179652
  217.5 6.1 %copy-start.9 = (bf16[1536,32]{0,1:T(8,128)(2,1)S(1)}, bf16[1536,32]{0,1:T(8,128)(2,1)}, u32[]{:S(2)}) copy-start(bf16[1536,32]{0,1:T(8,128)(2,1)} %param.26) | copy-start | bytes 294916
  228.5 55.4 %slice-start = ((s8[4718592]{0:T(1024)(128)(4,1)}), s8[4194304]{0:T(1024)(128)(4,1)S(1)}, s32[]{:S(2)}) async-start(s8[4718592]{0:T(1024)(128)(4,1)} %bitcast.156), calls=%async_computation.6 | async-start | bytes 8388608
  229.8 54.1 %slice-start.1 = ((s8[4718592]{0:T(1024)(128)(4,1)}), s8[524288]{0:T(1024)(128)(4,1)S(1)}, s32[]{:S(2)}) async-start(s8[4718592]{0:T(1024)(128)(4,1)} %bitcast.156), calls=%async_computation.7 | async-start | bytes 1048576
  282.0 1.9 copy-start.4
  355.8 2.3 copy-start.1
Sparse Core Ops, SparseCore 0:
  61.3 63.6 all-gather.1

commit v10 on v7

--- a/solution.py
+++ b/solution.py
@@ -104,20 +104,23 @@
     lane = 128
     chunks = picked.reshape(columns, -1, lane)
     blocks = (projection_weight, output_weight)
-    flat_blocks = [block.reshape(-1, lane) for block in blocks]
-    sizes = [chunks.shape[1]] + [flat.shape[0] for flat in flat_blocks]
+    dest_parity = jnp.arange(columns, dtype=jnp.int32) % 2
+    flat_blocks = []
+    for block in blocks:
+        rows_here, cols_here = block.shape
+        split = block.reshape(rows_here, 2, cols_here // 2)
+        chosen = jnp.take(split, dest_parity, axis=1).transpose(1, 0, 2)
+        flat_blocks.append(chosen.reshape(columns, -1, lane))
+    sizes = [chunks.shape[1]] + [flat.shape[1] for flat in flat_blocks]
     starts = [sum(sizes[:i]) for i in range(len(sizes) + 1)]
-    bundle = jnp.concatenate(
-        [chunks] + [jnp.broadcast_to(flat[None], (columns,) + flat.shape) for flat in flat_blocks],
-        axis=1,
-    )
+    bundle = jnp.concatenate([chunks] + flat_blocks, axis=1)
     bundle = lax.all_to_all(bundle, "col", 0, 0, tiled=True)
     received = bundle[:, starts[0] : starts[1]]
     slabs = []
     for i, block in enumerate(blocks):
         rows_here, cols_here = block.shape
-        piece = bundle[:, starts[i + 1] : starts[i + 2]].reshape(columns, rows_here, cols_here)
-        slabs.append(piece.transpose(1, 0, 2).reshape(rows_here, columns * cols_here))
+        piece = bundle[:, starts[i + 1] : starts[i + 2]].reshape(columns, rows_here, cols_here // 2)
+        slabs.append(piece.transpose(1, 0, 2).reshape(rows_here, columns * (cols_here // 2)))
     reduced = jnp.sum(received.astype(jnp.float32), axis=0).astype(jnp.bfloat16)
     spread = lax.all_to_all(
         jnp.broadcast_to(reduced[None], (columns,) + reduced.shape), "col", 0, 0, tiled=True
@@ -126,25 +129,20 @@
     partner = [(c, c ^ 1) for c in range(columns)]
 
     def gather_halves(slab):
-        half = slab.shape[1] // 2
-        own = lax.dynamic_slice_in_dim(slab, core_index * half, half, axis=1)
-        own = lax.all_gather(own, "row", axis=0, tiled=True)
+        own = lax.all_gather(slab, "row", axis=0, tiled=True)
         other = lax.ppermute(own, "col", partner)
         return own, other
 
     def times_halves(inputs, halves):
         own, other = halves
-        half = own.shape[1]
-        placed = jnp.zeros((inputs.shape[0], 2 * half), jnp.float32)
-        placed = lax.dynamic_update_slice_in_dim(
-            placed, jnp.dot(inputs, own, preferred_element_type=jnp.float32), core_index * half, 1
-        )
-        return lax.dynamic_update_slice_in_dim(
-            placed,
-            jnp.dot(inputs, other, preferred_element_type=jnp.float32),
-            (1 - core_index) * half,
-            1,
-        )
+        piece = own.shape[1] // columns
+        own_part = jnp.dot(inputs, own, preferred_element_type=jnp.float32)
+        other_part = jnp.dot(inputs, other, preferred_element_type=jnp.float32)
+        own_part = own_part.reshape(inputs.shape[0], columns, piece)
+        other_part = other_part.reshape(inputs.shape[0], columns, piece)
+        first = jnp.where(core_index == 0, own_part, other_part)
+        second = jnp.where(core_index == 0, other_part, own_part)
+        return jnp.stack([first, second], axis=2).reshape(inputs.shape[0], 2 * own.shape[1])
 
     qkv_halves = gather_halves(slabs[0])
     out_halves = gather_halves(slabs[1])

time: 354 us -> 361 us (1.020)
  blocking collectives: 103 us -> 134 us
  waiting for transfers between devices: 113 us -> 86 us
  local copies, waits for them, and re-layouts: 38.9 us -> 48.7 us
  starting transfers between devices: 22.8 us -> 18 us
    all_to_all x0 -> x1, blocking collectives: none -> 30.3 us  [local(): bundle = lax.all_to_all(bundle, 'col', 0, 0, tiled=True)]
    all_to_all x1 -> x0, waiting for transfers between devices: 29.7 us -> none  [local(): bundle = lax.all_to_all(bundle, 'col', 0, 0, tiled=True)]
    all_gather x2, waiting for transfers between devices: 40.7 us -> 49.7 us  [gather_halves(): own = lax.all_gather(slab, 'row', axis=0, tiled=True)]
    all_to_all x1 -> x0, starting transfers between devices: 8.57 us -> none  [local(): bundle = lax.all_to_all(bundle, 'col', 0, 0, tiled=True)]
    dot_general x0 -> x2, local copies, waits for them, and re-layouts: none -> 7.19 us  [the longest x1 4.35 us: times_halves(): other_part = jnp.dot(inputs, other, preferred_element_type=jnp.float32)]
    all_to_all x1, waiting for transfers between devices: 19.6 us -> 14.6 us  [local(): lax.all_to_all(jnp.broadcast_to(key_value_piece[None], (columns,) + key_v...]
  transfers between devices with their start and end apart: 7 -> 6, of which waited for: 4 -> 4; matrix products, arithmetic and copies ran while one was open for 16% -> 9% of each run, Pallas kernels for 0% -> 0%
where the time goes in v10:
time: 361 us; the launch traced here: 360 us
  blocking collectives  134 us (37%)
  waiting for transfers between devices  86 us (24%)
  local copies, waits for them, and re-layouts  48.7 us (13%)
  matrix products  41.7 us (12%)
  starting transfers between devices  18 us (5%)
  other arithmetic  17.3 us (5%)
  between operations  14.3 us (4%)
    all_to_all x1, blocking collectives, local(): lax.all_to_all(sending, 'col', split_axis=0, concat_axis=0, tiled=True)  52 us
    all_to_all x1, blocking collectives, local(): lax.all_to_all(answered, 'col', split_axis=0, concat_axis=0, tiled=True)  51.5 us
    all_gather x2, waiting for transfers between devices, gather_halves(): own = lax.all_gather(slab, 'row', axis=0, tiled=True)  49.7 us
    all_to_all x1, blocking collectives, local(): bundle = lax.all_to_all(bundle, 'col', 0, 0, tiled=True)  30.3 us
    all_to_all x1, waiting for transfers between devices, local(): lax.all_to_all(jnp.broadcast_to(reduced[None], (columns,) + reduced.shape...  21.6 us
    all_to_all x1, waiting for transfers between devices, local(): lax.all_to_all(jnp.broadcast_to(key_value_piece[None], (columns,) + key_v...  14.6 us
    dot_general x1, matrix products, local(): jnp.einsum('sjcf,jfd->sjcd', hidden_vals, expert_down_weight, preferred_e...  12.6 us
  transfers between devices with their start and end apart: 6, of which 4 were waited for; matrix products, arithmetic and copies ran while one was open for 9% of the time, Pallas kernels for 0%

profile of v10, /device:TPU:1, one launch (start us, length us, event | category | flops | bytes accessed | tf_op | source)
XLA Modules:
  0.0 359.8 jit_solution(13962131718034418507)
XLA Ops:
  6.6 0.9 dynamic-slice_reduce_fusion
  7.5 1.5 gather_fusion.4
  9.0 1.5 gather_fusion.5
  10.5 1.5 gather_fusion.6
  12.9 1.1 reshape.495
  16.9 1.0 reshape.499
  18.0 30.3 %all_to_all.25 = bf16[16,376,128]{2,1,0:T(8,128)(2,1)S(1)} all-to-all(bf16[16,376,128]{2,1,0:T(8,128)(2,1)S(1)} %pad_maximum_fusion), channel_id=1, replica_groups=mesh['row'=8,'col'=16] {'col'}, dimensions={0} | all-to-all | bytes 3080192 | tf_op jit(solution)/shard_map/all_to_all | solution.py:117
  49.0 0.9 copy.192
  51.0 0.9 copy.207
  51.9 38.2 %all-gather.3.cloned.1.call-done = bf16[1536,1024]{1,0:T(8,128)(2,1)} async-done(((bf16[192,1024]{1,0:T(8,128)(2,1)}), bf16[1536,1024]{1,0:T(8,128)(2,1)}) %all-gather.3.cloned.1.call-update) | async-done | bytes 3145744 | tf_op jit(solution)/shard_map/all_gather | solution.py:132
  90.1 3.0 collective-permute-start
  95.3 1.2 reduce-window.11
  96.6 1.0 broadcast_in_dim.194
  97.6 6.5 %all-to-all-start.1 = ((bf16[16,208,128]{2,1,0:T(8,128)(2,1)}), bf16[16,208,128]{2,1,0:T(8,128)(2,1)S(1)}, u32[]{:S(2)}, u32[]{:S(2)}) async-start(bf16[16,208,128]{2,1,0:T(8,128)(2,1)} %broadcast_in_dim.194), calls=%async_computation.1 | async-start | bytes 1703936 | tf_op jit(solution)/shard_map/all_to_all | solution.py:125
  105.5 21.6 %all-to-all-done.1 = bf16[16,208,128]{2,1,0:T(8,128)(2,1)S(1)} async-done(((bf16[16,208,128]{2,1,0:T(8,128)(2,1)}), bf16[16,208,128]{2,1,0:T(8,128)(2,1)S(1)}, u32[]{:S(2)}, u32[]{:S(2)}) %all-to-all-start.1) | async-done | bytes 852000 | tf_op jit(solution)/shard_map/all_to_all | solution.py:125
  127.0 0.9 reshape.503
  128.0 11.5 %all-gather.5.cloned.1.call-done = bf16[1536,768]{1,0:T(8,128)(2,1)} async-done(((bf16[192,768]{1,0:T(8,128)(2,1)}), bf16[1536,768]{1,0:T(8,128)(2,1)}) %all-gather.5.cloned.1.call-update) | async-done | bytes 2359312 | tf_op jit(solution)/shard_map/all_gather | solution.py:132
  139.5 2.4 collective-permute-start.1
  141.8 2.5 fusion.88
  144.4 2.5 broadcast_select_fusion.3
  147.9 1.4 fusion.24
  149.5 1.2 subtract_convert_fusion.3
  151.0 1.8 broadcast_in_dim.199
  152.9 6.1 %all-to-all-start.2 = ((bf16[16,128,512]{1,2,0:T(8,128)(2,1)}), bf16[16,128,512]{1,2,0:T(8,128)(2,1)}, u32[]{:S(2)}, u32[]{:S(2)}) async-start(bf16[16,128,512]{1,2,0:T(8,128)(2,1)} %broadcast_in_dim.199), calls=%async_computation.2 | async-start | bytes 4194304 | tf_op jit(solution)/shard_map/all_to_all | solution.py:180
  160.6 2.2 compare_and_fusion
  162.7 2.8 copy.208
  165.6 4.4 %copy.210 = bf16[768,1536]{1,0:T(8,128)(2,1)} copy(bf16[768,1536]{0,1:T(8,128)(2,1)} %bitcast.36) | data formatting | bytes 4718592 | tf_op jit(solution)/shard_map/dot_general | solution.py:140
  169.9 1.2 copy.197
  171.2 1.2 subtract_convert_fusion.1
  172.7 14.6 %all-to-all-done.2 = bf16[16,128,512]{1,2,0:T(8,128)(2,1)} async-done(((bf16[16,128,512]{1,2,0:T(8,128)(2,1)}), bf16[16,128,512]{1,2,0:T(8,128)(2,1)}, u32[]{:S(2)}, u32[]{:S(2)}) %all-to-all-start.2) | async-done | bytes 2097184 | tf_op jit(solution)/shard_map/all_to_all | solution.py:180
  187.4 1.9 copy_bitcast_fusion
  189.3 2.0 fusion.90
  191.3 2.2 copy.203
  193.5 6.5 %select_reduce_fusion = (f32[2,768]{1,0:T(2,128)S(1)}, f32[2,768,1664]{2,1,0:T(8,128)}) fusion(pred[768,1664]{1,0:T(8,128)(4,1)} %compare_and_fusion, bf16[2,768,128]{2,1,0:T(8,128)(2,1)S(1)} %bitcast.180, bf16[1664,2,128]{2,0,1:T(8,128)(2,1)} %copy.203), kind=kOutput, calls=%fused_computation.8 | convolution fusion | flops 661977600 | bytes 12752896 | tf_op jit(solution)/shard_map/hqd,hkd->hqk/dot_general | solution.py:201
  200.0 2.2 copy.204
  202.2 7.1 %fusion = f32[2,768]{1,0:T(2,128)S(1)} fusion(f32[2,768,1664]{2,1,0:T(8,128)} %get-tuple-element.27, f32[2,768]{1,0:T(2,128)S(1)} %broadcast_maximum_fusion, pred[768,1664]{1,0:T(8,128)(4,1)} %compare_and_fusion), kind=kLoop, calls=%fused_computation.9 | loop fusion | flops 10222080 | bytes 11513856 | tf_op jit(solution)/shard_map/reduce_sum | solution.py:207
  209.7 4.0 %fusion.44 = bf16[2,768,128]{2,1,0:T(8,128)(2,1)S(1)} fusion(f32[2,768,1664]{2,1,0:T(8,128)S(1)} %copy-done.2, f32[2,768]{1,0:T(2,128)S(1)} %broadcast_maximum_fusion, pred[768,1664]{1,0:T(8,128)(4,1)S(1)} %copy-done.5, bf16[1664,2,128]{2,0,1:T(8,128)(2,1)} %copy.204, f32[2,768]{1,0:T(2,128)S(1)} %fusion), kind=kOutput, calls=%fused_computation.53 | convolution fusion | flops 664928256 | bytes 12759040 | tf_op jit(solution)/shard_map/hqk,hkd->hqd/dot_general | solution.py:208
  214.8 0.9 copy-done.4
  216.9 1.6 multiply_reduce_fusion
  218.8 4.0 %gather_fusion.3 = f32[512]{0:T(512)S(1)} fusion(f32[128,32]{0,1:T(8,128)S(1)} %fusion.83, s32[512]{0:T(512)S(1)} %reshape.566), kind=kCustom, calls=%fused_computation.6 | custom fusion | bytes 8192 | tf_op jit(solution)/shard_map/jit(take_along_axis)/gather | solution.py:228
  223.7 1.3 convolution_convert_fusion
  225.0 52.0 %all_to_all.26 = bf16[16,2,40,1536]{3,2,1,0:T(8,128)(2,1)S(1)} all-to-all(bf16[16,2,40,1536]{3,2,1,0:T(8,128)(2,1)S(1)} %bitcast.158), channel_id=1, replica_groups=mesh['row'=8,'col'=16] {'col'}, dimensions={0} | all-to-all | bytes 7864320 | tf_op jit(solution)/shard_map/all_to_all | solution.py:242
  277.0 1.9 copy-done.7
  278.9 5.1 %fusion.7 = f32[2,16,40,768]{3,2,1,0:T(8,128)} fusion(bf16[2,1536,768]{2,1,0:T(8,128)(2,1)S(1)} %bitcast.188, bf16[16,2,40,1536]{3,2,1,0:T(8,128)(2,1)S(1)} %all_to_all.26), kind=kOutput, calls=%fused_computation.17 | convolution fusion | flops 3019898880 | bytes 12582912 | tf_op jit(solution)/shard_map/sjcd,jdf->sjcf/dot_general | solution.py:246
  284.1 12.6 %fusion.14 = bf16[16,2,40,1536]{3,2,0,1:T(8,128)(2,1)} fusion(bf16[2,768,1536]{2,1,0:T(8,128)(2,1)} %param.33, f32[2,16,40,768]{3,2,1,0:T(8,128)} %fusion.7, bf16[2,1536,768]{2,1,0:T(8,128)(2,1)} %param.31, bf16[16,2,40,1536]{3,2,1,0:T(8,128)(2,1)} %copy-done.7), kind=kOutput, calls=%fused_computation.23 | convolution fusion | flops 6044712960 | bytes 21233664 | tf_op jit(solution)/shard_map/sjcf,jfd->sjcd/dot_general | solution.py:250
  296.7 2.6 copy.223
  299.3 51.5 %all_to_all.27 = bf16[16,2,40,1536]{3,2,1,0:T(8,128)(2,1)S(1)} all-to-all(bf16[16,2,40,1536]{3,2,1,0:T(8,128)(2,1)S(1)} %copy.223), channel_id=1, replica_groups=mesh['row'=8,'col'=16] {'col'}, dimensions={0} | all-to-all | bytes 7864320 | tf_op jit(solution)/shard_map/all_to_all | solution.py:253
  351.4 1.5 fusion.27
  (154 shorter events, 16.7 us)
Async XLA Ops:
  6.5 5.5 %copy-start = (bf16[4,16,2048]{2,1,0:T(8,128)(2,1)S(1)}, bf16[4,16,2048]{2,1,0:T(8,128)(2,1)}, u32[]{:S(2)}) copy-start(bf16[4,16,2048]{2,1,0:T(8,128)(2,1)} %param.28) | copy-start | bytes 786436
  6.5 7.5 %copy-start.13 = (bf16[192,128]{1,0:T(8,128)(2,1)S(1)}, bf16[192,128]{1,0:T(8,128)(2,1)}, u32[]{:S(2)}) copy-start(bf16[192,128]{1,0:T(8,128)(2,1)} %param.24) | copy-start | bytes 147460
  6.5 83.6 %all-gather.3.cloned.1.call-start = ((), (), s32[]{:S(2)}) async-start(), calls=%async_computation.5 | async-start | bytes 3538944 | tf_op jit(solution)/shard_map/all_gather | solution.py:132
  12.9 2.8 copy-start.14
  48.3 44.9 %copy-start.17 = (bf16[1536]{0:T(1024)(128)(2,1)S(1)}, bf16[1536]{0:T(1024)(128)(2,1)}, u32[]{:S(2)}) copy-start(bf16[1536]{0:T(1024)(128)(2,1)} %param.22) | copy-start | bytes 9220
  48.3 46.8 %copy-start.12 = (s32[128,4]{0,1:T(4,128)S(1)}, s32[128,4]{0,1:T(4,128)}, u32[]{:S(2)}) copy-start(s32[128,4]{0,1:T(4,128)} %param.21) | copy-start | bytes 6148
  49.9 54.2 %copy-start.3 = (bf16[128,1536]{1,0:T(8,128)(2,1)S(1)}, bf16[128,1536]{1,0:T(8,128)(2,1)}, u32[]{:S(2)}) copy-start(bf16[128,1536]{1,0:T(8,128)(2,1)} %param.18) | copy-start | bytes 1179652
  49.9 89.5 %all-gather.5.cloned.1.call-start = ((), (), s32[]{:S(2)}) async-start(), calls=%async_computation.6 | async-start | bytes 2654208 | tf_op jit(solution)/shard_map/all_gather | solution.py:132
  90.1 54.3 %collective-permute-start = (bf16[1536,1024]{1,0:T(8,128)(2,1)}, bf16[1536,1024]{1,0:T(8,128)(2,1)}, u32[]{:S(2)}, u32[]{:S(2)}) collective-permute-start(bf16[1536,1024]{1,0:T(8,128)(2,1)} %all-gather.3.cloned.1.call-done), channel_id=1, source_target_pairs={{0,1},{1,0},{2,3},{3,2},{4,5},{5,4},{6,7},{7,6},{8,9},{9,8},{10,11... | collective-permute-start | bytes 9437192 | tf_op jit(solution)/shard_map/ppermute | solution.py:133
  93.4 0.5 copy-start.22
  93.5 0.6 copy-start.20
  93.6 50.8 %copy-start.24 = (s32[128]{0:T(128)}, s32[128]{0:T(128)S(1)}, u32[]{:S(2)}) copy-start(s32[128]{0:T(128)S(1)} %convert_reduce_fusion.2) | copy-start | bytes 1540
  94.2 50.1 %copy-start.9 = (f32[128,64]{0,1:T(8,128)}, f32[128,64]{0,1:T(8,128)S(1)}, u32[]{:S(2)}) copy-start(f32[128,64]{0,1:T(8,128)S(1)} %get-tuple-element.20) | copy-start | bytes 98308
  94.3 50.1 %copy-start.10 = (f32[128,64]{0,1:T(8,128)}, f32[128,64]{0,1:T(8,128)S(1)}, u32[]{:S(2)}) copy-start(f32[128,64]{0,1:T(8,128)S(1)} %get-tuple-element.21) | copy-start | bytes 98308
  97.6 29.4 %all-to-all-start.1 = ((bf16[16,208,128]{2,1,0:T(8,128)(2,1)}), bf16[16,208,128]{2,1,0:T(8,128)(2,1)S(1)}, u32[]{:S(2)}, u32[]{:S(2)}) async-start(bf16[16,208,128]{2,1,0:T(8,128)(2,1)} %broadcast_in_dim.194), calls=%async_computation.1 | async-start | bytes 1703936 | tf_op jit(solution)/shard_map/all_to_all | solution.py:125
  128.0 19.9 %copy-start.8 = (bf16[4,16,6656]{2,1,0:T(8,128)(2,1)}, bf16[4,16,6656]{2,1,0:T(8,128)(2,1)S(1)}, u32[]{:S(2)}) copy-start(bf16[4,16,6656]{2,1,0:T(8,128)(2,1)S(1)} %reshape.503) | copy-start | bytes 2555908
  139.5 26.1 %collective-permute-start.1 = (bf16[1536,768]{1,0:T(8,128)(2,1)}, bf16[1536,768]{1,0:T(8,128)(2,1)}, u32[]{:S(2)}, u32[]{:S(2)}) collective-permute-start(bf16[1536,768]{1,0:T(8,128)(2,1)} %all-gather.5.cloned.1.call-done), channel_id=1, source_target_pairs={{0,1},{1,0},{2,3},{3,2},{4,5},{5,4},{6,7},{7,6},{8,9},{9,8},{10,11... | collective-permute-start | bytes 7077896 | tf_op jit(solution)/shard_map/ppermute | solution.py:133
  149.3 3.5 copy-start.6
  149.4 9.8 %copy-start.18 = (bf16[1536]{0:T(1024)(128)(2,1)S(1)}, bf16[1536]{0:T(1024)(128)(2,1)}, u32[]{:S(2)}) copy-start(bf16[1536]{0:T(1024)(128)(2,1)} %param.23) | copy-start | bytes 9220
  149.4 9.8 %copy-start.16 = (s32[128,4,1]{0,1,2:T(4,128)S(1)}, s32[128,4,1]{0,1,2:T(4,128)}, u32[]{:S(2)}) copy-start(s32[128,4,1]{0,1,2:T(4,128)} %bitcast_or_fusion) | copy-start | bytes 6148
  150.7 9.2 %copy-start.23 = (s32[4,1]{0,1:T(1,128)S(1)}, s32[4,1]{0,1:T(1,128)}, u32[]{:S(2)}) copy-start(s32[4,1]{0,1:T(1,128)} %copy-done.22) | copy-start | bytes 52
  150.7 9.3 %copy-start.25 = (s32[128]{0:T(128)S(1)}, s32[128]{0:T(128)}, u32[]{:S(2)}) copy-start(s32[128]{0:T(128)} %copy-done.24) | copy-start | bytes 1540
  150.7 9.3 %copy-start.21 = (s32[128]{0:T(128)S(1)}, s32[128]{0:T(128)}, u32[]{:S(2)}) copy-start(s32[128]{0:T(128)} %copy-done.20) | copy-start | bytes 1540
  152.9 34.5 %all-to-all-start.2 = ((bf16[16,128,512]{1,2,0:T(8,128)(2,1)}), bf16[16,128,512]{1,2,0:T(8,128)(2,1)}, u32[]{:S(2)}, u32[]{:S(2)}) async-start(bf16[16,128,512]{1,2,0:T(8,128)(2,1)} %broadcast_in_dim.199), calls=%async_computation.2 | async-start | bytes 4194304 | tf_op jit(solution)/shard_map/all_to_all | solution.py:180
  165.6 4.4 %slice-start = ((f32[128,2048]{1,0:T(8,128)}), f32[128,1536]{1,0:T(8,128)S(1)}, s32[]{:S(2)}) async-start(f32[128,2048]{1,0:T(8,128)} %copy-done.6), calls=%async_computation.7 | async-start | bytes 1572864 | tf_op jit(solution)/shard_map/slice | solution.py:161
  202.2 7.2 %copy-start.2 = (f32[2,768,1664]{2,1,0:T(8,128)S(1)}, f32[2,768,1664]{2,1,0:T(8,128)}, u32[]{:S(2)}) copy-start(f32[2,768,1664]{2,1,0:T(8,128)} %get-tuple-element.27) | copy-start | bytes 30670852
  202.2 7.5 %copy-start.5 = (pred[768,1664]{1,0:T(8,128)(4,1)S(1)}, pred[768,1664]{1,0:T(8,128)(4,1)}, u32[]{:S(2)}) copy-start(pred[768,1664]{1,0:T(8,128)(4,1)} %compare_and_fusion) | copy-start | bytes 3833860
  214.0 1.7 copy-start.4
  215.7 1.2 copy-start.19
  216.4 2.1 copy-start.11
  218.8 4.2 %copy-start.15 = (s32[128,4]{0,1:T(4,128)S(1)}, s32[128,4]{0,1:T(4,128)}, u32[]{:S(2)}) copy-start(s32[128,4]{0,1:T(4,128)} %multiply_add_fusion) | copy-start | bytes 6148
  223.7 55.2 %slice-start.1 = ((s8[4718592]{0:T(1024)(128)(4,1)}), s8[4194304]{0:T(1024)(128)(4,1)S(1)}, s32[]{:S(2)}) async-start(s8[4718592]{0:T(1024)(128)(4,1)} %bitcast.187), calls=%async_computation.8 | async-start | bytes 8388608
  225.0 53.9 %slice-start.2 = ((s8[4718592]{0:T(1024)(128)(4,1)}), s8[524288]{0:T(1024)(128)(4,1)S(1)}, s32[]{:S(2)}) async-start(s8[4718592]{0:T(1024)(128)(4,1)} %bitcast.187), calls=%async_computation.9 | async-start | bytes 1048576
  277.0 1.9 copy-start.7
  350.7 2.2 copy-start.1
Sparse Core Ops, SparseCore 0:
  50.1 40.0 all-gather.2
  91.8 47.6 all-gather.4

commit v11 on v10

--- a/solution.py
+++ b/solution.py
@@ -106,10 +106,13 @@
     blocks = (projection_weight, output_weight)
     dest_parity = jnp.arange(columns, dtype=jnp.int32) % 2
     flat_blocks = []
-    for block in blocks:
+    for i, block in enumerate(blocks):
         rows_here, cols_here = block.shape
-        split = block.reshape(rows_here, 2, cols_here // 2)
-        chosen = jnp.take(split, dest_parity, axis=1).transpose(1, 0, 2)
+        if i == 0:
+            split = block.reshape(rows_here, 2, cols_here // 2)
+            chosen = jnp.take(split, dest_parity, axis=1).transpose(1, 0, 2)
+        else:
+            chosen = jnp.broadcast_to(block[None], (columns, rows_here, cols_here))
         flat_blocks.append(chosen.reshape(columns, -1, lane))
     sizes = [chunks.shape[1]] + [flat.shape[1] for flat in flat_blocks]
     starts = [sum(sizes[:i]) for i in range(len(sizes) + 1)]
@@ -119,8 +122,9 @@
     slabs = []
     for i, block in enumerate(blocks):
         rows_here, cols_here = block.shape
-        piece = bundle[:, starts[i + 1] : starts[i + 2]].reshape(columns, rows_here, cols_here // 2)
-        slabs.append(piece.transpose(1, 0, 2).reshape(rows_here, columns * (cols_here // 2)))
+        kept = cols_here // 2 if i == 0 else cols_here
+        piece = bundle[:, starts[i + 1] : starts[i + 2]].reshape(columns, rows_here, kept)
+        slabs.append(piece.transpose(1, 0, 2).reshape(rows_here, columns * kept))
     reduced = jnp.sum(received.astype(jnp.float32), axis=0).astype(jnp.bfloat16)
     spread = lax.all_to_all(
         jnp.broadcast_to(reduced[None], (columns,) + reduced.shape), "col", 0, 0, tiled=True
@@ -145,7 +149,25 @@
         return jnp.stack([first, second], axis=2).reshape(inputs.shape[0], 2 * own.shape[1])
 
     qkv_halves = gather_halves(slabs[0])
-    out_halves = gather_halves(slabs[1])
+    out_half = slabs[1].shape[1] // 2
+    out_halves = gather_halves(
+        lax.dynamic_slice_in_dim(slabs[1], core_index * out_half, out_half, axis=1)
+    )
+
+    def times_blocks(inputs, halves):
+        own, other = halves
+        half = own.shape[1]
+        placed = jnp.zeros((inputs.shape[0], 2 * half), jnp.float32)
+        placed = lax.dynamic_update_slice_in_dim(
+            placed, jnp.dot(inputs, own, preferred_element_type=jnp.float32), core_index * half, 1
+        )
+        return lax.dynamic_update_slice_in_dim(
+            placed,
+            jnp.dot(inputs, other, preferred_element_type=jnp.float32),
+            (1 - core_index) * half,
+            1,
+        )
+
     maps = spread.reshape(picked_shape)
     widths = [table.shape[-1] for table in tables]
     bounds = [sum(widths[:i]) for i in range(len(widths) + 1)]
@@ -218,7 +240,7 @@
         .reshape(token_rows, QUERY_HEADS * HEAD_SIZE)
         .astype(jnp.bfloat16)
     )
-    projected_rows = times_halves(attention_result, out_halves)
+    projected_rows = times_blocks(attention_result, out_halves)
     projected_rows = projected_rows + adapter_scale * adapter_change(
         attention_result, within_prompt, output_down_map, output_up_map
     )

time: 361 us -> 353 us (0.978)
  local copies, waits for them, and re-layouts: 48.7 us -> 43.3 us
  starting transfers between devices: 18 us -> 14.3 us
    all_gather x2, waiting for transfers between devices: 49.7 us -> 39.8 us  [gather_halves(): own = lax.all_gather(slab, 'row', axis=0, tiled=True)]
    dot_general x2 -> x0, local copies, waits for them, and re-layouts: 7.19 us -> none  [the longest x1 4.35 us: times_halves(): other_part = jnp.dot(inputs, other, preferred_element_type=jnp.float32)]
    all_to_all x1, waiting for transfers between devices: 14.6 us -> 19.5 us  [local(): lax.all_to_all(jnp.broadcast_to(key_value_piece[None], (columns,) + key_v...]
    dot_general x0 -> x2, matrix products: none -> 4.39 us  [the longest x1 2.21 us: times_blocks(): jnp.dot(inputs, own, preferred_element_type=jnp.float32)]
  transfers between devices with their start and end apart: 6 -> 6, of which waited for: 4 -> 3; matrix products, arithmetic and copies ran while one was open for 9% -> 16% of each run, Pallas kernels for 0% -> 0%
where the time goes in v11:
time: 353 us; the launch traced here: 352 us
  blocking collectives  137 us (39%)
  waiting for transfers between devices  82.7 us (23%)
  matrix products  44.6 us (13%)
  local copies, waits for them, and re-layouts  43.3 us (12%)
  other arithmetic  16 us (5%)
  starting transfers between devices  14.3 us (4%)
  between operations  14.2 us (4%)
    all_to_all x1, blocking collectives, local(): lax.all_to_all(sending, 'col', split_axis=0, concat_axis=0, tiled=True)  52 us
    all_to_all x1, blocking collectives, local(): lax.all_to_all(answered, 'col', split_axis=0, concat_axis=0, tiled=True)  51.5 us
    all_gather x2, waiting for transfers between devices, gather_halves(): own = lax.all_gather(slab, 'row', axis=0, tiled=True)  39.8 us
    all_to_all x1, blocking collectives, local(): bundle = lax.all_to_all(bundle, 'col', 0, 0, tiled=True)  33.8 us
    all_to_all x1, waiting for transfers between devices, local(): lax.all_to_all(jnp.broadcast_to(reduced[None], (columns,) + reduced.shape...  23.4 us
    all_to_all x1, waiting for transfers between devices, local(): lax.all_to_all(jnp.broadcast_to(key_value_piece[None], (columns,) + key_v...  19.5 us
    dot_general x1, matrix products, local(): jnp.einsum('sjcf,jfd->sjcd', hidden_vals, expert_down_weight, preferred_e...  12.6 us
  transfers between devices with their start and end apart: 6, of which 3 were waited for; matrix products, arithmetic and copies ran while one was open for 16% of the time, Pallas kernels for 0%

profile of v11, /device:TPU:1, one launch (start us, length us, event | category | flops | bytes accessed | tf_op | source)
XLA Modules:
  0.0 352.3 jit_solution(7812873291571173382)
XLA Ops:
  6.6 0.9 dynamic-slice_reduce_fusion
  7.5 1.5 gather_fusion.3
  9.0 1.5 gather_fusion.4
  10.5 1.5 gather_fusion.5
  12.9 1.1 reshape.483
  16.1 33.8 %all_to_all.25 = bf16[16,448,128]{2,1,0:T(8,128)(2,1)S(1)} all-to-all(bf16[16,448,128]{2,1,0:T(8,128)(2,1)S(1)} %pad_maximum_fusion), channel_id=1, replica_groups=mesh['row'=8,'col'=16] {'col'}, dimensions={0} | all-to-all | bytes 3670016 | tf_op jit(solution)/shard_map/all_to_all | solution.py:120
  50.2 1.1 copy.156
  51.4 2.0 copy.157
  53.4 39.8 %all-gather.3.cloned.1.call-done = bf16[1536,1024]{1,0:T(8,128)(2,1)} async-done(((bf16[192,1024]{1,0:T(8,128)(2,1)}), bf16[1536,1024]{1,0:T(8,128)(2,1)}) %all-gather.3.cloned.1.call-update) | async-done | bytes 3145744 | tf_op jit(solution)/shard_map/all_gather | solution.py:136
  93.2 3.0 collective-permute-start
  97.9 1.2 reduce-window.11
  99.1 0.9 slice.96
  100.0 1.7 reshape.497
  101.7 1.4 copy.171
  103.1 2.0 reshape.498
  105.0 0.7 constant_dynamic-slice_fusion.1
  105.9 1.0 broadcast_in_dim.196
  107.0 6.5 %all-to-all-start.1 = ((bf16[16,208,128]{2,1,0:T(8,128)(2,1)}), bf16[16,208,128]{2,1,0:T(8,128)(2,1)S(1)}, u32[]{:S(2)}, u32[]{:S(2)}) async-start(bf16[16,208,128]{2,1,0:T(8,128)(2,1)} %broadcast_in_dim.196), calls=%async_computation.1 | async-start | bytes 1703936 | tf_op jit(solution)/shard_map/all_to_all | solution.py:129
  113.7 23.4 %all-to-all-done.1 = bf16[16,208,128]{2,1,0:T(8,128)(2,1)S(1)} async-done(((bf16[16,208,128]{2,1,0:T(8,128)(2,1)}), bf16[16,208,128]{2,1,0:T(8,128)(2,1)S(1)}, u32[]{:S(2)}, u32[]{:S(2)}) %all-to-all-start.1) | async-done | bytes 852000 | tf_op jit(solution)/shard_map/all_to_all | solution.py:129
  137.1 1.9 reshape.489
  139.0 2.5 fusion.88
  141.5 2.6 broadcast_select_fusion.2
  145.0 1.9 fusion.24
  147.7 1.8 broadcast_in_dim.201
  149.5 4.3 %all-to-all-start.2 = ((bf16[16,128,512]{1,2,0:T(8,128)(2,1)}), bf16[16,128,512]{1,2,0:T(8,128)(2,1)S(1)}, u32[]{:S(2)}, u32[]{:S(2)}) async-start(bf16[16,128,512]{1,2,0:T(8,128)(2,1)} %broadcast_in_dim.201), calls=%async_computation.2 | async-start | bytes 4194304 | tf_op jit(solution)/shard_map/all_to_all | solution.py:202
  155.3 0.8 convert_reduce_fusion.1
  157.5 2.2 compare_and_fusion
  160.1 1.2 copy.162
  161.2 1.2 subtract_convert_fusion.1
  162.7 19.5 %all-to-all-done.2 = bf16[16,128,512]{1,2,0:T(8,128)(2,1)S(1)} async-done(((bf16[16,128,512]{1,2,0:T(8,128)(2,1)}), bf16[16,128,512]{1,2,0:T(8,128)(2,1)S(1)}, u32[]{:S(2)}, u32[]{:S(2)}) %all-to-all-start.2) | async-done | bytes 2097184 | tf_op jit(solution)/shard_map/all_to_all | solution.py:202
  182.5 1.7 fusion.90
  184.3 2.2 copy.168
  186.4 6.4 %select_reduce_fusion = (f32[2,768]{1,0:T(2,128)S(1)}, f32[2,768,1664]{2,1,0:T(8,128)}) fusion(pred[768,1664]{1,0:T(8,128)(4,1)S(1)} %copy-done.4, bf16[2,768,128]{2,1,0:T(8,128)(2,1)S(1)} %bitcast.161, bf16[1664,2,128]{2,0,1:T(8,128)(2,1)} %copy.168), kind=kOutput, calls=%fused_computation.7 | convolution fusion | flops 661977600 | bytes 12752896 | tf_op jit(solution)/shard_map/hqd,hkd->hqk/dot_general | solution.py:223
  192.8 1.2 copy.169
  194.1 7.0 %fusion = f32[2,768]{1,0:T(2,128)S(1)} fusion(f32[2,768,1664]{2,1,0:T(8,128)} %get-tuple-element.25, f32[2,768]{1,0:T(2,128)S(1)} %broadcast_maximum_fusion, pred[768,1664]{1,0:T(8,128)(4,1)S(1)} %copy-done.4), kind=kLoop, calls=%fused_computation.8 | loop fusion | flops 10222080 | bytes 11513856 | tf_op jit(solution)/shard_map/reduce_sum | solution.py:229
  201.2 3.6 %fusion.44 = bf16[2,768,128]{2,1,0:T(8,128)(2,1)S(1)} fusion(f32[2,768,1664]{2,1,0:T(8,128)S(1)} %copy-done.2, f32[2,768]{1,0:T(2,128)S(1)} %broadcast_maximum_fusion, pred[768,1664]{1,0:T(8,128)(4,1)S(1)} %copy-done.4, bf16[1664,2,128]{2,0,1:T(8,128)(2,1)S(1)} %copy-done.7, f32[2,768]{1,0:T(2,128)S(1)} %fusion), kind=kOutput, calls=%fused_computation.54 | convolution fusion | flops 664928256 | bytes 12759040 | tf_op jit(solution)/shard_map/hqk,hkd->hqd/dot_general | solution.py:230
  205.1 2.2 convolution_dynamic-update-slice_fusion.1
  207.3 2.2 convolution_dynamic-update-slice_fusion
  209.5 1.6 multiply_reduce_fusion
  211.5 3.8 %gather_fusion.2 = f32[512]{0:T(512)S(1)} fusion(f32[128,32]{0,1:T(8,128)S(1)} %fusion.83, s32[512]{0:T(512)S(1)} %reshape.543), kind=kCustom, calls=%fused_computation.5 | custom fusion | bytes 8192 | tf_op jit(solution)/shard_map/jit(take_along_axis)/gather | solution.py:250
  216.1 1.3 convolution_convert_fusion
  217.4 52.0 %all_to_all.26 = bf16[16,2,40,1536]{3,2,1,0:T(8,128)(2,1)S(1)} all-to-all(bf16[16,2,40,1536]{3,2,1,0:T(8,128)(2,1)S(1)} %bitcast.145), channel_id=1, replica_groups=mesh['row'=8,'col'=16] {'col'}, dimensions={0} | all-to-all | bytes 7864320 | tf_op jit(solution)/shard_map/all_to_all | solution.py:264
  269.4 1.9 copy-done.6
  271.3 5.2 %fusion.7 = f32[2,16,40,768]{3,2,1,0:T(8,128)} fusion(bf16[2,1536,768]{2,1,0:T(8,128)(2,1)S(1)} %bitcast.169, bf16[16,2,40,1536]{3,2,1,0:T(8,128)(2,1)S(1)} %all_to_all.26), kind=kOutput, calls=%fused_computation.16 | convolution fusion | flops 3019898880 | bytes 12582912 | tf_op jit(solution)/shard_map/sjcd,jdf->sjcf/dot_general | solution.py:268
  276.4 12.6 %fusion.14 = bf16[16,2,40,1536]{3,2,0,1:T(8,128)(2,1)} fusion(bf16[2,768,1536]{2,1,0:T(8,128)(2,1)} %param.33, f32[2,16,40,768]{3,2,1,0:T(8,128)} %fusion.7, bf16[2,1536,768]{2,1,0:T(8,128)(2,1)} %param.31, bf16[16,2,40,1536]{3,2,1,0:T(8,128)(2,1)} %copy-done.6), kind=kOutput, calls=%fused_computation.22 | convolution fusion | flops 6044712960 | bytes 21233664 | tf_op jit(solution)/shard_map/sjcf,jfd->sjcd/dot_general | solution.py:272
  289.1 2.6 copy.181
  291.7 51.5 %all_to_all.27 = bf16[16,2,40,1536]{3,2,1,0:T(8,128)(2,1)S(1)} all-to-all(bf16[16,2,40,1536]{3,2,1,0:T(8,128)(2,1)S(1)} %copy.181), channel_id=1, replica_groups=mesh['row'=8,'col'=16] {'col'}, dimensions={0} | all-to-all | bytes 7864320 | tf_op jit(solution)/shard_map/all_to_all | solution.py:275
  343.9 1.6 fusion.27
  (136 shorter events, 12.9 us)
Async XLA Ops:
  6.5 5.5 %copy-start = (bf16[4,16,2048]{2,1,0:T(8,128)(2,1)S(1)}, bf16[4,16,2048]{2,1,0:T(8,128)(2,1)}, u32[]{:S(2)}) copy-start(bf16[4,16,2048]{2,1,0:T(8,128)(2,1)} %param.28) | copy-start | bytes 786436
  6.5 7.5 %copy-start.12 = (bf16[192,128]{1,0:T(8,128)(2,1)S(1)}, bf16[192,128]{1,0:T(8,128)(2,1)}, u32[]{:S(2)}) copy-start(bf16[192,128]{1,0:T(8,128)(2,1)} %param.24) | copy-start | bytes 147460
  6.5 86.7 %all-gather.3.cloned.1.call-start = ((), (), s32[]{:S(2)}) async-start(), calls=%async_computation.5 | async-start | bytes 3538944 | tf_op jit(solution)/shard_map/all_gather | solution.py:136
  12.9 2.8 copy-start.13
  16.1 80.2 %copy-start.14 = (bf16[1536]{0:T(1024)(128)(2,1)S(1)}, bf16[1536]{0:T(1024)(128)(2,1)}, u32[]{:S(2)}) copy-start(bf16[1536]{0:T(1024)(128)(2,1)} %param.22) | copy-start | bytes 9220
  16.1 81.6 %copy-start.11 = (s32[128,4]{0,1:T(4,128)S(1)}, s32[128,4]{0,1:T(4,128)}, u32[]{:S(2)}) copy-start(s32[128,4]{0,1:T(4,128)} %param.21) | copy-start | bytes 6148
  53.4 106.3 %all-gather.5.cloned.1.call-start = ((), (), s32[]{:S(2)}) async-start(), calls=%async_computation.6 | async-start | bytes 2654208 | tf_op jit(solution)/shard_map/all_gather | solution.py:136
  93.2 48.3 %collective-permute-start = (bf16[1536,1024]{1,0:T(8,128)(2,1)}, bf16[1536,1024]{1,0:T(8,128)(2,1)}, u32[]{:S(2)}, u32[]{:S(2)}) collective-permute-start(bf16[1536,1024]{1,0:T(8,128)(2,1)} %all-gather.3.cloned.1.call-done), channel_id=1, source_target_pairs={{0,1},{1,0},{2,3},{3,2},{4,5},{5,4},{6,7},{7,6},{8,9},{9,8},{10,11... | collective-permute-start | bytes 9437192 | tf_op jit(solution)/shard_map/ppermute | solution.py:137
  96.5 9.4 %copy-start.18 = (s32[4,1]{0,1:T(1,128)}, s32[4,1]{0,1:T(1,128)S(1)}, u32[]{:S(2)}) copy-start(s32[4,1]{0,1:T(1,128)S(1)} %reduce-window.10) | copy-start | bytes 52
  96.6 0.6 copy-start.17
  96.7 17.0 %copy-start.19 = (s32[128]{0:T(128)}, s32[128]{0:T(128)S(1)}, u32[]{:S(2)}) copy-start(s32[128]{0:T(128)S(1)} %convert_reduce_fusion.2) | copy-start | bytes 1540
  97.5 9.5 %copy-start.8 = (f32[128,64]{0,1:T(8,128)}, f32[128,64]{0,1:T(8,128)S(1)}, u32[]{:S(2)}) copy-start(f32[128,64]{0,1:T(8,128)S(1)} %get-tuple-element.18) | copy-start | bytes 98308
  97.5 9.5 %copy-start.9 = (f32[128,64]{0,1:T(8,128)}, f32[128,64]{0,1:T(8,128)S(1)}, u32[]{:S(2)}) copy-start(f32[128,64]{0,1:T(8,128)S(1)} %get-tuple-element.19) | copy-start | bytes 98308
  101.7 11.8 %copy-start.3 = (bf16[128,1536]{1,0:T(8,128)(2,1)S(1)}, bf16[128,1536]{1,0:T(8,128)(2,1)}, u32[]{:S(2)}) copy-start(bf16[128,1536]{1,0:T(8,128)(2,1)} %param.18) | copy-start | bytes 1179652
  107.0 30.2 %all-to-all-start.1 = ((bf16[16,208,128]{2,1,0:T(8,128)(2,1)}), bf16[16,208,128]{2,1,0:T(8,128)(2,1)S(1)}, u32[]{:S(2)}, u32[]{:S(2)}) async-start(bf16[16,208,128]{2,1,0:T(8,128)(2,1)} %broadcast_in_dim.196), calls=%async_computation.1 | async-start | bytes 1703936 | tf_op jit(solution)/shard_map/all_to_all | solution.py:129
  113.7 31.3 %copy-start.15 = (pred[128,4]{0,1:T(4,128)(4,1)}, pred[128,4]{0,1:T(4,128)(4,1)S(1)}, u32[]{:S(2)}) copy-start(pred[128,4]{0,1:T(4,128)(4,1)S(1)} %iota_compare_fusion.3) | copy-start | bytes 1540
  146.9 2.5 copy-start.5
  149.5 32.7 %all-to-all-start.2 = ((bf16[16,128,512]{1,2,0:T(8,128)(2,1)}), bf16[16,128,512]{1,2,0:T(8,128)(2,1)S(1)}, u32[]{:S(2)}, u32[]{:S(2)}) async-start(bf16[16,128,512]{1,2,0:T(8,128)(2,1)} %broadcast_in_dim.201), calls=%async_computation.2 | async-start | bytes 4194304 | tf_op jit(solution)/shard_map/all_to_all | solution.py:202
  153.8 6.3 %slice-start = ((f32[128,2048]{1,0:T(8,128)}), f32[128,1536]{1,0:T(8,128)S(1)}, s32[]{:S(2)}) async-start(f32[128,2048]{1,0:T(8,128)} %copy-done.5), calls=%async_computation.7 | async-start | bytes 1572864 | tf_op jit(solution)/shard_map/slice | solution.py:183
  159.7 47.7 %collective-permute-start.1 = (bf16[1536,768]{1,0:T(8,128)(2,1)}, bf16[1536,768]{1,0:T(8,128)(2,1)}, u32[]{:S(2)}, u32[]{:S(2)}) collective-permute-start(bf16[1536,768]{1,0:T(8,128)(2,1)} %all-gather.5.cloned.1.call-done), channel_id=1, source_target_pairs={{0,1},{1,0},{2,3},{3,2},{4,5},{5,4},{6,7},{7,6},{8,9},{9,8},{10,11... | collective-permute-start | bytes 7077896 | tf_op jit(solution)/shard_map/ppermute | solution.py:137
  182.5 3.9 %copy-start.4 = (pred[768,1664]{1,0:T(8,128)(4,1)S(1)}, pred[768,1664]{1,0:T(8,128)(4,1)}, u32[]{:S(2)}) copy-start(pred[768,1664]{1,0:T(8,128)(4,1)} %compare_and_fusion) | copy-start | bytes 3833860
  194.1 7.0 %copy-start.2 = (f32[2,768,1664]{2,1,0:T(8,128)S(1)}, f32[2,768,1664]{2,1,0:T(8,128)}, u32[]{:S(2)}) copy-start(f32[2,768,1664]{2,1,0:T(8,128)} %get-tuple-element.25) | copy-start | bytes 30670852
  194.1 7.1 %copy-start.7 = (bf16[1664,2,128]{2,0,1:T(8,128)(2,1)S(1)}, bf16[1664,2,128]{2,0,1:T(8,128)(2,1)}, u32[]{:S(2)}) copy-start(bf16[1664,2,128]{2,0,1:T(8,128)(2,1)} %copy.169) | copy-start | bytes 2555908
  204.8 4.7 %copy-start.16 = (pred[128,4]{0,1:T(4,128)(4,1)S(1)}, pred[128,4]{0,1:T(4,128)(4,1)}, u32[]{:S(2)}) copy-start(pred[128,4]{0,1:T(4,128)(4,1)} %copy-done.15) | copy-start | bytes 1540
  205.1 6.1 %copy-start.10 = (bf16[1536,32]{0,1:T(8,128)(2,1)S(1)}, bf16[1536,32]{0,1:T(8,128)(2,1)}, u32[]{:S(2)}) copy-start(bf16[1536,32]{0,1:T(8,128)(2,1)} %param.26) | copy-start | bytes 294916
  216.1 55.2 %slice-start.1 = ((s8[4718592]{0:T(1024)(128)(4,1)}), s8[4194304]{0:T(1024)(128)(4,1)S(1)}, s32[]{:S(2)}) async-start(s8[4718592]{0:T(1024)(128)(4,1)} %bitcast.168), calls=%async_computation.8 | async-start | bytes 8388608
  217.4 53.9 %slice-start.2 = ((s8[4718592]{0:T(1024)(128)(4,1)}), s8[524288]{0:T(1024)(128)(4,1)S(1)}, s32[]{:S(2)}) async-start(s8[4718592]{0:T(1024)(128)(4,1)} %bitcast.168), calls=%async_computation.9 | async-start | bytes 1048576
  269.4 1.9 copy-start.6
  343.1 2.3 copy-start.1
Sparse Core Ops, SparseCore 0:
  53.5 39.6 all-gather.2
  105.9 42.7 all-gather.4

commit v12 on v11

--- a/solution.py
+++ b/solution.py
@@ -262,16 +262,18 @@
     ).astype(jnp.bfloat16)
     sending = dispatch_rows.reshape(columns, local_experts, CAP, model_width)
     arrived = lax.all_to_all(sending, "col", split_axis=0, concat_axis=0, tiled=True)
+    expert_rows = arrived.transpose(1, 0, 2, 3).reshape(local_experts, columns * CAP, model_width)
     gate_vals = jnp.einsum(
-        "sjcd,jdf->sjcf", arrived, expert_gate_weight, preferred_element_type=jnp.float32
+        "jnd,jdf->jnf", expert_rows, expert_gate_weight, preferred_element_type=jnp.float32
     )
     up_vals = jnp.einsum(
-        "sjcd,jdf->sjcf", arrived, expert_up_weight, preferred_element_type=jnp.float32
+        "jnd,jdf->jnf", expert_rows, expert_up_weight, preferred_element_type=jnp.float32
     )
     hidden_vals = (jnp.maximum(gate_vals, 0.0) * up_vals).astype(jnp.bfloat16)
     answered = jnp.einsum(
-        "sjcf,jfd->sjcd", hidden_vals, expert_down_weight, preferred_element_type=jnp.float32
+        "jnf,jfd->jnd", hidden_vals, expert_down_weight, preferred_element_type=jnp.float32
     ).astype(jnp.bfloat16)
+    answered = answered.reshape(local_experts, columns, CAP, model_width).transpose(1, 0, 2, 3)
     returned = lax.all_to_all(answered, "col", split_axis=0, concat_axis=0, tiled=True)
     returned_rows = returned.reshape(slot_total, model_width)
     mix_matrix = jnp.sum(jnp.where(matches, mixing[:, :, None], 0.0), axis=1)

time: 353 us -> 353 us (level)
  no operation moved by 1% of the time
where the time goes in v12:
time: 353 us
  blocking collectives  137 us (39%)
  waiting for transfers between devices  82.7 us (23%)
  matrix products  44.4 us (13%)
  local copies, waits for them, and re-layouts  43.5 us (12%)
  other arithmetic  16 us (5%)
  starting transfers between devices  14.3 us (4%)
  between operations  14.2 us (4%)
    all_to_all x1, blocking collectives, local(): lax.all_to_all(sending, 'col', split_axis=0, concat_axis=0, tiled=True)  52.1 us
    all_to_all x1, blocking collectives, local(): lax.all_to_all(answered, 'col', split_axis=0, concat_axis=0, tiled=True)  51.5 us
    all_gather x2, waiting for transfers between devices, gather_halves(): own = lax.all_gather(slab, 'row', axis=0, tiled=True)  39.8 us
    all_to_all x1, blocking collectives, local(): bundle = lax.all_to_all(bundle, 'col', 0, 0, tiled=True)  33.8 us
    all_to_all x1, waiting for transfers between devices, local(): lax.all_to_all(jnp.broadcast_to(reduced[None], (columns,) + reduced.shape...  23.4 us
    all_to_all x1, waiting for transfers between devices, local(): lax.all_to_all(jnp.broadcast_to(key_value_piece[None], (columns,) + key_v...  19.5 us
    dot_general x1, matrix products, local(): jnp.einsum('jnf,jfd->jnd', hidden_vals, expert_down_weight, preferred_ele...  12.5 us
  transfers between devices with their start and end apart: 6, of which 3 were waited for; matrix products, arithmetic and copies ran while one was open for 16% of the time, Pallas kernels for 0%

profile of v12, /device:TPU:1, one launch (start us, length us, event | category | flops | bytes accessed | tf_op | source)
XLA Modules:
  0.0 352.5 jit_solution(5770353323086013008)
XLA Ops:
  6.6 0.9 dynamic-slice_reduce_fusion
  7.5 1.5 gather_fusion.3
  9.0 1.5 gather_fusion.4
  10.5 1.5 gather_fusion.5
  12.9 1.1 reshape.489
  16.1 33.8 %all_to_all.25 = bf16[16,448,128]{2,1,0:T(8,128)(2,1)S(1)} all-to-all(bf16[16,448,128]{2,1,0:T(8,128)(2,1)S(1)} %pad_maximum_fusion), channel_id=1, replica_groups=mesh['row'=8,'col'=16] {'col'}, dimensions={0} | all-to-all | bytes 3670016 | tf_op jit(solution)/shard_map/all_to_all | solution.py:120
  50.2 1.1 copy.155
  51.4 2.0 copy.156
  53.4 39.8 %all-gather.3.cloned.1.call-done = bf16[1536,1024]{1,0:T(8,128)(2,1)} async-done(((bf16[192,1024]{1,0:T(8,128)(2,1)}), bf16[1536,1024]{1,0:T(8,128)(2,1)}) %all-gather.3.cloned.1.call-update) | async-done | bytes 3145744 | tf_op jit(solution)/shard_map/all_gather | solution.py:136
  93.2 3.0 collective-permute-start
  97.9 1.2 reduce-window.11
  99.1 0.9 slice.96
  100.0 1.7 reshape.503
  101.7 1.4 copy.170
  103.1 2.0 reshape.504
  105.0 0.7 constant_dynamic-slice_fusion.1
  105.9 1.0 broadcast_in_dim.196
  107.0 6.5 %all-to-all-start.1 = ((bf16[16,208,128]{2,1,0:T(8,128)(2,1)}), bf16[16,208,128]{2,1,0:T(8,128)(2,1)S(1)}, u32[]{:S(2)}, u32[]{:S(2)}) async-start(bf16[16,208,128]{2,1,0:T(8,128)(2,1)} %broadcast_in_dim.196), calls=%async_computation.1 | async-start | bytes 1703936 | tf_op jit(solution)/shard_map/all_to_all | solution.py:129
  113.7 23.4 %all-to-all-done.1 = bf16[16,208,128]{2,1,0:T(8,128)(2,1)S(1)} async-done(((bf16[16,208,128]{2,1,0:T(8,128)(2,1)}), bf16[16,208,128]{2,1,0:T(8,128)(2,1)S(1)}, u32[]{:S(2)}, u32[]{:S(2)}) %all-to-all-start.1) | async-done | bytes 852000 | tf_op jit(solution)/shard_map/all_to_all | solution.py:129
  137.1 1.9 reshape.495
  139.0 2.5 fusion.63
  141.5 2.6 broadcast_select_fusion.2
  145.0 1.9 fusion.10
  147.7 1.8 broadcast_in_dim.201
  149.5 4.3 %all-to-all-start.2 = ((bf16[16,128,512]{1,2,0:T(8,128)(2,1)}), bf16[16,128,512]{1,2,0:T(8,128)(2,1)S(1)}, u32[]{:S(2)}, u32[]{:S(2)}) async-start(bf16[16,128,512]{1,2,0:T(8,128)(2,1)} %broadcast_in_dim.201), calls=%async_computation.2 | async-start | bytes 4194304 | tf_op jit(solution)/shard_map/all_to_all | solution.py:202
  155.3 0.8 convert_reduce_fusion.1
  157.5 2.2 compare_and_fusion
  160.1 1.2 copy.161
  161.2 1.2 subtract_convert_fusion.1
  162.7 19.5 %all-to-all-done.2 = bf16[16,128,512]{1,2,0:T(8,128)(2,1)S(1)} async-done(((bf16[16,128,512]{1,2,0:T(8,128)(2,1)}), bf16[16,128,512]{1,2,0:T(8,128)(2,1)S(1)}, u32[]{:S(2)}, u32[]{:S(2)}) %all-to-all-start.2) | async-done | bytes 2097184 | tf_op jit(solution)/shard_map/all_to_all | solution.py:202
  182.5 1.7 fusion.65
  184.3 2.2 copy.167
  186.4 6.4 %select_reduce_fusion = (f32[2,768]{1,0:T(2,128)S(1)}, f32[2,768,1664]{2,1,0:T(8,128)}) fusion(pred[768,1664]{1,0:T(8,128)(4,1)S(1)} %copy-done.4, bf16[2,768,128]{2,1,0:T(8,128)(2,1)S(1)} %bitcast.149, bf16[1664,2,128]{2,0,1:T(8,128)(2,1)} %copy.167), kind=kOutput, calls=%fused_computation.7 | convolution fusion | flops 661977600 | bytes 12752896 | tf_op jit(solution)/shard_map/hqd,hkd->hqk/dot_general | solution.py:223
  192.8 1.2 copy.168
  194.1 7.0 %fusion = f32[2,768]{1,0:T(2,128)S(1)} fusion(f32[2,768,1664]{2,1,0:T(8,128)} %get-tuple-element.25, f32[2,768]{1,0:T(2,128)S(1)} %broadcast_maximum_fusion, pred[768,1664]{1,0:T(8,128)(4,1)S(1)} %copy-done.4), kind=kLoop, calls=%fused_computation.8 | loop fusion | flops 10222080 | bytes 11513856 | tf_op jit(solution)/shard_map/reduce_sum | solution.py:229
  201.2 3.6 %fusion.19 = bf16[2,768,128]{2,1,0:T(8,128)(2,1)S(1)} fusion(f32[2,768,1664]{2,1,0:T(8,128)S(1)} %copy-done.2, f32[2,768]{1,0:T(2,128)S(1)} %broadcast_maximum_fusion, pred[768,1664]{1,0:T(8,128)(4,1)S(1)} %copy-done.4, bf16[1664,2,128]{2,0,1:T(8,128)(2,1)S(1)} %copy-done.7, f32[2,768]{1,0:T(2,128)S(1)} %fusion), kind=kOutput, calls=%fused_computation.44 | convolution fusion | flops 664928256 | bytes 12759040 | tf_op jit(solution)/shard_map/hqk,hkd->hqd/dot_general | solution.py:230
  205.1 2.2 convolution_dynamic-update-slice_fusion.1
  207.3 2.2 convolution_dynamic-update-slice_fusion
  209.5 1.6 multiply_reduce_fusion
  211.5 3.8 %gather_fusion.2 = f32[512]{0:T(512)S(1)} fusion(f32[128,32]{0,1:T(8,128)S(1)} %fusion.58, s32[512]{0:T(512)S(1)} %reshape.551), kind=kCustom, calls=%fused_computation.5 | custom fusion | bytes 8192 | tf_op jit(solution)/shard_map/jit(take_along_axis)/gather | solution.py:250
  216.1 1.3 convolution_convert_fusion
  217.4 52.1 %all_to_all.26 = bf16[16,2,40,1536]{3,2,1,0:T(8,128)(2,1)S(1)} all-to-all(bf16[16,2,40,1536]{3,2,1,0:T(8,128)(2,1)S(1)} %bitcast.129), channel_id=1, replica_groups=mesh['row'=8,'col'=16] {'col'}, dimensions={0} | all-to-all | bytes 7864320 | tf_op jit(solution)/shard_map/all_to_all | solution.py:264
  269.8 1.9 copy-done.6
  271.7 5.1 %fusion.68 = f32[2,640,768]{2,1,0:T(8,128)} fusion(bf16[2,640,1536]{2,1,0:T(8,128)(2,1)S(1)} %bitcast.136, bf16[2,1536,768]{2,1,0:T(8,128)(2,1)S(1)} %bitcast.157), kind=kOutput, calls=%fused_computation.153 | convolution fusion | flops 3019898880 | bytes 12582912 | tf_op jit(solution)/shard_map/jnd,jdf->jnf/dot_general | solution.py:266
  276.8 12.5 %convolution_convert_fusion.1 = bf16[2,640,1536]{2,1,0:T(8,128)(2,1)} fusion(bf16[2,768,1536]{2,1,0:T(8,128)(2,1)} %param.33, f32[2,640,768]{2,1,0:T(8,128)} %fusion.68, bf16[2,640,1536]{2,1,0:T(8,128)(2,1)} %bitcast.137, bf16[2,1536,768]{2,1,0:T(8,128)(2,1)} %param.32), kind=kOutput, calls=%fused_computation.14 | convolution fusion | flops 6044712960 | bytes 21233664 | tf_op jit(solution)/shard_map/jnf,jfd->jnd/dot_general | solution.py:273
  289.3 2.6 copy.190
  291.9 51.5 %all_to_all.27 = bf16[16,2,40,1536]{3,2,1,0:T(8,128)(2,1)S(1)} all-to-all(bf16[16,2,40,1536]{3,2,1,0:T(8,128)(2,1)S(1)} %bitcast.130), channel_id=1, replica_groups=mesh['row'=8,'col'=16] {'col'}, dimensions={0} | all-to-all | bytes 7864320 | tf_op jit(solution)/shard_map/all_to_all | solution.py:277
  344.1 1.6 fusion.13
  (137 shorter events, 13.2 us)
Async XLA Ops:
  6.5 5.5 %copy-start = (bf16[4,16,2048]{2,1,0:T(8,128)(2,1)S(1)}, bf16[4,16,2048]{2,1,0:T(8,128)(2,1)}, u32[]{:S(2)}) copy-start(bf16[4,16,2048]{2,1,0:T(8,128)(2,1)} %param.28) | copy-start | bytes 786436
  6.5 7.5 %copy-start.12 = (bf16[192,128]{1,0:T(8,128)(2,1)S(1)}, bf16[192,128]{1,0:T(8,128)(2,1)}, u32[]{:S(2)}) copy-start(bf16[192,128]{1,0:T(8,128)(2,1)} %param.24) | copy-start | bytes 147460
  6.5 86.7 %all-gather.3.cloned.1.call-start = ((), (), s32[]{:S(2)}) async-start(), calls=%async_computation.5 | async-start | bytes 3538944 | tf_op jit(solution)/shard_map/all_gather | solution.py:136
  12.9 2.8 copy-start.13
  16.1 80.2 %copy-start.14 = (bf16[1536]{0:T(1024)(128)(2,1)S(1)}, bf16[1536]{0:T(1024)(128)(2,1)}, u32[]{:S(2)}) copy-start(bf16[1536]{0:T(1024)(128)(2,1)} %param.22) | copy-start | bytes 9220
  16.1 81.6 %copy-start.11 = (s32[128,4]{0,1:T(4,128)S(1)}, s32[128,4]{0,1:T(4,128)}, u32[]{:S(2)}) copy-start(s32[128,4]{0,1:T(4,128)} %param.21) | copy-start | bytes 6148
  53.4 106.3 %all-gather.5.cloned.1.call-start = ((), (), s32[]{:S(2)}) async-start(), calls=%async_computation.6 | async-start | bytes 2654208 | tf_op jit(solution)/shard_map/all_gather | solution.py:136
  93.2 48.3 %collective-permute-start = (bf16[1536,1024]{1,0:T(8,128)(2,1)}, bf16[1536,1024]{1,0:T(8,128)(2,1)}, u32[]{:S(2)}, u32[]{:S(2)}) collective-permute-start(bf16[1536,1024]{1,0:T(8,128)(2,1)} %all-gather.3.cloned.1.call-done), channel_id=1, source_target_pairs={{0,1},{1,0},{2,3},{3,2},{4,5},{5,4},{6,7},{7,6},{8,9},{9,8},{10,11... | collective-permute-start | bytes 9437192 | tf_op jit(solution)/shard_map/ppermute | solution.py:137
  96.5 9.4 %copy-start.18 = (s32[4,1]{0,1:T(1,128)}, s32[4,1]{0,1:T(1,128)S(1)}, u32[]{:S(2)}) copy-start(s32[4,1]{0,1:T(1,128)S(1)} %reduce-window.10) | copy-start | bytes 52
  96.6 0.6 copy-start.17
  96.7 17.0 %copy-start.19 = (s32[128]{0:T(128)}, s32[128]{0:T(128)S(1)}, u32[]{:S(2)}) copy-start(s32[128]{0:T(128)S(1)} %convert_reduce_fusion.2) | copy-start | bytes 1540
  97.5 9.5 %copy-start.8 = (f32[128,64]{0,1:T(8,128)}, f32[128,64]{0,1:T(8,128)S(1)}, u32[]{:S(2)}) copy-start(f32[128,64]{0,1:T(8,128)S(1)} %get-tuple-element.18) | copy-start | bytes 98308
  97.5 9.5 %copy-start.9 = (f32[128,64]{0,1:T(8,128)}, f32[128,64]{0,1:T(8,128)S(1)}, u32[]{:S(2)}) copy-start(f32[128,64]{0,1:T(8,128)S(1)} %get-tuple-element.19) | copy-start | bytes 98308
  101.7 11.8 %copy-start.3 = (bf16[128,1536]{1,0:T(8,128)(2,1)S(1)}, bf16[128,1536]{1,0:T(8,128)(2,1)}, u32[]{:S(2)}) copy-start(bf16[128,1536]{1,0:T(8,128)(2,1)} %param.18) | copy-start | bytes 1179652
  107.0 30.2 %all-to-all-start.1 = ((bf16[16,208,128]{2,1,0:T(8,128)(2,1)}), bf16[16,208,128]{2,1,0:T(8,128)(2,1)S(1)}, u32[]{:S(2)}, u32[]{:S(2)}) async-start(bf16[16,208,128]{2,1,0:T(8,128)(2,1)} %broadcast_in_dim.196), calls=%async_computation.1 | async-start | bytes 1703936 | tf_op jit(solution)/shard_map/all_to_all | solution.py:129
  113.7 31.3 %copy-start.15 = (pred[128,4]{0,1:T(4,128)(4,1)}, pred[128,4]{0,1:T(4,128)(4,1)S(1)}, u32[]{:S(2)}) copy-start(pred[128,4]{0,1:T(4,128)(4,1)S(1)} %iota_compare_fusion.3) | copy-start | bytes 1540
  146.9 2.5 copy-start.5
  149.5 32.7 %all-to-all-start.2 = ((bf16[16,128,512]{1,2,0:T(8,128)(2,1)}), bf16[16,128,512]{1,2,0:T(8,128)(2,1)S(1)}, u32[]{:S(2)}, u32[]{:S(2)}) async-start(bf16[16,128,512]{1,2,0:T(8,128)(2,1)} %broadcast_in_dim.201), calls=%async_computation.2 | async-start | bytes 4194304 | tf_op jit(solution)/shard_map/all_to_all | solution.py:202
  153.8 6.3 %slice-start = ((f32[128,2048]{1,0:T(8,128)}), f32[128,1536]{1,0:T(8,128)S(1)}, s32[]{:S(2)}) async-start(f32[128,2048]{1,0:T(8,128)} %copy-done.5), calls=%async_computation.7 | async-start | bytes 1572864 | tf_op jit(solution)/shard_map/slice | solution.py:183
  159.7 47.7 %collective-permute-start.1 = (bf16[1536,768]{1,0:T(8,128)(2,1)}, bf16[1536,768]{1,0:T(8,128)(2,1)}, u32[]{:S(2)}, u32[]{:S(2)}) collective-permute-start(bf16[1536,768]{1,0:T(8,128)(2,1)} %all-gather.5.cloned.1.call-done), channel_id=1, source_target_pairs={{0,1},{1,0},{2,3},{3,2},{4,5},{5,4},{6,7},{7,6},{8,9},{9,8},{10,11... | collective-permute-start | bytes 7077896 | tf_op jit(solution)/shard_map/ppermute | solution.py:137
  182.5 3.9 %copy-start.4 = (pred[768,1664]{1,0:T(8,128)(4,1)S(1)}, pred[768,1664]{1,0:T(8,128)(4,1)}, u32[]{:S(2)}) copy-start(pred[768,1664]{1,0:T(8,128)(4,1)} %compare_and_fusion) | copy-start | bytes 3833860
  194.1 7.0 %copy-start.2 = (f32[2,768,1664]{2,1,0:T(8,128)S(1)}, f32[2,768,1664]{2,1,0:T(8,128)}, u32[]{:S(2)}) copy-start(f32[2,768,1664]{2,1,0:T(8,128)} %get-tuple-element.25) | copy-start | bytes 30670852
  194.1 7.1 %copy-start.7 = (bf16[1664,2,128]{2,0,1:T(8,128)(2,1)S(1)}, bf16[1664,2,128]{2,0,1:T(8,128)(2,1)}, u32[]{:S(2)}) copy-start(bf16[1664,2,128]{2,0,1:T(8,128)(2,1)} %copy.168) | copy-start | bytes 2555908
  204.8 4.7 %copy-start.16 = (pred[128,4]{0,1:T(4,128)(4,1)S(1)}, pred[128,4]{0,1:T(4,128)(4,1)}, u32[]{:S(2)}) copy-start(pred[128,4]{0,1:T(4,128)(4,1)} %copy-done.15) | copy-start | bytes 1540
  205.1 6.1 %copy-start.10 = (bf16[1536,32]{0,1:T(8,128)(2,1)S(1)}, bf16[1536,32]{0,1:T(8,128)(2,1)}, u32[]{:S(2)}) copy-start(bf16[1536,32]{0,1:T(8,128)(2,1)} %param.26) | copy-start | bytes 294916
  217.4 54.3 %slice-start.1 = ((s8[4718592]{0:T(1024)(128)(4,1)}), s8[4194304]{0:T(1024)(128)(4,1)S(1)}, s32[]{:S(2)}) async-start(s8[4718592]{0:T(1024)(128)(4,1)} %bitcast.156), calls=%async_computation.8 | async-start | bytes 8388608
  269.5 2.2 slice-start.2
  269.8 1.9 copy-start.6
  343.4 2.3 copy-start.1
Sparse Core Ops, SparseCore 0:
  53.5 39.6 all-gather.2
  105.9 42.7 all-gather.4

commit v13 on v11

--- a/solution.py
+++ b/solution.py
@@ -247,7 +247,9 @@
     residual = (hidden_input.astype(jnp.float32) + projected_rows).astype(jnp.bfloat16)
     normed_two = rms_scaled(residual, expert_norm_gain)
     logits = jnp.dot(normed_two, router, preferred_element_type=jnp.float32)
-    squashed = jax.nn.sigmoid(jnp.take_along_axis(logits, routes, axis=1))
+    route_hits = routes[:, :, None] == jnp.arange(logits.shape[1], dtype=jnp.int32)[None, None, :]
+    picked_logits = jnp.sum(jnp.where(route_hits, logits[:, None, :], 0.0), axis=2)
+    squashed = jax.nn.sigmoid(picked_logits)
     mixing = squashed / jnp.sum(squashed, axis=1, keepdims=True)
     expert_total = router.shape[1]
     local_experts = expert_gate_weight.shape[0]

time: 353 us -> 348 us (0.986)
  local copies, waits for them, and re-layouts: 43.3 us -> 39.5 us
    gather x5 -> x0, local copies, waits for them, and re-layouts: 4.15 us -> none  [local(): squashed = jax.nn.sigmoid(jnp.take_along_axis(logits, routes, axis=1))]
where the time goes in v13:
time: 348 us; the launch traced here: 347 us
  blocking collectives  137 us (39%)
  waiting for transfers between devices  82.5 us (24%)
  matrix products  44.6 us (13%)
  local copies, waits for them, and re-layouts  39.5 us (11%)
  starting transfers between devices  14.3 us (4%)
  other arithmetic  14.3 us (4%)
  between operations  14.1 us (4%)
    all_to_all x1, blocking collectives, local(): lax.all_to_all(sending, 'col', split_axis=0, concat_axis=0, tiled=True)  52 us
    all_to_all x1, blocking collectives, local(): lax.all_to_all(answered, 'col', split_axis=0, concat_axis=0, tiled=True)  51.5 us
    all_gather x2, waiting for transfers between devices, gather_halves(): own = lax.all_gather(slab, 'row', axis=0, tiled=True)  39.8 us
    all_to_all x1, blocking collectives, local(): bundle = lax.all_to_all(bundle, 'col', 0, 0, tiled=True)  33.8 us
    all_to_all x1, waiting for transfers between devices, local(): lax.all_to_all(jnp.broadcast_to(reduced[None], (columns,) + reduced.shape...  22.3 us
    all_to_all x1, waiting for transfers between devices, local(): lax.all_to_all(jnp.broadcast_to(key_value_piece[None], (columns,) + key_v...  20.4 us
    dot_general x1, matrix products, local(): jnp.einsum('sjcf,jfd->sjcd', hidden_vals, expert_down_weight, preferred_e...  12.6 us
    reduce_sum x1, other arithmetic, local(): running_new = jnp.sum(weights, axis=-1)  7 us
  transfers between devices with their start and end apart: 6, of which 3 were waited for; matrix products, arithmetic and copies ran while one was open for 16% of the time, Pallas kernels for 0%

profile of v13, /device:TPU:1, one launch (start us, length us, event | category | flops | bytes accessed | tf_op | source)
XLA Modules:
  0.0 346.7 jit_solution(18121547654360179314)
XLA Ops:
  6.6 0.9 dynamic-slice_reduce_fusion
  7.5 1.5 gather_fusion.2
  9.0 1.5 gather_fusion.3
  10.5 1.5 gather_fusion.4
  12.9 1.1 reshape.483
  16.1 33.8 %all_to_all.25 = bf16[16,448,128]{2,1,0:T(8,128)(2,1)S(1)} all-to-all(bf16[16,448,128]{2,1,0:T(8,128)(2,1)S(1)} %pad_maximum_fusion), channel_id=1, replica_groups=mesh['row'=8,'col'=16] {'col'}, dimensions={0} | all-to-all | bytes 3670016 | tf_op jit(solution)/shard_map/all_to_all | solution.py:120
  50.2 1.1 copy.138
  51.4 2.0 copy.139
  53.4 39.8 %all-gather.3.cloned.1.call-done = bf16[1536,1024]{1,0:T(8,128)(2,1)} async-done(((bf16[192,1024]{1,0:T(8,128)(2,1)}), bf16[1536,1024]{1,0:T(8,128)(2,1)}) %all-gather.3.cloned.1.call-update) | async-done | bytes 3145744 | tf_op jit(solution)/shard_map/all_gather | solution.py:136
  93.2 3.0 collective-permute-start
  97.4 0.9 slice.94
  98.3 1.7 reshape.497
  100.0 1.4 copy.153
  101.4 2.0 reshape.498
  103.4 0.7 constant_dynamic-slice_fusion.1
  104.2 1.0 broadcast_in_dim.207
  105.3 6.5 %all-to-all-start.1 = ((bf16[16,208,128]{2,1,0:T(8,128)(2,1)}), bf16[16,208,128]{2,1,0:T(8,128)(2,1)S(1)}, u32[]{:S(2)}, u32[]{:S(2)}) async-start(bf16[16,208,128]{2,1,0:T(8,128)(2,1)} %broadcast_in_dim.207), calls=%async_computation.1 | async-start | bytes 1703936 | tf_op jit(solution)/shard_map/all_to_all | solution.py:129
  111.8 1.2 reduce-window.11
  113.2 22.3 %all-to-all-done.1 = bf16[16,208,128]{2,1,0:T(8,128)(2,1)S(1)} async-done(((bf16[16,208,128]{2,1,0:T(8,128)(2,1)}), bf16[16,208,128]{2,1,0:T(8,128)(2,1)S(1)}, u32[]{:S(2)}, u32[]{:S(2)}) %all-to-all-start.1) | async-done | bytes 852000 | tf_op jit(solution)/shard_map/all_to_all | solution.py:129
  135.4 1.9 reshape.489
  137.3 2.5 fusion.88
  139.8 2.6 broadcast_select_fusion.2
  143.3 1.9 fusion.24
  146.0 1.8 broadcast_in_dim.212
  147.8 4.3 %all-to-all-start.2 = ((bf16[16,128,512]{1,2,0:T(8,128)(2,1)}), bf16[16,128,512]{1,2,0:T(8,128)(2,1)S(1)}, u32[]{:S(2)}, u32[]{:S(2)}) async-start(bf16[16,128,512]{1,2,0:T(8,128)(2,1)} %broadcast_in_dim.212), calls=%async_computation.2 | async-start | bytes 4194304 | tf_op jit(solution)/shard_map/all_to_all | solution.py:202
  152.9 2.2 compare_and_fusion
  155.5 2.1 slice.87
  157.6 1.4 copy.144
  159.0 0.9 subtract_convert_fusion.1
  160.2 20.4 %all-to-all-done.2 = bf16[16,128,512]{1,2,0:T(8,128)(2,1)S(1)} async-done(((bf16[16,128,512]{1,2,0:T(8,128)(2,1)}), bf16[16,128,512]{1,2,0:T(8,128)(2,1)S(1)}, u32[]{:S(2)}, u32[]{:S(2)}) %all-to-all-start.2) | async-done | bytes 2097184 | tf_op jit(solution)/shard_map/all_to_all | solution.py:202
  180.8 1.7 fusion.90
  182.6 2.2 copy.150
  184.8 6.4 %select_reduce_fusion = (f32[2,768]{1,0:T(2,128)S(1)}, f32[2,768,1664]{2,1,0:T(8,128)}) fusion(pred[768,1664]{1,0:T(8,128)(4,1)S(1)} %copy-done.4, bf16[2,768,128]{2,1,0:T(8,128)(2,1)S(1)} %bitcast.157, bf16[1664,2,128]{2,0,1:T(8,128)(2,1)} %copy.150), kind=kOutput, calls=%fused_computation.6 | convolution fusion | flops 661977600 | bytes 12752896 | tf_op jit(solution)/shard_map/hqd,hkd->hqk/dot_general | solution.py:223
  191.2 1.2 copy.151
  192.4 7.0 %fusion = f32[2,768]{1,0:T(2,128)S(1)} fusion(f32[2,768,1664]{2,1,0:T(8,128)} %get-tuple-element.25, f32[2,768]{1,0:T(2,128)S(1)} %broadcast_maximum_fusion, pred[768,1664]{1,0:T(8,128)(4,1)S(1)} %copy-done.4), kind=kLoop, calls=%fused_computation.7 | loop fusion | flops 10222080 | bytes 11513856 | tf_op jit(solution)/shard_map/reduce_sum | solution.py:229
  199.5 3.6 %fusion.44 = bf16[2,768,128]{2,1,0:T(8,128)(2,1)S(1)} fusion(f32[2,768,1664]{2,1,0:T(8,128)S(1)} %copy-done.2, f32[2,768]{1,0:T(2,128)S(1)} %broadcast_maximum_fusion, pred[768,1664]{1,0:T(8,128)(4,1)S(1)} %copy-done.4, bf16[1664,2,128]{2,0,1:T(8,128)(2,1)S(1)} %copy-done.7, f32[2,768]{1,0:T(2,128)S(1)} %fusion), kind=kOutput, calls=%fused_computation.53 | convolution fusion | flops 664928256 | bytes 12759040 | tf_op jit(solution)/shard_map/hqk,hkd->hqd/dot_general | solution.py:230
  203.4 2.2 convolution_dynamic-update-slice_fusion.1
  205.6 2.2 convolution_dynamic-update-slice_fusion
  207.8 1.6 multiply_reduce_fusion
  210.5 1.3 convolution_convert_fusion
  211.8 52.0 %all_to_all.26 = bf16[16,2,40,1536]{3,2,1,0:T(8,128)(2,1)S(1)} all-to-all(bf16[16,2,40,1536]{3,2,1,0:T(8,128)(2,1)S(1)} %bitcast.141), channel_id=1, replica_groups=mesh['row'=8,'col'=16] {'col'}, dimensions={0} | all-to-all | bytes 7864320 | tf_op jit(solution)/shard_map/all_to_all | solution.py:266
  263.8 1.9 copy-done.6
  265.7 5.2 %fusion.7 = f32[2,16,40,768]{3,2,1,0:T(8,128)} fusion(bf16[2,1536,768]{2,1,0:T(8,128)(2,1)S(1)} %bitcast.165, bf16[16,2,40,1536]{3,2,1,0:T(8,128)(2,1)S(1)} %all_to_all.26), kind=kOutput, calls=%fused_computation.15 | convolution fusion | flops 3019898880 | bytes 12582912 | tf_op jit(solution)/shard_map/sjcd,jdf->sjcf/dot_general | solution.py:270
  270.8 12.6 %fusion.14 = bf16[16,2,40,1536]{3,2,0,1:T(8,128)(2,1)} fusion(bf16[2,768,1536]{2,1,0:T(8,128)(2,1)} %param.33, f32[2,16,40,768]{3,2,1,0:T(8,128)} %fusion.7, bf16[2,1536,768]{2,1,0:T(8,128)(2,1)} %param.31, bf16[16,2,40,1536]{3,2,1,0:T(8,128)(2,1)} %copy-done.6), kind=kOutput, calls=%fused_computation.21 | convolution fusion | flops 6044712960 | bytes 21233664 | tf_op jit(solution)/shard_map/sjcf,jfd->sjcd/dot_general | solution.py:274
  283.5 2.6 copy.161
  286.1 51.5 %all_to_all.27 = bf16[16,2,40,1536]{3,2,1,0:T(8,128)(2,1)S(1)} all-to-all(bf16[16,2,40,1536]{3,2,1,0:T(8,128)(2,1)S(1)} %copy.161), channel_id=1, replica_groups=mesh['row'=8,'col'=16] {'col'}, dimensions={0} | all-to-all | bytes 7864320 | tf_op jit(solution)/shard_map/all_to_all | solution.py:277
  337.5 0.7 fusion.63
  338.2 1.6 fusion.27
  (122 shorter events, 9.4 us)
Async XLA Ops:
  6.5 5.5 %copy-start = (bf16[4,16,2048]{2,1,0:T(8,128)(2,1)S(1)}, bf16[4,16,2048]{2,1,0:T(8,128)(2,1)}, u32[]{:S(2)}) copy-start(bf16[4,16,2048]{2,1,0:T(8,128)(2,1)} %param.28) | copy-start | bytes 786436
  6.5 7.5 %copy-start.11 = (bf16[192,128]{1,0:T(8,128)(2,1)S(1)}, bf16[192,128]{1,0:T(8,128)(2,1)}, u32[]{:S(2)}) copy-start(bf16[192,128]{1,0:T(8,128)(2,1)} %param.24) | copy-start | bytes 147460
  6.5 86.7 %all-gather.3.cloned.1.call-start = ((), (), s32[]{:S(2)}) async-start(), calls=%async_computation.5 | async-start | bytes 3538944 | tf_op jit(solution)/shard_map/all_gather | solution.py:136
  12.9 2.8 copy-start.12
  16.1 80.2 %copy-start.14 = (bf16[1536]{0:T(1024)(128)(2,1)S(1)}, bf16[1536]{0:T(1024)(128)(2,1)}, u32[]{:S(2)}) copy-start(bf16[1536]{0:T(1024)(128)(2,1)} %param.22) | copy-start | bytes 9220
  16.1 81.1 %copy-start.13 = (s32[128,4]{0,1:T(4,128)S(1)}, s32[128,4]{0,1:T(4,128)}, u32[]{:S(2)}) copy-start(s32[128,4]{0,1:T(4,128)} %param.21) | copy-start | bytes 6148
  53.4 101.8 %all-gather.5.cloned.1.call-start = ((), (), s32[]{:S(2)}) async-start(), calls=%async_computation.6 | async-start | bytes 2654208 | tf_op jit(solution)/shard_map/all_gather | solution.py:136
  93.2 46.6 %collective-permute-start = (bf16[1536,1024]{1,0:T(8,128)(2,1)}, bf16[1536,1024]{1,0:T(8,128)(2,1)}, u32[]{:S(2)}, u32[]{:S(2)}) collective-permute-start(bf16[1536,1024]{1,0:T(8,128)(2,1)} %all-gather.3.cloned.1.call-done), channel_id=1, source_target_pairs={{0,1},{1,0},{2,3},{3,2},{4,5},{5,4},{6,7},{7,6},{8,9},{9,8},{10,11... | collective-permute-start | bytes 9437192 | tf_op jit(solution)/shard_map/ppermute | solution.py:137
  97.0 8.3 %copy-start.8 = (f32[128,64]{0,1:T(8,128)}, f32[128,64]{0,1:T(8,128)S(1)}, u32[]{:S(2)}) copy-start(f32[128,64]{0,1:T(8,128)S(1)} %get-tuple-element.18) | copy-start | bytes 98308
  97.0 8.3 %copy-start.9 = (f32[128,64]{0,1:T(8,128)}, f32[128,64]{0,1:T(8,128)S(1)}, u32[]{:S(2)}) copy-start(f32[128,64]{0,1:T(8,128)S(1)} %get-tuple-element.19) | copy-start | bytes 98308
  100.0 13.0 %copy-start.3 = (bf16[128,1536]{1,0:T(8,128)(2,1)S(1)}, bf16[128,1536]{1,0:T(8,128)(2,1)}, u32[]{:S(2)}) copy-start(bf16[128,1536]{1,0:T(8,128)(2,1)} %param.18) | copy-start | bytes 1179652
  105.3 30.2 %all-to-all-start.1 = ((bf16[16,208,128]{2,1,0:T(8,128)(2,1)}), bf16[16,208,128]{2,1,0:T(8,128)(2,1)S(1)}, u32[]{:S(2)}, u32[]{:S(2)}) async-start(bf16[16,208,128]{2,1,0:T(8,128)(2,1)} %broadcast_in_dim.207), calls=%async_computation.1 | async-start | bytes 1703936 | tf_op jit(solution)/shard_map/all_to_all | solution.py:129
  145.2 2.5 copy-start.5
  145.3 7.1 %copy-start.15 = (bf16[1536]{0:T(1024)(128)(2,1)S(1)}, bf16[1536]{0:T(1024)(128)(2,1)}, u32[]{:S(2)}) copy-start(bf16[1536]{0:T(1024)(128)(2,1)} %param.23) | copy-start | bytes 9220
  147.8 32.8 %all-to-all-start.2 = ((bf16[16,128,512]{1,2,0:T(8,128)(2,1)}), bf16[16,128,512]{1,2,0:T(8,128)(2,1)S(1)}, u32[]{:S(2)}, u32[]{:S(2)}) async-start(bf16[16,128,512]{1,2,0:T(8,128)(2,1)} %broadcast_in_dim.212), calls=%async_computation.2 | async-start | bytes 4194304 | tf_op jit(solution)/shard_map/all_to_all | solution.py:202
  155.1 50.5 %collective-permute-start.1 = (bf16[1536,768]{1,0:T(8,128)(2,1)}, bf16[1536,768]{1,0:T(8,128)(2,1)}, u32[]{:S(2)}, u32[]{:S(2)}) collective-permute-start(bf16[1536,768]{1,0:T(8,128)(2,1)} %all-gather.5.cloned.1.call-done), channel_id=1, source_target_pairs={{0,1},{1,0},{2,3},{3,2},{4,5},{5,4},{6,7},{7,6},{8,9},{9,8},{10,11... | collective-permute-start | bytes 7077896 | tf_op jit(solution)/shard_map/ppermute | solution.py:137
  180.8 3.9 %copy-start.4 = (pred[768,1664]{1,0:T(8,128)(4,1)S(1)}, pred[768,1664]{1,0:T(8,128)(4,1)}, u32[]{:S(2)}) copy-start(pred[768,1664]{1,0:T(8,128)(4,1)} %compare_and_fusion) | copy-start | bytes 3833860
  192.4 7.0 %copy-start.2 = (f32[2,768,1664]{2,1,0:T(8,128)S(1)}, f32[2,768,1664]{2,1,0:T(8,128)}, u32[]{:S(2)}) copy-start(f32[2,768,1664]{2,1,0:T(8,128)} %get-tuple-element.25) | copy-start | bytes 30670852
  192.4 7.1 %copy-start.7 = (bf16[1664,2,128]{2,0,1:T(8,128)(2,1)S(1)}, bf16[1664,2,128]{2,0,1:T(8,128)(2,1)}, u32[]{:S(2)}) copy-start(bf16[1664,2,128]{2,0,1:T(8,128)(2,1)} %copy.151) | copy-start | bytes 2555908
  203.4 6.1 %copy-start.10 = (bf16[1536,32]{0,1:T(8,128)(2,1)S(1)}, bf16[1536,32]{0,1:T(8,128)(2,1)}, u32[]{:S(2)}) copy-start(bf16[1536,32]{0,1:T(8,128)(2,1)} %param.26) | copy-start | bytes 294916
  210.5 55.2 %slice-start = ((s8[4718592]{0:T(1024)(128)(4,1)}), s8[4194304]{0:T(1024)(128)(4,1)S(1)}, s32[]{:S(2)}) async-start(s8[4718592]{0:T(1024)(128)(4,1)} %bitcast.164), calls=%async_computation.7 | async-start | bytes 8388608
  211.8 53.9 %slice-start.1 = ((s8[4718592]{0:T(1024)(128)(4,1)}), s8[524288]{0:T(1024)(128)(4,1)S(1)}, s32[]{:S(2)}) async-start(s8[4718592]{0:T(1024)(128)(4,1)} %bitcast.164), calls=%async_computation.8 | async-start | bytes 1048576
  263.8 1.9 copy-start.6
  337.5 2.3 copy-start.1
Sparse Core Ops, SparseCore 0:
  53.5 39.6 all-gather.2
  104.2 42.7 all-gather.4

commit v14 on v13

--- a/solution.py
+++ b/solution.py
@@ -92,10 +92,16 @@
     owner_column = adapter_row // local_adapters
     nearby_slot = adapter_row % local_adapters
     owned_here = (owner_column == col_index)[:, None, None]
+    slot_hits = nearby_slot[:, None] == jnp.arange(local_adapters, dtype=jnp.int32)[None, :]
+
+    def pick_local(table):
+        chosen = jnp.where(slot_hits[:, :, None, None], table[None], jnp.zeros((), table.dtype))
+        return jnp.sum(chosen.astype(jnp.float32), axis=1).astype(table.dtype)
+
     tables = (adapter_projection_down, adapter_projection_up, adapter_output_down, adapter_output_up)
     picked = jnp.concatenate(
         [
-            jnp.where(owned_here, jnp.take(table, nearby_slot, axis=0), jnp.zeros((), table.dtype))
+            jnp.where(owned_here, pick_local(table), jnp.zeros((), table.dtype))
             for table in tables
         ],
         axis=-1,

time: 348 us -> 347 us (level)
  waiting for transfers between devices: 82.5 us -> 72.4 us
  other arithmetic: 14.3 us -> 22.2 us
    all_to_all x1, waiting for transfers between devices: 20.4 us -> 11.8 us  [local(): lax.all_to_all(jnp.broadcast_to(key_value_piece[None], (columns,) + key_v...]
    gather x4 -> x0, local copies, waits for them, and re-layouts: 5.03 us -> none  [local(): jnp.take(table, nearby_slot, axis=0)]
  transfers between devices with their start and end apart: 6 -> 6, of which waited for: 3 -> 3; matrix products, arithmetic and copies ran while one was open for 16% -> 19% of each run, Pallas kernels for 0% -> 0%
where the time goes in v14:
time: 347 us; the launch traced here: 346 us
  blocking collectives  137 us (39%)
  waiting for transfers between devices  72.4 us (21%)
  matrix products  43.2 us (12%)
  local copies, waits for them, and re-layouts  42.7 us (12%)
  other arithmetic  22.2 us (6%)
  starting transfers between devices  14.1 us (4%)
  between operations  14 us (4%)
    all_to_all x1, blocking collectives, local(): lax.all_to_all(sending, 'col', split_axis=0, concat_axis=0, tiled=True)  52 us
    all_to_all x1, blocking collectives, local(): lax.all_to_all(answered, 'col', split_axis=0, concat_axis=0, tiled=True)  51.5 us
    all_gather x2, waiting for transfers between devices, gather_halves(): own = lax.all_gather(slab, 'row', axis=0, tiled=True)  39.8 us
    all_to_all x1, blocking collectives, local(): bundle = lax.all_to_all(bundle, 'col', 0, 0, tiled=True)  33.8 us
    all_to_all x1, waiting for transfers between devices, local(): lax.all_to_all(jnp.broadcast_to(reduced[None], (columns,) + reduced.shape...  20.8 us
    dot_general x1, matrix products, local(): jnp.einsum('sjcf,jfd->sjcd', hidden_vals, expert_down_weight, preferred_e...  12.6 us
    all_to_all x1, waiting for transfers between devices, local(): lax.all_to_all(jnp.broadcast_to(key_value_piece[None], (columns,) + key_v...  11.8 us
    reduce_sum x1, other arithmetic, local(): running_new = jnp.sum(weights, axis=-1)  7 us
  transfers between devices with their start and end apart: 6, of which 3 were waited for; matrix products, arithmetic and copies ran while one was open for 19% of the time, Pallas kernels for 0%

profile of v14, /device:TPU:1, one launch (start us, length us, event | category | flops | bytes accessed | tf_op | source)
XLA Modules:
  0.0 345.9 jit_solution(10431742396750001264)
XLA Ops:
  6.6 0.9 dynamic-slice_reduce_fusion
  7.6 1.1 select_reduce_fusion.2
  8.8 1.6 select_reduce_fusion.5
  10.6 1.1 reshape.456
  13.8 33.8 %all_to_all.25 = bf16[16,448,128]{2,1,0:T(8,128)(2,1)S(1)} all-to-all(bf16[16,448,128]{2,1,0:T(8,128)(2,1)S(1)} %pad_maximum_fusion), channel_id=1, replica_groups=mesh['row'=8,'col'=16] {'col'}, dimensions={0} | all-to-all | bytes 3670016 | tf_op jit(solution)/shard_map/all_to_all | solution.py:126
  47.9 1.1 copy.137
  49.0 2.0 copy.138
  51.1 39.8 %all-gather.3.cloned.1.call-done = bf16[1536,1024]{1,0:T(8,128)(2,1)} async-done(((bf16[192,1024]{1,0:T(8,128)(2,1)}), bf16[1536,1024]{1,0:T(8,128)(2,1)}) %all-gather.3.cloned.1.call-update) | async-done | bytes 3145744 | tf_op jit(solution)/shard_map/all_gather | solution.py:142
  90.9 3.0 collective-permute-start
  97.6 1.7 reshape.470
  99.3 1.4 copy.152
  100.7 2.0 reshape.471
  103.6 1.0 broadcast_in_dim.262
  104.6 6.5 %all-to-all-start.1 = ((bf16[16,208,128]{2,1,0:T(8,128)(2,1)}), bf16[16,208,128]{2,1,0:T(8,128)(2,1)S(1)}, u32[]{:S(2)}, u32[]{:S(2)}) async-start(bf16[16,208,128]{2,1,0:T(8,128)(2,1)} %broadcast_in_dim.262), calls=%async_computation.1 | async-start | bytes 1703936 | tf_op jit(solution)/shard_map/all_to_all | solution.py:135
  111.1 2.1 reduce-window.11
  114.0 20.8 %all-to-all-done.1 = bf16[16,208,128]{2,1,0:T(8,128)(2,1)S(1)} async-done(((bf16[16,208,128]{2,1,0:T(8,128)(2,1)}), bf16[16,208,128]{2,1,0:T(8,128)(2,1)S(1)}, u32[]{:S(2)}, u32[]{:S(2)}) %all-to-all-start.1) | async-done | bytes 852000 | tf_op jit(solution)/shard_map/all_to_all | solution.py:135
  134.8 0.9 reshape.462
  135.7 2.5 fusion.86
  138.2 2.6 broadcast_select_fusion.3
  141.7 1.5 fusion.24
  143.4 1.3 subtract_convert_fusion.3
  145.1 1.8 broadcast_in_dim.267
  146.8 4.3 %all-to-all-start.2 = ((bf16[16,128,512]{1,2,0:T(8,128)(2,1)}), bf16[16,128,512]{1,2,0:T(8,128)(2,1)S(1)}, u32[]{:S(2)}, u32[]{:S(2)}) async-start(bf16[16,128,512]{1,2,0:T(8,128)(2,1)} %broadcast_in_dim.267), calls=%async_computation.2 | async-start | bytes 4194304 | tf_op jit(solution)/shard_map/all_to_all | solution.py:208
  151.1 1.1 slice_reduce_fusion.1
  152.4 0.9 fusion.67
  154.0 0.9 copy.157
  157.0 2.2 compare_and_fusion
  159.4 2.1 slice.79
  161.5 2.3 copy.143
  163.8 1.2 subtract_convert_fusion.1
  165.8 1.9 copy.144
  167.7 11.8 %all-to-all-done.2 = bf16[16,128,512]{1,2,0:T(8,128)(2,1)S(1)} async-done(((bf16[16,128,512]{1,2,0:T(8,128)(2,1)}), bf16[16,128,512]{1,2,0:T(8,128)(2,1)S(1)}, u32[]{:S(2)}, u32[]{:S(2)}) %all-to-all-start.2) | async-done | bytes 2097184 | tf_op jit(solution)/shard_map/all_to_all | solution.py:208
  179.9 2.0 fusion.88
  181.9 2.2 copy.149
  184.1 6.4 %select_reduce_fusion = (f32[2,768]{1,0:T(2,128)S(1)}, f32[2,768,1664]{2,1,0:T(8,128)}) fusion(pred[768,1664]{1,0:T(8,128)(4,1)S(1)} %copy-done.3, bf16[2,768,128]{2,1,0:T(8,128)(2,1)S(1)} %bitcast.153, bf16[1664,2,128]{2,0,1:T(8,128)(2,1)} %copy.149), kind=kOutput, calls=%fused_computation.2 | convolution fusion | flops 661977600 | bytes 12752896 | tf_op jit(solution)/shard_map/hqd,hkd->hqk/dot_general | solution.py:229
  190.5 2.2 copy.150
  192.7 7.0 %fusion = f32[2,768]{1,0:T(2,128)S(1)} fusion(f32[2,768,1664]{2,1,0:T(8,128)} %get-tuple-element.24, f32[2,768]{1,0:T(2,128)S(1)} %broadcast_maximum_fusion, pred[768,1664]{1,0:T(8,128)(4,1)S(1)} %copy-done.3), kind=kLoop, calls=%fused_computation.3 | loop fusion | flops 10222080 | bytes 11513856 | tf_op jit(solution)/shard_map/reduce_sum | solution.py:235
  199.8 3.6 %fusion.44 = bf16[2,768,128]{2,1,0:T(8,128)(2,1)S(1)} fusion(f32[2,768,1664]{2,1,0:T(8,128)S(1)} %copy-done.1, f32[2,768]{1,0:T(2,128)S(1)} %broadcast_maximum_fusion, pred[768,1664]{1,0:T(8,128)(4,1)S(1)} %copy-done.3, bf16[1664,2,128]{2,0,1:T(8,128)(2,1)S(1)} %copy-done.6, f32[2,768]{1,0:T(2,128)S(1)} %fusion), kind=kOutput, calls=%fused_computation.50 | convolution fusion | flops 664928256 | bytes 12759040 | tf_op jit(solution)/shard_map/hqk,hkd->hqd/dot_general | solution.py:236
  203.7 2.2 convolution_dynamic-update-slice_fusion.1
  205.9 2.2 convolution_dynamic-update-slice_fusion
  209.7 1.3 convolution_convert_fusion
  211.0 52.0 %all_to_all.26 = bf16[16,2,40,1536]{3,2,1,0:T(8,128)(2,1)S(1)} all-to-all(bf16[16,2,40,1536]{3,2,1,0:T(8,128)(2,1)S(1)} %bitcast.137), channel_id=1, replica_groups=mesh['row'=8,'col'=16] {'col'}, dimensions={0} | all-to-all | bytes 7864320 | tf_op jit(solution)/shard_map/all_to_all | solution.py:272
  263.0 1.9 copy-done.5
  264.9 5.2 %fusion.7 = f32[2,16,40,768]{3,2,1,0:T(8,128)} fusion(bf16[2,1536,768]{2,1,0:T(8,128)(2,1)S(1)} %bitcast.161, bf16[16,2,40,1536]{3,2,1,0:T(8,128)(2,1)S(1)} %all_to_all.26), kind=kOutput, calls=%fused_computation.11 | convolution fusion | flops 3019898880 | bytes 12582912 | tf_op jit(solution)/shard_map/sjcd,jdf->sjcf/dot_general | solution.py:276
  270.1 12.6 %fusion.14 = bf16[16,2,40,1536]{3,2,0,1:T(8,128)(2,1)} fusion(bf16[2,768,1536]{2,1,0:T(8,128)(2,1)} %param.31, f32[2,16,40,768]{3,2,1,0:T(8,128)} %fusion.7, bf16[2,1536,768]{2,1,0:T(8,128)(2,1)} %param.29, bf16[16,2,40,1536]{3,2,1,0:T(8,128)(2,1)} %copy-done.5), kind=kOutput, calls=%fused_computation.17 | convolution fusion | flops 6044712960 | bytes 21233664 | tf_op jit(solution)/shard_map/sjcf,jfd->sjcd/dot_general | solution.py:280
  282.7 2.6 copy.160
  285.3 51.5 %all_to_all.27 = bf16[16,2,40,1536]{3,2,1,0:T(8,128)(2,1)S(1)} all-to-all(bf16[16,2,40,1536]{3,2,1,0:T(8,128)(2,1)S(1)} %copy.160), channel_id=1, replica_groups=mesh['row'=8,'col'=16] {'col'}, dimensions={0} | all-to-all | bytes 7864320 | tf_op jit(solution)/shard_map/all_to_all | solution.py:283
  337.5 1.6 fusion.27
  (125 shorter events, 16.3 us)
Async XLA Ops:
  6.5 202.2 %copy-start = (bf16[1536,32]{0,1:T(8,128)(2,1)S(1)}, bf16[1536,32]{0,1:T(8,128)(2,1)}, u32[]{:S(2)}) copy-start(bf16[1536,32]{0,1:T(8,128)(2,1)} %param.24) | copy-start | bytes 294916
  6.5 5.2 %copy-start.10 = (bf16[192,128]{1,0:T(8,128)(2,1)S(1)}, bf16[192,128]{1,0:T(8,128)(2,1)}, u32[]{:S(2)}) copy-start(bf16[192,128]{1,0:T(8,128)(2,1)} %param.22) | copy-start | bytes 147460
  6.5 84.3 %all-gather.3.cloned.1.call-start = ((), (), s32[]{:S(2)}) async-start(), calls=%async_computation.5 | async-start | bytes 3538944 | tf_op jit(solution)/shard_map/all_gather | solution.py:142
  10.5 2.8 copy-start.11
  13.7 80.2 %copy-start.13 = (bf16[1536]{0:T(1024)(128)(2,1)S(1)}, bf16[1536]{0:T(1024)(128)(2,1)}, u32[]{:S(2)}) copy-start(bf16[1536]{0:T(1024)(128)(2,1)} %param.20) | copy-start | bytes 9220
  13.7 82.8 %copy-start.12 = (s32[128,4]{0,1:T(4,128)S(1)}, s32[128,4]{0,1:T(4,128)}, u32[]{:S(2)}) copy-start(s32[128,4]{0,1:T(4,128)} %param.19) | copy-start | bytes 6148
  51.0 108.2 %all-gather.5.cloned.1.call-start = ((), (), s32[]{:S(2)}) async-start(), calls=%async_computation.6 | async-start | bytes 2654208 | tf_op jit(solution)/shard_map/all_gather | solution.py:142
  90.9 47.4 %collective-permute-start = (bf16[1536,1024]{1,0:T(8,128)(2,1)}, bf16[1536,1024]{1,0:T(8,128)(2,1)}, u32[]{:S(2)}, u32[]{:S(2)}) collective-permute-start(bf16[1536,1024]{1,0:T(8,128)(2,1)} %all-gather.3.cloned.1.call-done), channel_id=1, source_target_pairs={{0,1},{1,0},{2,3},{3,2},{4,5},{5,4},{6,7},{7,6},{8,9},{9,8},{10,11... | collective-permute-start | bytes 9437192 | tf_op jit(solution)/shard_map/ppermute | solution.py:143
  94.2 0.7 copy-start.17
  94.2 0.5 copy-start.16
  94.3 19.1 %copy-start.18 = (s32[128]{0:T(128)}, s32[128]{0:T(128)S(1)}, u32[]{:S(2)}) copy-start(s32[128]{0:T(128)S(1)} %convert_reduce_fusion.2) | copy-start | bytes 1540
  95.1 2.5 copy-start.8
  99.3 13.9 %copy-start.2 = (bf16[128,1536]{1,0:T(8,128)(2,1)S(1)}, bf16[128,1536]{1,0:T(8,128)(2,1)}, u32[]{:S(2)}) copy-start(bf16[128,1536]{1,0:T(8,128)(2,1)} %param.16) | copy-start | bytes 1179652
  104.6 30.2 %all-to-all-start.1 = ((bf16[16,208,128]{2,1,0:T(8,128)(2,1)}), bf16[16,208,128]{2,1,0:T(8,128)(2,1)S(1)}, u32[]{:S(2)}, u32[]{:S(2)}) async-start(bf16[16,208,128]{2,1,0:T(8,128)(2,1)} %broadcast_in_dim.262), calls=%async_computation.1 | async-start | bytes 1703936 | tf_op jit(solution)/shard_map/all_to_all | solution.py:135
  143.2 3.6 %copy-start.4 = (f32[128,2048]{1,0:T(8,128)}, f32[128,2048]{1,0:T(8,128)S(1)}, u32[]{:S(2)}) copy-start(f32[128,2048]{1,0:T(8,128)S(1)} %fusion.24) | copy-start | bytes 3145732
  143.4 8.9 %copy-start.14 = (bf16[1536]{0:T(1024)(128)(2,1)S(1)}, bf16[1536]{0:T(1024)(128)(2,1)}, u32[]{:S(2)}) copy-start(bf16[1536]{0:T(1024)(128)(2,1)} %param.21) | copy-start | bytes 9220
  146.8 32.7 %all-to-all-start.2 = ((bf16[16,128,512]{1,2,0:T(8,128)(2,1)}), bf16[16,128,512]{1,2,0:T(8,128)(2,1)S(1)}, u32[]{:S(2)}, u32[]{:S(2)}) async-start(bf16[16,128,512]{1,2,0:T(8,128)(2,1)} %broadcast_in_dim.267), calls=%async_computation.2 | async-start | bytes 4194304 | tf_op jit(solution)/shard_map/all_to_all | solution.py:208
  152.3 11.5 %copy-start.9 = (f32[128,64]{0,1:T(8,128)S(1)}, f32[128,64]{0,1:T(8,128)}, u32[]{:S(2)}) copy-start(f32[128,64]{0,1:T(8,128)} %copy-done.8) | copy-start | bytes 98308
  159.2 46.7 %collective-permute-start.1 = (bf16[1536,768]{1,0:T(8,128)(2,1)}, bf16[1536,768]{1,0:T(8,128)(2,1)}, u32[]{:S(2)}, u32[]{:S(2)}) collective-permute-start(bf16[1536,768]{1,0:T(8,128)(2,1)} %all-gather.5.cloned.1.call-done), channel_id=1, source_target_pairs={{0,1},{1,0},{2,3},{3,2},{4,5},{5,4},{6,7},{7,6},{8,9},{9,8},{10,11... | collective-permute-start | bytes 7077896 | tf_op jit(solution)/shard_map/ppermute | solution.py:143
  179.9 4.2 %copy-start.3 = (pred[768,1664]{1,0:T(8,128)(4,1)S(1)}, pred[768,1664]{1,0:T(8,128)(4,1)}, u32[]{:S(2)}) copy-start(pred[768,1664]{1,0:T(8,128)(4,1)} %compare_and_fusion) | copy-start | bytes 3833860
  179.9 4.2 %copy-start.7 = (bf16[2,6,128,128]{3,2,1,0:T(8,128)(2,1)S(1)}, bf16[2,6,128,128]{3,2,1,0:T(8,128)(2,1)}, u32[]{:S(2)}) copy-start(bf16[2,6,128,128]{3,2,1,0:T(8,128)(2,1)} %copy.144) | copy-start | bytes 1179652
  192.7 7.0 %copy-start.1 = (f32[2,768,1664]{2,1,0:T(8,128)S(1)}, f32[2,768,1664]{2,1,0:T(8,128)}, u32[]{:S(2)}) copy-start(f32[2,768,1664]{2,1,0:T(8,128)} %get-tuple-element.24) | copy-start | bytes 30670852
  192.7 7.1 %copy-start.6 = (bf16[1664,2,128]{2,0,1:T(8,128)(2,1)S(1)}, bf16[1664,2,128]{2,0,1:T(8,128)(2,1)}, u32[]{:S(2)}) copy-start(bf16[1664,2,128]{2,0,1:T(8,128)(2,1)} %copy.150) | copy-start | bytes 2555908
  203.4 4.7 %copy-start.15 = (pred[128,4]{0,1:T(4,128)(4,1)S(1)}, pred[128,4]{0,1:T(4,128)(4,1)}, u32[]{:S(2)}) copy-start(pred[128,4]{0,1:T(4,128)(4,1)} %iota_compare_fusion.4) | copy-start | bytes 1540
  209.7 55.2 %slice-start = ((s8[4718592]{0:T(1024)(128)(4,1)}), s8[4194304]{0:T(1024)(128)(4,1)S(1)}, s32[]{:S(2)}) async-start(s8[4718592]{0:T(1024)(128)(4,1)} %bitcast.160), calls=%async_computation.7 | async-start | bytes 8388608
  211.0 53.9 %slice-start.1 = ((s8[4718592]{0:T(1024)(128)(4,1)}), s8[524288]{0:T(1024)(128)(4,1)S(1)}, s32[]{:S(2)}) async-start(s8[4718592]{0:T(1024)(128)(4,1)} %bitcast.160), calls=%async_computation.8 | async-start | bytes 1048576
  263.0 1.9 copy-start.5
Sparse Core Ops, SparseCore 0:
  51.2 39.6 all-gather.2
  103.6 42.7 all-gather.4
